TPU v7x, 128 devices: a whole 4x4x4 slice. The times are simulated.
128 devices in a mesh: group: 8 (over y, core), member: 16 (over x, z).
Axes of the slice: x: 4, y: 4, z: 4, core: 2. Of those that a mesh axis runs over, the one named last changes fastest.
Arguments:
- queries: bfloat16 [2048, 64, 576], P(('group', 'member')), may hold values from -240 to 240
- latent_cache: bfloat16 [2048, 128, 576], P(('group', 'member')), may hold values from -4 to 4
- new_key: bfloat16 [2048, 576], P(('group', 'member')), may hold values from -4 to 4
- parent_beam: int32 [2048], P(('group', 'member')), may hold values from 0 to 3
- value_up: bfloat16 [64, 512, 128], P('member'), may hold values from -0.25 to 0.25
- out_proj: bfloat16 [8192, 3584], P('member', 'group'), may hold values from -0.0625 to 0.0625
- residual: bfloat16 [2048, 3584], P('member', 'group'), may hold values from -6 to 6
- expert_ids: int32 [2048, 8], P('member'), may hold values from 0 to 127, all different within a row; in each aligned block of 128 rows (0 to 127, 128 to 255, ...) at most 16 rows name the same one
- route_gates: float32 [2048, 8], P('member'), may hold values from 0.1 to 0.6
- w_gate: bfloat16 [128, 3584, 1024], P(('group', 'member')), may hold values from -0.09375 to 0.09375
- w_up: bfloat16 [128, 3584, 1024], P(('group', 'member')), may hold values from -0.09375 to 0.09375
- w_down: bfloat16 [128, 1024, 3584], P(('group', 'member')), may hold values from -0.1875 to 0.1875
Outputs:
- layer_out: bfloat16 [2048, 3584], P('member', 'group')
Inputs may be any that keep to these rules, and one draw needn't show every extreme that they name: `expert_ids`: each row names 8 different experts. Within each aligned block of 128 rows no expert is named by more than 16 rows, a bound that some block reaches.
All inputs are finite; a program needn't handle non-finite values.
Results may differ from a plain program's by a relative error of at most 0.019.
Values may be sent and summed in bfloat16 or wider, within the bound.
No kernel may reach another device: no remote copies, remote signals or barrier semaphores. Data moves between devices by JAX's collectives and lax.ppermute only.
A program may use at most 128 MiB of HBM per device.

v0:
```python
import jax
import jax.numpy as jnp
from jax import lax
from jax.sharding import PartitionSpec as P

ROPE = 64
VHEAD = 128
TOP = 8
BEAM = 4


def per_device(
    queries,
    latent_cache,
    new_key,
    parent_beam,
    value_up,
    out_proj,
    residual,
    expert_ids,
    route_gates,
    w_gate,
    w_up,
    w_down,
):
    rows = queries.shape[0]
    latent = value_up.shape[1]
    members = lax.axis_size("member")
    groups = lax.axis_size("group")
    experts = groups * members
    columns = out_proj.shape[1]
    scale = (VHEAD + ROPE) ** (-0.5)
    local_rows = jnp.arange(rows, dtype=jnp.int32)
    parent = local_rows // BEAM * BEAM + parent_beam
    keys = jnp.concatenate([jnp.take(latent_cache, parent, axis=0), new_key[:, None, :]], axis=1)
    scores = jnp.einsum("rhw,rcw->rhc", queries, keys, preferred_element_type=jnp.float32) * scale
    shifted = jnp.exp(scores - jnp.max(scores, axis=-1, keepdims=True))
    weights = (shifted / jnp.sum(shifted, axis=-1, keepdims=True)).astype(jnp.bfloat16)
    latent_out = jnp.einsum(
        "rhc,rcl->rhl", weights, keys[:, :, :latent], preferred_element_type=jnp.float32
    ).astype(jnp.bfloat16)
    by_heads = lax.all_to_all(latent_out, "member", split_axis=1, concat_axis=0, tiled=True)
    per_head = jnp.einsum(
        "rhl,hlv->rhv", by_heads, value_up, preferred_element_type=jnp.float32
    ).astype(jnp.bfloat16)
    per_head = per_head.reshape(per_head.shape[0], per_head.shape[1] * per_head.shape[2])
    partial_sums = jnp.dot(
        lax.all_gather(per_head, "group", axis=0, tiled=True),
        out_proj,
        preferred_element_type=jnp.float32,
    )
    attention = lax.psum_scatter(
        partial_sums.astype(jnp.bfloat16), "member", scatter_dimension=0, tiled=True
    ).astype(jnp.float32)
    hidden_in = (residual.astype(jnp.float32) + attention).astype(jnp.bfloat16)
    block_rows = hidden_in.shape[0]
    capacity = max(2, 2 * rows * TOP // members)
    flat_ids = expert_ids.reshape(-1)
    onehot = (flat_ids[:, None] == jnp.arange(experts, dtype=jnp.int32)[None, :]).astype(jnp.int32)
    ranking = jnp.sum((jnp.cumsum(onehot, axis=0) - onehot) * onehot, axis=1)
    slot_index = flat_ids * capacity + ranking
    positions = jnp.arange(experts * capacity, dtype=jnp.int32)
    matches = (positions[:, None] == slot_index[None, :]).reshape(
        experts * capacity, block_rows, TOP
    )
    send_map = jnp.any(matches, axis=2).astype(jnp.bfloat16)
    outgoing = jnp.dot(send_map, hidden_in, preferred_element_type=jnp.float32).astype(jnp.bfloat16)
    arrived = lax.all_to_all(
        outgoing.reshape(experts, capacity, columns),
        ("group", "member"),
        split_axis=0,
        concat_axis=0,
        tiled=True,
    )
    expert_rows = (
        arrived.reshape(groups, members, capacity, columns)
        .transpose(1, 2, 0, 3)
        .reshape(members * capacity, groups * columns)
    )
    gate = jnp.dot(expert_rows, w_gate[0], preferred_element_type=jnp.float32)
    upper = jnp.dot(expert_rows, w_up[0], preferred_element_type=jnp.float32)
    inner = (jax.nn.silu(gate) * upper).astype(jnp.bfloat16)
    results = jnp.dot(inner, w_down[0], preferred_element_type=jnp.float32).astype(jnp.bfloat16)
    arranged = (
        results.reshape(members, capacity, groups, columns)
        .transpose(2, 0, 1, 3)
        .reshape(experts, capacity, columns)
    )
    returned = lax.all_to_all(
        arranged, ("group", "member"), split_axis=0, concat_axis=0, tiled=True
    )
    returned = returned.reshape(experts * capacity, columns)
    picked = returned[slot_index.reshape(block_rows, TOP)].astype(jnp.float32)
    mixed = jnp.sum(route_gates[:, :, None] * picked, axis=1)
    return (hidden_in.astype(jnp.float32) + mixed).astype(jnp.bfloat16)


def solution(mesh):
    in_specs = (
        P(("group", "member"), None, None),
        P(("group", "member"), None, None),
        P(("group", "member"), None),
        P(("group", "member")),
        P("member", None, None),
        P("member", "group"),
        P("member", "group"),
        P("member", None),
        P("member", None),
        P(("group", "member"), None, None),
        P(("group", "member"), None, None),
        P(("group", "member"), None, None),
    )
    out_specs = P("member", "group")
    return jax.shard_map(
        per_device, mesh=mesh, in_specs=in_specs, out_specs=out_specs, check_vma=False
    )
```

profile of v0, /device:TPU:1, one launch (start us, length us, event | category | flops | bytes accessed | tf_op | source)
XLA Modules:
  0.0 279.7 jit_solution(13756100547000978620)
XLA Ops:
  8.2 2.3 gather_fusion
  10.5 4.3 %copy.68 = bf16[16,128,576]{2,1,0:T(8,128)(2,1)} copy(bf16[16,128,576]{1,2,0:T(8,128)(2,1)} %gather_fusion) | data formatting | bytes 4718592 | tf_op jit(solution)/shard_map/jit(_take)/gather | solution.py:35
  14.9 2.2 broadcast_select_fusion
  19.0 3.6 %fusion.20 = bf16[16,64,512]{2,1,0:T(8,128)(2,1)S(1)} fusion(bf16[16,1,576]{2,1,0:T(2,128)(2,1)S(1)} %copy.69, bf16[16,128,576]{2,1,0:T(8,128)(2,1)} %copy-done.2, f32[16,64]{1,0:T(8,128)S(1)} %fusion.52, f32[16,64,129]{2,1,0:T(8,128)S(1)} %fusion.31), kind=kOutput, calls=%fused_computation.26 | convolution fusion | flops 140415104 | bytes 3958784 | tf_op jit(solution)/shard_map/rhc,rcl->rhl/dot_general | solution.py:39
  23.1 24.3 %all_to_all.28 = bf16[16,64,512]{2,0,1:T(8,128)(2,1)S(1)} all-to-all(bf16[16,64,512]{2,0,1:T(8,128)(2,1)S(1)} %copy.70), channel_id=1, replica_groups=mesh['group'=8,'member'=16] {'member'}, dimensions={1} | all-to-all | bytes 2097152 | tf_op jit(solution)/shard_map/all_to_all | solution.py:42
  49.0 26.7 %all-gather.2.cloned.1.call-done = bf16[2048,512]{0,1:T(8,128)(2,1)} async-done(((bf16[256,512]{0,1:T(8,128)(2,1)}), bf16[2048,512]{0,1:T(8,128)(2,1)}) %all-gather.2.cloned.1.call-update) | async-done | bytes 2097168 | tf_op jit(solution)/shard_map/all_gather | solution.py:48
  75.7 2.7 convolution_convert_fusion
  78.4 2.4 copy.85
  82.2 7.4 %fusion.1 = pred[2048,128]{1,0:T(8,128)(4,1)S(1)} fusion(s32[128,8]{0,1:T(8,128)S(1)} %get-tuple-element.6), kind=kLoop, calls=%fused_computation.4 | loop fusion | flops 3932160 | bytes 266240 | tf_op jit(solution)/shard_map/reduce_or | solution.py:66
  89.6 65.7 %reduce-scatter.4.cloned.1.call-done = bf16[128,448]{1,0:T(8,128)(2,1)} async-done(((bf16[2048,448]{1,0:T(8,128)(2,1)}), bf16[128,448]{1,0:T(8,128)(2,1)}) %reduce-scatter.4.cloned.1.call-update) | async-done | bytes 114704
  156.4 1.9 convolution_convert_fusion.1
  158.3 2.8 %copy.79 = bf16[2048,448]{1,0:T(8,128)(2,1)S(1)} copy(bf16[2048,448]{0,1:T(8,128)(2,1)} %convolution_convert_fusion.1) | data formatting | bytes 3670016 | tf_op jit(solution)/shard_map/convert_element_type | solution.py:67
  161.1 38.6 %all_to_all.29 = bf16[128,16,448]{2,1,0:T(8,128)(2,1)S(1)} all-to-all(bf16[128,16,448]{2,1,0:T(8,128)(2,1)S(1)} %bitcast.62), channel_id=1, replica_groups=mesh['group'=8,'member'=16] {'group','member'}, dimensions={0} | all-to-all | bytes 3670016 | tf_op jit(solution)/shard_map/all_to_all | solution.py:68
  199.7 1.4 copy.88
  201.1 3.3 %reshape.70 = bf16[256,3584]{1,0:T(8,128)(2,1)} reshape(bf16[16,16,8,448]{3,2,1,0:T(8,128)(2,1)S(1)} %bitcast.64) | data formatting | bytes 3670016 | tf_op jit(solution)/shard_map/reshape | solution.py:78
  204.4 5.8 %fusion.6 = f32[256,1024]{1,0:T(8,128)S(1)} fusion(bf16[256,3584]{1,0:T(8,128)(2,1)} %reshape.70, bf16[1,3584,1024]{2,1,0:T(8,128)(2,1)} %param.21), kind=kOutput, calls=%fused_computation.9 | convolution fusion | flops 1879048192 | bytes 10223616 | tf_op jit(solution)/shard_map/dot_general | solution.py:80
  210.3 10.5 %fusion.8 = bf16[256,3584]{1,0:T(8,128)(2,1)} fusion(bf16[1,1024,3584]{2,1,0:T(8,128)(2,1)} %param.23, bf16[256,3584]{1,0:T(8,128)(2,1)S(1)} %copy-done.3, bf16[1,3584,1024]{2,1,0:T(8,128)(2,1)} %param.22, f32[256,1024]{1,0:T(8,128)S(1)} %fusion.6), kind=kOutput, calls=%fused_computation.11 | convolution fusion | flops 3760586752 | bytes 19398656 | tf_op jit(solution)/shard_map/dot_general | solution.py:83
  220.7 3.9 %reshape.71 = bf16[16,16,8,448]{3,2,1,0:T(8,128)(2,1)S(1)} reshape(bf16[256,3584]{1,0:T(8,128)(2,1)} %fusion.8) | data formatting | bytes 3670016 | tf_op jit(solution)/shard_map/reshape | solution.py:85
  224.6 2.0 copy.81
  226.6 5.8 %all-to-all-start.2 = ((bf16[128,16,448]{2,1,0:T(8,128)(2,1)}), bf16[128,16,448]{2,1,0:T(8,128)(2,1)}, u32[]{:S(2)}, u32[]{:S(2)}) async-start(bf16[128,16,448]{2,1,0:T(8,128)(2,1)} %bitcast.17), calls=%async_computation.2 | async-start | bytes 4194304 | tf_op jit(solution)/shard_map/all_to_all | solution.py:89
  233.4 28.5 %all-to-all-done.2 = bf16[128,16,448]{2,1,0:T(8,128)(2,1)} async-done(((bf16[128,16,448]{2,1,0:T(8,128)(2,1)}), bf16[128,16,448]{2,1,0:T(8,128)(2,1)}, u32[]{:S(2)}, u32[]{:S(2)}) %all-to-all-start.2) | async-done | bytes 1835040 | tf_op jit(solution)/shard_map/all_to_all | solution.py:89
  261.9 6.0 %gather_fusion.1 = bf16[1024,448]{1,0:T(8,128)(2,1)S(1)} fusion(bf16[2048,448]{1,0:T(8,128)(2,1)} %bitcast.18, s32[1024]{0:T(1024)S(1)} %broadcast_clamp_fusion), kind=kCustom, calls=%fused_computation.1 | custom fusion | bytes 1839104 | tf_op jit(solution)/shard_map/gather | solution.py:93
  267.9 2.2 fusion.19
  271.2 1.6 add_convert_fusion
  (54 shorter events, 10.1 us)
Async XLA Ops:
  6.5 1.7 copy-start
  6.5 69.1 %all-gather.2.cloned.1.call-start = ((), (), s32[]{:S(2)}) async-start(), calls=%async_computation.4 | async-start | bytes 2359296 | tf_op jit(solution)/shard_map/all_gather | solution.py:48
  10.5 4.3 %copy-start.6 = (bf16[16,576]{1,0:T(8,128)(2,1)S(1)}, bf16[16,576]{1,0:T(8,128)(2,1)}, u32[]{:S(2)}) copy-start(bf16[16,576]{1,0:T(8,128)(2,1)} %param.14) | copy-start | bytes 55300
  14.9 2.2 copy-start.9
  17.1 1.5 copy-start.2
  23.1 24.4 %copy-start.4 = (bf16[4,512,128]{2,1,0:T(8,128)(2,1)S(1)}, bf16[4,512,128]{2,1,0:T(8,128)(2,1)}, u32[]{:S(2)}) copy-start(bf16[4,512,128]{2,1,0:T(8,128)(2,1)} %param.16) | copy-start | bytes 1572868
  47.4 28.2 %copy-start.10 = (bf16[512,448]{0,1:T(8,128)(2,1)S(1)}, bf16[512,448]{0,1:T(8,128)(2,1)}, u32[]{:S(2)}) copy-start(bf16[512,448]{0,1:T(8,128)(2,1)} %param.17) | copy-start | bytes 1376260
  48.8 106.5 %reduce-scatter.4.cloned.1.call-start = ((), (), s32[]{:S(2)}) async-start(), calls=%async_computation.5 | async-start | bytes 2228224
  78.4 2.5 copy-start.7
  80.9 75.5 %copy-start.5 = (bf16[128,448]{0,1:T(8,128)(2,1)S(1)}, bf16[128,448]{0,1:T(8,128)(2,1)}, u32[]{:S(2)}) copy-start(bf16[128,448]{0,1:T(8,128)(2,1)} %param.18) | copy-start | bytes 344068
  204.4 5.8 %copy-start.3 = (bf16[256,3584]{1,0:T(8,128)(2,1)S(1)}, bf16[256,3584]{1,0:T(8,128)(2,1)}, u32[]{:S(2)}) copy-start(bf16[256,3584]{1,0:T(8,128)(2,1)} %reshape.70) | copy-start | bytes 5505028
  226.6 6.1 %copy-start.8 = (f32[128,8]{0,1:T(8,128)S(1)}, f32[128,8]{0,1:T(8,128)}, u32[]{:S(2)}) copy-start(f32[128,8]{0,1:T(8,128)} %param.20) | copy-start | bytes 12292
  226.6 35.3 %all-to-all-start.2 = ((bf16[128,16,448]{2,1,0:T(8,128)(2,1)}), bf16[128,16,448]{2,1,0:T(8,128)(2,1)}, u32[]{:S(2)}, u32[]{:S(2)}) async-start(bf16[128,16,448]{2,1,0:T(8,128)(2,1)} %bitcast.17), calls=%async_computation.2 | async-start | bytes 4194304 | tf_op jit(solution)/shard_map/all_to_all | solution.py:89
  261.9 10.9 %copy-start.1 = (bf16[16,128,576]{1,2,0:T(8,128)(2,1)S(1)}, bf16[16,128,576]{1,2,0:T(8,128)(2,1)}, u32[]{:S(2)}) copy-start(bf16[16,128,576]{1,2,0:T(8,128)(2,1)} %param.13) | copy-start | bytes 7077892
Sparse Core Ops, SparseCore 0:
  48.9 26.7 all-gather.1
  81.0 74.2 reduce-scatter.3
where the time goes:
time: 280 us
  waiting for transfers between devices  121 us (43%)
  blocking collectives  62.9 us (22%)
  local copies, waits for them, and re-layouts  34 us (12%)
  matrix products  26.9 us (10%)
  other arithmetic  15.3 us (5%)
  between operations  13.7 us (5%)
  starting transfers between devices  6.07 us (2%)
    unnamed x3, waiting for transfers between devices  65.7 us
    all_to_all x1, blocking collectives, per_device(): lax.all_to_all(outgoing.reshape(experts, capacity, columns), ('group', 'm...  38.6 us
    all_to_all x1, waiting for transfers between devices, per_device(): lax.all_to_all(arranged, ('group', 'member'), split_axis=0, concat_axis=0...  28.5 us
    all_gather x1, waiting for transfers between devices, per_device(): lax.all_gather(per_head, 'group', axis=0, tiled=True)  26.7 us
    all_to_all x1, blocking collectives, per_device(): lax.all_to_all(latent_out, 'member', split_axis=1, concat_axis=0, tiled=T...  24.3 us
    dot_general x1, matrix products, per_device(): jnp.dot(inner, w_down[0], preferred_element_type=jnp.float32)  10.5 us
    reduce_or x1, other arithmetic, per_device(): send_map = jnp.any(matches, axis=2).astype(jnp.bfloat16)  7.43 us
    gather x2, local copies, waits for them, and re-layouts, per_device(): jnp.take(latent_cache, parent, axis=0)  6.61 us
  transfers between devices with their start and end apart: 3, of which 3 were waited for; matrix products, arithmetic and copies ran while one was open for 3% of the time, Pallas kernels for 0%

commit v1 on v0

--- a/solution.py
+++ b/solution.py
@@ -49,9 +49,14 @@
         out_proj,
         preferred_element_type=jnp.float32,
     )
-    attention = lax.psum_scatter(
-        partial_sums.astype(jnp.bfloat16), "member", scatter_dimension=0, tiled=True
-    ).astype(jnp.float32)
+    pieces = lax.all_to_all(
+        partial_sums.astype(jnp.bfloat16).reshape(members, -1, columns),
+        "member",
+        split_axis=0,
+        concat_axis=0,
+        tiled=True,
+    )
+    attention = jnp.sum(pieces.astype(jnp.float32), axis=0)
     hidden_in = (residual.astype(jnp.float32) + attention).astype(jnp.bfloat16)
     block_rows = hidden_in.shape[0]
     capacity = max(2, 2 * rows * TOP // members)

time: 280 us -> 238 us (0.85)
  waiting for transfers between devices: 121 us -> 72.9 us
  starting transfers between devices: 6.07 us -> 12.7 us
    unnamed x3 -> x1, waiting for transfers between devices: 65.7 us -> 0.02 us
    all_to_all x0 -> x1, waiting for transfers between devices: none -> 17.5 us  [per_device(): lax.all_to_all(partial_sums.astype(jnp.bfloat16).reshape(members, -1, col...]
    all_to_all x0 -> x1, starting transfers between devices: none -> 6.81 us  [per_device(): lax.all_to_all(partial_sums.astype(jnp.bfloat16).reshape(members, -1, col...]
    unnamed x26, local copies, waits for them, and re-layouts: 5.46 us -> 2.65 us
  transfers between devices with their start and end apart: 3 -> 3, of which waited for: 3 -> 3; matrix products, arithmetic and copies ran while one was open for 3% -> 4% of each run, Pallas kernels for 0% -> 0%
where the time goes in v1:
time: 238 us; the launch traced here: 237 us
  waiting for transfers between devices  72.9 us (31%)
  blocking collectives  61.2 us (26%)
  local copies, waits for them, and re-layouts  32.9 us (14%)
  matrix products  28.3 us (12%)
  other arithmetic  15.6 us (7%)
  between operations  13.6 us (6%)
  starting transfers between devices  12.7 us (5%)
    all_to_all x1, blocking collectives, per_device(): lax.all_to_all(outgoing.reshape(experts, capacity, columns), ('group', 'm...  37 us
    all_to_all x1, waiting for transfers between devices, per_device(): lax.all_to_all(arranged, ('group', 'member'), split_axis=0, concat_axis=0...  28.5 us
    all_gather x1, waiting for transfers between devices, per_device(): lax.all_gather(per_head, 'group', axis=0, tiled=True)  26.9 us
    all_to_all x1, blocking collectives, per_device(): lax.all_to_all(latent_out, 'member', split_axis=1, concat_axis=0, tiled=T...  24.3 us
    all_to_all x1, waiting for transfers between devices, per_device(): lax.all_to_all(partial_sums.astype(jnp.bfloat16).reshape(members, -1, col...  17.5 us
    dot_general x1, matrix products, per_device(): jnp.dot(inner, w_down[0], preferred_element_type=jnp.float32)  10.8 us
    reduce_or x1, other arithmetic, per_device(): send_map = jnp.any(matches, axis=2).astype(jnp.bfloat16)  7.43 us
    dot_general x1, matrix products, per_device(): gate = jnp.dot(expert_rows, w_gate[0], preferred_element_type=jnp.float32)  6.82 us
  transfers between devices with their start and end apart: 3, of which 3 were waited for; matrix products, arithmetic and copies ran while one was open for 4% of the time, Pallas kernels for 0%

profile of v1, /device:TPU:1, one launch (start us, length us, event | category | flops | bytes accessed | tf_op | source)
XLA Modules:
  0.0 237.1 jit_solution(4509807502747620464)
XLA Ops:
  8.2 2.3 gather_fusion
  10.5 4.3 %copy.84 = bf16[16,128,576]{2,1,0:T(8,128)(2,1)} copy(bf16[16,128,576]{1,2,0:T(8,128)(2,1)} %gather_fusion) | data formatting | bytes 4718592 | tf_op jit(solution)/shard_map/jit(_take)/gather | solution.py:35
  14.9 2.2 broadcast_select_fusion
  19.0 3.6 %fusion.21 = bf16[16,64,512]{2,1,0:T(8,128)(2,1)S(1)} fusion(bf16[16,1,576]{2,1,0:T(2,128)(2,1)S(1)} %copy.85, bf16[16,128,576]{2,1,0:T(8,128)(2,1)} %copy-done.2, f32[16,64]{1,0:T(8,128)S(1)} %fusion.53, f32[16,64,129]{2,1,0:T(8,128)S(1)} %fusion.32), kind=kOutput, calls=%fused_computation.29 | convolution fusion | flops 140415104 | bytes 3958784 | tf_op jit(solution)/shard_map/rhc,rcl->rhl/dot_general | solution.py:39
  23.1 24.3 %all_to_all.33 = bf16[16,64,512]{2,0,1:T(8,128)(2,1)S(1)} all-to-all(bf16[16,64,512]{2,0,1:T(8,128)(2,1)S(1)} %copy.86), channel_id=1, replica_groups=mesh['group'=8,'member'=16] {'member'}, dimensions={1} | all-to-all | bytes 2097152 | tf_op jit(solution)/shard_map/all_to_all | solution.py:42
  48.8 26.9 %all-gather.2.cloned.1.call-done = bf16[2048,512]{0,1:T(8,128)(2,1)} async-done(((bf16[256,512]{0,1:T(8,128)(2,1)}), bf16[2048,512]{0,1:T(8,128)(2,1)}) %all-gather.2.cloned.1.call-update) | async-done | bytes 2097168 | tf_op jit(solution)/shard_map/all_gather | solution.py:48
  75.7 2.7 %fusion.20 = bf16[56,16,8,128]{3,2,1,0:T(8,128)(2,1)S(1)} fusion(bf16[512,448]{0,1:T(8,128)(2,1)S(1)} %copy-done.11, bf16[2048,512]{0,1:T(8,128)(2,1)} %all-gather.2.cloned.1.call-done), kind=kOutput, calls=%fused_computation.28 | convolution fusion | flops 940441600 | bytes 4390912 | tf_op jit(solution)/shard_map/dot_general | solution.py:47
  78.4 1.7 copy.106
  80.1 6.8 %all-to-all-start.1 = ((bf16[16,128,448]{1,2,0:T(8,128)(2,1)}), bf16[16,128,448]{1,2,0:T(8,128)(2,1)S(1)}, u32[]{:S(2)}, u32[]{:S(2)}) async-start(bf16[16,128,448]{1,2,0:T(8,128)(2,1)} %bitcast.65), calls=%async_computation.1 | async-start | bytes 3670016 | tf_op jit(solution)/shard_map/all_to_all | solution.py:52
  88.3 7.4 %fusion.1 = pred[2048,128]{1,0:T(8,128)(4,1)S(1)} fusion(s32[128,8]{0,1:T(8,128)S(1)} %get-tuple-element.6), kind=kLoop, calls=%fused_computation.4 | loop fusion | flops 3932160 | bytes 266240 | tf_op jit(solution)/shard_map/reduce_or | solution.py:71
  95.7 17.5 %all-to-all-done.1 = bf16[16,128,448]{1,2,0:T(8,128)(2,1)S(1)} async-done(((bf16[16,128,448]{1,2,0:T(8,128)(2,1)}), bf16[16,128,448]{1,2,0:T(8,128)(2,1)S(1)}, u32[]{:S(2)}, u32[]{:S(2)}) %all-to-all-start.1) | async-done | bytes 1835040 | tf_op jit(solution)/shard_map/all_to_all | solution.py:52
  114.2 1.9 convolution_convert_fusion.1
  116.1 2.8 %copy.96 = bf16[2048,448]{1,0:T(8,128)(2,1)S(1)} copy(bf16[2048,448]{0,1:T(8,128)(2,1)} %convolution_convert_fusion.1) | data formatting | bytes 3670016 | tf_op jit(solution)/shard_map/convert_element_type | solution.py:72
  118.9 37.0 %all_to_all.34 = bf16[128,16,448]{2,1,0:T(8,128)(2,1)S(1)} all-to-all(bf16[128,16,448]{2,1,0:T(8,128)(2,1)S(1)} %bitcast.66), channel_id=1, replica_groups=mesh['group'=8,'member'=16] {'group','member'}, dimensions={0} | all-to-all | bytes 3670016 | tf_op jit(solution)/shard_map/all_to_all | solution.py:73
  157.2 3.3 %reshape.74 = bf16[256,3584]{1,0:T(8,128)(2,1)} reshape(bf16[16,16,8,448]{3,2,1,0:T(8,128)(2,1)S(1)} %bitcast.68) | data formatting | bytes 3670016 | tf_op jit(solution)/shard_map/reshape | solution.py:83
  160.5 6.8 %fusion.6 = f32[256,1024]{1,0:T(8,128)} fusion(bf16[256,3584]{1,0:T(8,128)(2,1)} %reshape.74, bf16[1,3584,1024]{2,1,0:T(8,128)(2,1)} %param.21), kind=kOutput, calls=%fused_computation.9 | convolution fusion | flops 1879048192 | bytes 10223616 | tf_op jit(solution)/shard_map/dot_general | solution.py:85
  167.4 10.8 %fusion.8 = bf16[256,3584]{1,0:T(8,128)(2,1)} fusion(bf16[1,1024,3584]{2,1,0:T(8,128)(2,1)} %param.23, bf16[256,3584]{1,0:T(8,128)(2,1)S(1)} %copy-done.4, bf16[1,3584,1024]{2,1,0:T(8,128)(2,1)} %param.22, f32[256,1024]{1,0:T(8,128)} %fusion.6), kind=kOutput, calls=%fused_computation.11 | convolution fusion | flops 3760586752 | bytes 19398656 | tf_op jit(solution)/shard_map/dot_general | solution.py:88
  178.2 3.9 %reshape.75 = bf16[16,16,8,448]{3,2,1,0:T(8,128)(2,1)S(1)} reshape(bf16[256,3584]{1,0:T(8,128)(2,1)} %fusion.8) | data formatting | bytes 3670016 | tf_op jit(solution)/shard_map/reshape | solution.py:90
  182.1 2.0 copy.98
  184.1 5.8 %all-to-all-start.3 = ((bf16[128,16,448]{2,1,0:T(8,128)(2,1)}), bf16[128,16,448]{2,1,0:T(8,128)(2,1)}, u32[]{:S(2)}, u32[]{:S(2)}) async-start(bf16[128,16,448]{2,1,0:T(8,128)(2,1)} %bitcast.17), calls=%async_computation.3 | async-start | bytes 4194304 | tf_op jit(solution)/shard_map/all_to_all | solution.py:94
  190.9 28.5 %all-to-all-done.3 = bf16[128,16,448]{2,1,0:T(8,128)(2,1)} async-done(((bf16[128,16,448]{2,1,0:T(8,128)(2,1)}), bf16[128,16,448]{2,1,0:T(8,128)(2,1)}, u32[]{:S(2)}, u32[]{:S(2)}) %all-to-all-start.3) | async-done | bytes 1835040 | tf_op jit(solution)/shard_map/all_to_all | solution.py:94
  219.3 6.0 %gather_fusion.1 = bf16[1024,448]{1,0:T(8,128)(2,1)S(1)} fusion(bf16[2048,448]{1,0:T(8,128)(2,1)} %bitcast.18, s32[1024]{0:T(1024)S(1)} %broadcast_clamp_fusion), kind=kCustom, calls=%fused_computation.1 | custom fusion | bytes 1839104 | tf_op jit(solution)/shard_map/gather | solution.py:98
  225.3 2.2 fusion.19
  228.7 1.6 add_convert_fusion
  (55 shorter events, 11.1 us)
Async XLA Ops:
  6.5 1.7 copy-start
  6.5 69.1 %all-gather.2.cloned.1.call-start = ((), (), s32[]{:S(2)}) async-start(), calls=%async_computation.4 | async-start | bytes 2359296 | tf_op jit(solution)/shard_map/all_gather | solution.py:48
  10.5 4.3 %copy-start.7 = (bf16[16,576]{1,0:T(8,128)(2,1)S(1)}, bf16[16,576]{1,0:T(8,128)(2,1)}, u32[]{:S(2)}) copy-start(bf16[16,576]{1,0:T(8,128)(2,1)} %param.14) | copy-start | bytes 55300
  14.9 2.2 copy-start.10
  17.1 1.5 copy-start.2
  23.1 24.4 %copy-start.5 = (bf16[4,512,128]{2,1,0:T(8,128)(2,1)S(1)}, bf16[4,512,128]{2,1,0:T(8,128)(2,1)}, u32[]{:S(2)}) copy-start(bf16[4,512,128]{2,1,0:T(8,128)(2,1)} %param.16) | copy-start | bytes 1572868
  47.4 28.2 %copy-start.11 = (bf16[512,448]{0,1:T(8,128)(2,1)S(1)}, bf16[512,448]{0,1:T(8,128)(2,1)}, u32[]{:S(2)}) copy-start(bf16[512,448]{0,1:T(8,128)(2,1)} %param.17) | copy-start | bytes 1376260
  80.1 6.8 %copy-start.8 = (s32[128,8]{0,1:T(8,128)S(1)}, s32[128,8]{0,1:T(8,128)}, u32[]{:S(2)}) copy-start(s32[128,8]{0,1:T(8,128)} %param.19) | copy-start | bytes 12292
  80.1 33.1 %all-to-all-start.1 = ((bf16[16,128,448]{1,2,0:T(8,128)(2,1)}), bf16[16,128,448]{1,2,0:T(8,128)(2,1)S(1)}, u32[]{:S(2)}, u32[]{:S(2)}) async-start(bf16[16,128,448]{1,2,0:T(8,128)(2,1)} %bitcast.65), calls=%async_computation.1 | async-start | bytes 3670016 | tf_op jit(solution)/shard_map/all_to_all | solution.py:52
  87.6 26.6 %copy-start.6 = (bf16[128,448]{0,1:T(8,128)(2,1)S(1)}, bf16[128,448]{0,1:T(8,128)(2,1)}, u32[]{:S(2)}) copy-start(bf16[128,448]{0,1:T(8,128)(2,1)} %param.18) | copy-start | bytes 344068
  113.5 0.7 copy-start.3
  160.5 6.8 %copy-start.4 = (bf16[256,3584]{1,0:T(8,128)(2,1)S(1)}, bf16[256,3584]{1,0:T(8,128)(2,1)}, u32[]{:S(2)}) copy-start(bf16[256,3584]{1,0:T(8,128)(2,1)} %reshape.74) | copy-start | bytes 5505028
  184.1 6.1 %copy-start.9 = (f32[128,8]{0,1:T(8,128)S(1)}, f32[128,8]{0,1:T(8,128)}, u32[]{:S(2)}) copy-start(f32[128,8]{0,1:T(8,128)} %param.20) | copy-start | bytes 12292
  184.1 35.3 %all-to-all-start.3 = ((bf16[128,16,448]{2,1,0:T(8,128)(2,1)}), bf16[128,16,448]{2,1,0:T(8,128)(2,1)}, u32[]{:S(2)}, u32[]{:S(2)}) async-start(bf16[128,16,448]{2,1,0:T(8,128)(2,1)} %bitcast.17), calls=%async_computation.3 | async-start | bytes 4194304 | tf_op jit(solution)/shard_map/all_to_all | solution.py:94
  219.3 11.0 %copy-start.1 = (bf16[16,128,576]{1,2,0:T(8,128)(2,1)S(1)}, bf16[16,128,576]{1,2,0:T(8,128)(2,1)}, u32[]{:S(2)}) copy-start(bf16[16,128,576]{1,2,0:T(8,128)(2,1)} %param.13) | copy-start | bytes 7077892
Sparse Core Ops, SparseCore 0:
  48.9 26.7 all-gather.1

commit v2 on v0

--- a/solution.py
+++ b/solution.py
@@ -33,25 +33,38 @@
     local_rows = jnp.arange(rows, dtype=jnp.int32)
     parent = local_rows // BEAM * BEAM + parent_beam
     keys = jnp.concatenate([jnp.take(latent_cache, parent, axis=0), new_key[:, None, :]], axis=1)
-    scores = jnp.einsum("rhw,rcw->rhc", queries, keys, preferred_element_type=jnp.float32) * scale
-    shifted = jnp.exp(scores - jnp.max(scores, axis=-1, keepdims=True))
-    weights = (shifted / jnp.sum(shifted, axis=-1, keepdims=True)).astype(jnp.bfloat16)
-    latent_out = jnp.einsum(
-        "rhc,rcl->rhl", weights, keys[:, :, :latent], preferred_element_type=jnp.float32
-    ).astype(jnp.bfloat16)
-    by_heads = lax.all_to_all(latent_out, "member", split_axis=1, concat_axis=0, tiled=True)
-    per_head = jnp.einsum(
-        "rhl,hlv->rhv", by_heads, value_up, preferred_element_type=jnp.float32
-    ).astype(jnp.bfloat16)
-    per_head = per_head.reshape(per_head.shape[0], per_head.shape[1] * per_head.shape[2])
-    partial_sums = jnp.dot(
-        lax.all_gather(per_head, "group", axis=0, tiled=True),
-        out_proj,
-        preferred_element_type=jnp.float32,
-    )
-    attention = lax.psum_scatter(
-        partial_sums.astype(jnp.bfloat16), "member", scatter_dimension=0, tiled=True
-    ).astype(jnp.float32)
+    chunks = 2
+    step = rows // chunks
+    pieces = []
+    for c in range(chunks):
+        asked = queries[c * step:(c + 1) * step]
+        held = keys[c * step:(c + 1) * step]
+        scores = jnp.einsum("rhw,rcw->rhc", asked, held, preferred_element_type=jnp.float32) * scale
+        shifted = jnp.exp(scores - jnp.max(scores, axis=-1, keepdims=True))
+        weights = (shifted / jnp.sum(shifted, axis=-1, keepdims=True)).astype(jnp.bfloat16)
+        latent_out = jnp.einsum(
+            "rhc,rcl->rhl", weights, held[:, :, :latent], preferred_element_type=jnp.float32
+        ).astype(jnp.bfloat16)
+        by_heads = lax.all_to_all(latent_out, "member", split_axis=1, concat_axis=0, tiled=True)
+        per_head = jnp.einsum(
+            "rhl,hlv->rhv", by_heads, value_up, preferred_element_type=jnp.float32
+        ).astype(jnp.bfloat16)
+        per_head = per_head.reshape(per_head.shape[0], per_head.shape[1] * per_head.shape[2])
+        partial_sums = jnp.dot(
+            lax.all_gather(per_head, "group", axis=0, tiled=True),
+            out_proj,
+            preferred_element_type=jnp.float32,
+        )
+        arrived_sums = lax.all_to_all(
+            partial_sums.astype(jnp.bfloat16).reshape(members, -1, columns),
+            "member",
+            split_axis=0,
+            concat_axis=0,
+            tiled=True,
+        )
+        summed = jnp.sum(arrived_sums.astype(jnp.float32), axis=0)
+        pieces.append(summed.reshape(-1, step, columns))
+    attention = jnp.stack(pieces, axis=1).reshape(-1, columns)
     hidden_in = (residual.astype(jnp.float32) + attention).astype(jnp.bfloat16)
     block_rows = hidden_in.shape[0]
     capacity = max(2, 2 * rows * TOP // members)

time: 280 us -> 238 us (0.85)
  waiting for transfers between devices: 121 us -> 55.9 us
  starting transfers between devices: 6.07 us -> 19.2 us
  matrix products: 26.9 us -> 32.7 us
  blocking collectives: 62.9 us -> 68.6 us
    unnamed x3 -> x2, waiting for transfers between devices: 65.7 us -> 0.03 us
    all_to_all x0 -> x2, starting transfers between devices: none -> 13.4 us  [per_device(): lax.all_to_all(partial_sums.astype(jnp.bfloat16).reshape(members, -1, col...]
    all_to_all x0 -> x2, waiting for transfers between devices: none -> 7.28 us  [per_device(): lax.all_to_all(partial_sums.astype(jnp.bfloat16).reshape(members, -1, col...]
    all_to_all x1 -> x2, blocking collectives: 24.3 us -> 31.1 us  [per_device(): lax.all_to_all(latent_out, 'member', split_axis=1, concat_axis=0, tiled=T...]
    all_gather x1 -> x2, waiting for transfers between devices: 26.7 us -> 20.2 us  [per_device(): lax.all_gather(per_head, 'group', axis=0, tiled=True)]
    convert_element_type x1 -> x5, local copies, waits for them, and re-layouts: 0.59 us -> 4.02 us  [the longest x2 2.65 us: per_device(): partial_sums.astype(jnp.bfloat16).reshape(members, -1, columns)]
    unnamed x26 -> x25, local copies, waits for them, and re-layouts: 5.46 us -> 2.65 us
    dot_general x2 -> x4, matrix products: 4.82 us -> 7.45 us  [the longest x2 4.61 us: per_device(): jnp.einsum('rhc,rcl->rhl', weights, held[:, :, :latent], preferred_elemen...]
  transfers between devices with their start and end apart: 3 -> 5, of which waited for: 3 -> 4; matrix products, arithmetic and copies ran while one was open for 3% -> 9% of each run, Pallas kernels for 0% -> 0%
where the time goes in v2:
time: 238 us; the launch traced here: 237 us
  blocking collectives  68.6 us (29%)
  waiting for transfers between devices  55.9 us (23%)
  local copies, waits for them, and re-layouts  33.5 us (14%)
  matrix products  32.7 us (14%)
  starting transfers between devices  19.2 us (8%)
  between operations  13.7 us (6%)
  other arithmetic  13.5 us (6%)
    all_to_all x1, blocking collectives, per_device(): lax.all_to_all(outgoing.reshape(experts, capacity, columns), ('group', 'm...  37.5 us
    all_to_all x2, blocking collectives, per_device(): lax.all_to_all(latent_out, 'member', split_axis=1, concat_axis=0, tiled=T...  31.1 us
    all_to_all x1, waiting for transfers between devices, per_device(): lax.all_to_all(arranged, ('group', 'member'), split_axis=0, concat_axis=0...  28.5 us
    all_gather x2, waiting for transfers between devices, per_device(): lax.all_gather(per_head, 'group', axis=0, tiled=True)  20.2 us
    all_to_all x2, starting transfers between devices, per_device(): lax.all_to_all(partial_sums.astype(jnp.bfloat16).reshape(members, -1, col...  13.4 us
    dot_general x1, matrix products, per_device(): jnp.dot(inner, w_down[0], preferred_element_type=jnp.float32)  10.8 us
    reduce_or x1, other arithmetic, per_device(): send_map = jnp.any(matches, axis=2).astype(jnp.bfloat16)  7.43 us
    all_to_all x2, waiting for transfers between devices, per_device(): lax.all_to_all(partial_sums.astype(jnp.bfloat16).reshape(members, -1, col...  7.28 us
  transfers between devices with their start and end apart: 5, of which 4 were waited for; matrix products, arithmetic and copies ran while one was open for 9% of the time, Pallas kernels for 0%

profile of v2, /device:TPU:1, one launch (start us, length us, event | category | flops | bytes accessed | tf_op | source)
XLA Modules:
  0.0 237.2 jit_solution(4019409785269201127)
XLA Ops:
  8.2 2.3 gather_fusion
  10.5 4.3 %copy.88 = bf16[16,128,576]{2,1,0:T(8,128)(2,1)} copy(bf16[16,128,576]{1,2,0:T(8,128)(2,1)} %gather_fusion) | data formatting | bytes 4718592 | tf_op jit(solution)/shard_map/jit(_take)/gather | solution.py:35
  14.9 2.2 broadcast_select_fusion
  18.8 2.3 convolution_convert_fusion.4
  21.5 18.6 %all_to_all.56 = bf16[8,64,512]{2,0,1:T(8,128)(2,1)S(1)} all-to-all(bf16[8,64,512]{2,0,1:T(8,128)(2,1)S(1)} %copy.90), channel_id=1, replica_groups=mesh['group'=8,'member'=16] {'member'}, dimensions={1} | all-to-all | bytes 1048576 | tf_op jit(solution)/shard_map/all_to_all | solution.py:48
  41.1 2.2 fusion.28
  43.5 2.3 convolution_convert_fusion.3
  46.1 12.5 %all_to_all.57 = bf16[8,64,512]{2,0,1:T(8,128)(2,1)S(1)} all-to-all(bf16[8,64,512]{2,0,1:T(8,128)(2,1)S(1)} %copy.94), channel_id=1, replica_groups=mesh['group'=8,'member'=16] {'member'}, dimensions={1} | all-to-all | bytes 1048576 | tf_op jit(solution)/shard_map/all_to_all | solution.py:48
  59.6 4.7 %all-gather.3.cloned.1.call-done = bf16[1024,512]{0,1:T(8,128)(2,1)} async-done(((bf16[128,512]{0,1:T(8,128)(2,1)}), bf16[1024,512]{0,1:T(8,128)(2,1)}) %all-gather.3.cloned.1.call-update) | async-done | bytes 1048592 | tf_op jit(solution)/shard_map/all_gather | solution.py:54
  67.5 6.7 %all-to-all-start.1 = ((bf16[16,64,448]{2,1,0:T(8,128)(2,1)}), bf16[16,64,448]{2,1,0:T(8,128)(2,1)S(1)}, u32[]{:S(2)}, u32[]{:S(2)}) async-start(bf16[16,64,448]{2,1,0:T(8,128)(2,1)} %bitcast.7), calls=%async_computation.1 | async-start | bytes 2097152 | tf_op jit(solution)/shard_map/all_to_all | solution.py:58
  74.8 15.5 %all-gather.5.cloned.1.call-done = bf16[1024,512]{0,1:T(8,128)(2,1)} async-done(((bf16[128,512]{0,1:T(8,128)(2,1)}), bf16[1024,512]{0,1:T(8,128)(2,1)}) %all-gather.5.cloned.1.call-update) | async-done | bytes 1048592 | tf_op jit(solution)/shard_map/all_gather | solution.py:54
  93.4 6.7 %all-to-all-start.3 = ((bf16[16,64,448]{2,1,0:T(8,128)(2,1)}), bf16[16,64,448]{2,1,0:T(8,128)(2,1)S(1)}, u32[]{:S(2)}, u32[]{:S(2)}) async-start(bf16[16,64,448]{2,1,0:T(8,128)(2,1)} %bitcast.15), calls=%async_computation.3 | async-start | bytes 2097152 | tf_op jit(solution)/shard_map/all_to_all | solution.py:58
  101.0 7.4 %fusion.2 = pred[2048,128]{1,0:T(8,128)(4,1)S(1)} fusion(s32[128,8]{0,1:T(8,128)S(1)} %get-tuple-element.6), kind=kLoop, calls=%fused_computation.5 | loop fusion | flops 3932160 | bytes 266240 | tf_op jit(solution)/shard_map/reduce_or | solution.py:79
  108.6 7.3 %all-to-all-done.3 = bf16[16,64,448]{2,1,0:T(8,128)(2,1)S(1)} async-done(((bf16[16,64,448]{2,1,0:T(8,128)(2,1)}), bf16[16,64,448]{2,1,0:T(8,128)(2,1)S(1)}, u32[]{:S(2)}, u32[]{:S(2)}) %all-to-all-start.3) | async-done | bytes 917536 | tf_op jit(solution)/shard_map/all_to_all | solution.py:58
  118.1 2.8 %copy.105 = bf16[2048,448]{1,0:T(8,128)(2,1)S(1)} copy(bf16[2048,448]{0,1:T(8,128)(2,1)} %convolution_convert_fusion) | data formatting | bytes 3670016 | tf_op jit(solution)/shard_map/convert_element_type | solution.py:80
  120.9 37.5 %all_to_all.58 = bf16[128,16,448]{2,1,0:T(8,128)(2,1)S(1)} all-to-all(bf16[128,16,448]{2,1,0:T(8,128)(2,1)S(1)} %bitcast.86), channel_id=1, replica_groups=mesh['group'=8,'member'=16] {'group','member'}, dimensions={0} | all-to-all | bytes 3670016 | tf_op jit(solution)/shard_map/all_to_all | solution.py:81
  159.9 3.3 %reshape.88 = bf16[256,3584]{1,0:T(8,128)(2,1)} reshape(bf16[16,16,8,448]{3,2,1,0:T(8,128)(2,1)S(1)} %bitcast.88) | data formatting | bytes 3670016 | tf_op jit(solution)/shard_map/reshape | solution.py:91
  163.2 6.8 %fusion.7 = f32[256,1024]{1,0:T(8,128)} fusion(bf16[256,3584]{1,0:T(8,128)(2,1)} %reshape.88, bf16[1,3584,1024]{2,1,0:T(8,128)(2,1)} %param.21), kind=kOutput, calls=%fused_computation.10 | convolution fusion | flops 1879048192 | bytes 10223616 | tf_op jit(solution)/shard_map/dot_general | solution.py:93
  170.0 10.8 %fusion.9 = bf16[256,3584]{1,0:T(8,128)(2,1)} fusion(bf16[1,1024,3584]{2,1,0:T(8,128)(2,1)} %param.23, bf16[256,3584]{1,0:T(8,128)(2,1)S(1)} %copy-done.4, bf16[1,3584,1024]{2,1,0:T(8,128)(2,1)} %param.22, f32[256,1024]{1,0:T(8,128)} %fusion.7), kind=kOutput, calls=%fused_computation.12 | convolution fusion | flops 3760586752 | bytes 19398656 | tf_op jit(solution)/shard_map/dot_general | solution.py:96
  180.8 3.9 %reshape.89 = bf16[16,16,8,448]{3,2,1,0:T(8,128)(2,1)S(1)} reshape(bf16[256,3584]{1,0:T(8,128)(2,1)} %fusion.9) | data formatting | bytes 3670016 | tf_op jit(solution)/shard_map/reshape | solution.py:98
  184.7 2.0 copy.107
  186.7 5.8 %all-to-all-start.5 = ((bf16[128,16,448]{2,1,0:T(8,128)(2,1)}), bf16[128,16,448]{2,1,0:T(8,128)(2,1)}, u32[]{:S(2)}, u32[]{:S(2)}) async-start(bf16[128,16,448]{2,1,0:T(8,128)(2,1)} %bitcast.28), calls=%async_computation.5 | async-start | bytes 4194304 | tf_op jit(solution)/shard_map/all_to_all | solution.py:102
  193.5 28.5 %all-to-all-done.5 = bf16[128,16,448]{2,1,0:T(8,128)(2,1)} async-done(((bf16[128,16,448]{2,1,0:T(8,128)(2,1)}), bf16[128,16,448]{2,1,0:T(8,128)(2,1)}, u32[]{:S(2)}, u32[]{:S(2)}) %all-to-all-start.5) | async-done | bytes 1835040 | tf_op jit(solution)/shard_map/all_to_all | solution.py:102
  222.0 6.0 %gather_fusion.1 = bf16[1024,448]{1,0:T(8,128)(2,1)S(1)} fusion(bf16[2048,448]{1,0:T(8,128)(2,1)} %bitcast.29, s32[1024]{0:T(1024)S(1)} %broadcast_clamp_fusion), kind=kCustom, calls=%fused_computation.1 | custom fusion | bytes 1839104 | tf_op jit(solution)/shard_map/gather | solution.py:106
  (70 shorter events, 21.2 us)
Async XLA Ops:
  6.5 1.7 copy-start
  6.5 57.8 %all-gather.3.cloned.1.call-start = ((), (), s32[]{:S(2)}) async-start(), calls=%async_computation.6 | async-start | bytes 1179648 | tf_op jit(solution)/shard_map/all_gather | solution.py:54
  10.5 4.3 %copy-start.6 = (bf16[16,576]{1,0:T(8,128)(2,1)S(1)}, bf16[16,576]{1,0:T(8,128)(2,1)}, u32[]{:S(2)}) copy-start(bf16[16,576]{1,0:T(8,128)(2,1)} %param.14) | copy-start | bytes 55300
  14.9 2.2 copy-start.9
  17.1 1.5 copy-start.2
  18.8 21.2 %copy-start.3 = (bf16[4,512,128]{2,1,0:T(8,128)(2,1)S(1)}, bf16[4,512,128]{2,1,0:T(8,128)(2,1)}, u32[]{:S(2)}) copy-start(bf16[4,512,128]{2,1,0:T(8,128)(2,1)} %param.16) | copy-start | bytes 1572868
  41.1 49.2 %all-gather.5.cloned.1.call-start = ((), (), s32[]{:S(2)}) async-start(), calls=%async_computation.7 | async-start | bytes 1179648 | tf_op jit(solution)/shard_map/all_gather | solution.py:54
  45.8 18.5 %copy-start.10 = (bf16[512,448]{0,1:T(8,128)(2,1)S(1)}, bf16[512,448]{0,1:T(8,128)(2,1)}, u32[]{:S(2)}) copy-start(bf16[512,448]{0,1:T(8,128)(2,1)} %param.17) | copy-start | bytes 1376260
  66.2 8.0 %copy-start.7 = (s32[128,8]{0,1:T(8,128)S(1)}, s32[128,8]{0,1:T(8,128)}, u32[]{:S(2)}) copy-start(s32[128,8]{0,1:T(8,128)} %param.19) | copy-start | bytes 12292
  67.5 25.9 %all-to-all-start.1 = ((bf16[16,64,448]{2,1,0:T(8,128)(2,1)}), bf16[16,64,448]{2,1,0:T(8,128)(2,1)S(1)}, u32[]{:S(2)}, u32[]{:S(2)}) async-start(bf16[16,64,448]{2,1,0:T(8,128)(2,1)} %bitcast.7), calls=%async_computation.1 | async-start | bytes 2097152 | tf_op jit(solution)/shard_map/all_to_all | solution.py:58
  92.1 8.2 %copy-start.5 = (bf16[128,448]{0,1:T(8,128)(2,1)S(1)}, bf16[128,448]{0,1:T(8,128)(2,1)}, u32[]{:S(2)}) copy-start(bf16[128,448]{0,1:T(8,128)(2,1)} %param.18) | copy-start | bytes 344068
  93.4 22.5 %all-to-all-start.3 = ((bf16[16,64,448]{2,1,0:T(8,128)(2,1)}), bf16[16,64,448]{2,1,0:T(8,128)(2,1)S(1)}, u32[]{:S(2)}, u32[]{:S(2)}) async-start(bf16[16,64,448]{2,1,0:T(8,128)(2,1)} %bitcast.15), calls=%async_computation.3 | async-start | bytes 2097152 | tf_op jit(solution)/shard_map/all_to_all | solution.py:58
  163.2 6.8 %copy-start.4 = (bf16[256,3584]{1,0:T(8,128)(2,1)S(1)}, bf16[256,3584]{1,0:T(8,128)(2,1)}, u32[]{:S(2)}) copy-start(bf16[256,3584]{1,0:T(8,128)(2,1)} %reshape.88) | copy-start | bytes 5505028
  186.7 6.1 %copy-start.8 = (f32[128,8]{0,1:T(8,128)S(1)}, f32[128,8]{0,1:T(8,128)}, u32[]{:S(2)}) copy-start(f32[128,8]{0,1:T(8,128)} %param.20) | copy-start | bytes 12292
  186.7 35.3 %all-to-all-start.5 = ((bf16[128,16,448]{2,1,0:T(8,128)(2,1)}), bf16[128,16,448]{2,1,0:T(8,128)(2,1)}, u32[]{:S(2)}, u32[]{:S(2)}) async-start(bf16[128,16,448]{2,1,0:T(8,128)(2,1)} %bitcast.28), calls=%async_computation.5 | async-start | bytes 4194304 | tf_op jit(solution)/shard_map/all_to_all | solution.py:102
  222.0 8.4 %copy-start.1 = (bf16[16,128,576]{1,2,0:T(8,128)(2,1)S(1)}, bf16[16,128,576]{1,2,0:T(8,128)(2,1)}, u32[]{:S(2)}) copy-start(bf16[16,128,576]{1,2,0:T(8,128)(2,1)} %param.13) | copy-start | bytes 7077892
Sparse Core Ops, SparseCore 0:
  41.2 23.0 all-gather.2
  66.0 24.2 all-gather.4

commit v3 on v1

--- a/solution.py
+++ b/solution.py
@@ -77,26 +77,38 @@
         concat_axis=0,
         tiled=True,
     )
-    expert_rows = (
-        arrived.reshape(groups, members, capacity, columns)
-        .transpose(1, 2, 0, 3)
-        .reshape(members * capacity, groups * columns)
+    arrived = arrived.reshape(groups, members * capacity, columns)
+    gate = jnp.einsum(
+        "gsc,gcf->sf", arrived, w_gate[0].reshape(groups, columns, -1),
+        preferred_element_type=jnp.float32,
     )
-    gate = jnp.dot(expert_rows, w_gate[0], preferred_element_type=jnp.float32)
-    upper = jnp.dot(expert_rows, w_up[0], preferred_element_type=jnp.float32)
+    upper = jnp.einsum(
+        "gsc,gcf->sf", arrived, w_up[0].reshape(groups, columns, -1),
+        preferred_element_type=jnp.float32,
+    )
     inner = (jax.nn.silu(gate) * upper).astype(jnp.bfloat16)
-    results = jnp.dot(inner, w_down[0], preferred_element_type=jnp.float32).astype(jnp.bfloat16)
-    arranged = (
-        results.reshape(members, capacity, groups, columns)
-        .transpose(2, 0, 1, 3)
-        .reshape(experts, capacity, columns)
-    )
+    results = jnp.einsum(
+        "sf,fgc->gsc", inner, w_down[0].reshape(-1, groups, columns),
+        preferred_element_type=jnp.float32,
+    ).astype(jnp.bfloat16)
     returned = lax.all_to_all(
-        arranged, ("group", "member"), split_axis=0, concat_axis=0, tiled=True
+        results.reshape(experts, capacity, columns),
+        ("group", "member"),
+        split_axis=0,
+        concat_axis=0,
+        tiled=True,
     )
     returned = returned.reshape(experts * capacity, columns)
-    picked = returned[slot_index.reshape(block_rows, TOP)].astype(jnp.float32)
-    mixed = jnp.sum(route_gates[:, :, None] * picked, axis=1)
+    slots = slot_index.reshape(block_rows, TOP)
+    gate_hi = route_gates.astype(jnp.bfloat16)
+    gate_lo = (route_gates - gate_hi.astype(jnp.float32)).astype(jnp.bfloat16)
+    hit = slots[:, :, None] == positions[None, None, :]
+    zero = jnp.zeros((), jnp.bfloat16)
+    map_hi = jnp.sum(jnp.where(hit, gate_hi[:, :, None], zero), axis=1)
+    map_lo = jnp.sum(jnp.where(hit, gate_lo[:, :, None], zero), axis=1)
+    mixed = jnp.dot(map_hi, returned, preferred_element_type=jnp.float32) + jnp.dot(
+        map_lo, returned, preferred_element_type=jnp.float32
+    )
     return (hidden_in.astype(jnp.float32) + mixed).astype(jnp.bfloat16)
 
 

time: 238 us -> 222 us (0.933)
  blocking collectives: 61.2 us -> 24.3 us
  waiting for transfers between devices: 72.9 us -> 87.3 us
  starting transfers between devices: 12.7 us -> 20.2 us
  local copies, waits for them, and re-layouts: 32.9 us -> 27.9 us
  matrix products: 28.3 us -> 30.9 us
    all_to_all x1 -> x0, blocking collectives: 37 us -> none  [per_device(): lax.all_to_all(outgoing.reshape(experts, capacity, columns), ('group', 'm...]
    all_to_all x1 -> x2, waiting for transfers between devices: 28.5 us -> 42.9 us  [the longest x1 23.7 us: per_device(): lax.all_to_all(results.reshape(experts, capacity, columns), ('group', 'me...]
    reshape x4 -> x0, local copies, waits for them, and re-layouts: 10.6 us -> none  [the longest x2 5.89 us: per_device(): results.reshape(members, capacity, groups, columns).transpose(2, 0, 1, 3)]
    unnamed x26 -> x24, local copies, waits for them, and re-layouts: 2.65 us -> 11.7 us
    all_to_all x1 -> x2, starting transfers between devices: 5.85 us -> 13.4 us  [the longest x1 7.54 us: per_device(): lax.all_to_all(outgoing.reshape(experts, capacity, columns), ('group', 'm...]
    gather x1 -> x0, local copies, waits for them, and re-layouts: 6 us -> none  [per_device(): picked = returned[slot_index.reshape(block_rows, TOP)].astype(jnp.float32)]
    convert_element_type x0 -> x3, local copies, waits for them, and re-layouts: none -> 4.07 us  [the longest x1 3.83 us: per_device(): results = jnp.einsum('sf,fgc->gsc', inner, w_down[0].reshape(-1, groups,...]
    dot_general x2 -> x4, matrix products: 17.6 us -> 21.5 us  [the longest x1 10.7 us: per_device(): jnp.einsum('sf,fgc->gsc', inner, w_down[0].reshape(-1, groups, columns),...]
  transfers between devices with their start and end apart: 3 -> 4, of which waited for: 3 -> 4; matrix products, arithmetic and copies ran while one was open for 4% -> 11% of each run, Pallas kernels for 0% -> 0%
where the time goes in v3:
time: 222 us; the launch traced here: 221 us
  waiting for transfers between devices  87.3 us (39%)
  matrix products  30.9 us (14%)
  local copies, waits for them, and re-layouts  27.9 us (13%)
  blocking collectives  24.3 us (11%)
  starting transfers between devices  20.2 us (9%)
  other arithmetic  17.1 us (8%)
  between operations  13.6 us (6%)
    all_gather x1, waiting for transfers between devices, per_device(): lax.all_gather(per_head, 'group', axis=0, tiled=True)  26.9 us
    all_to_all x1, blocking collectives, per_device(): lax.all_to_all(latent_out, 'member', split_axis=1, concat_axis=0, tiled=T...  24.3 us
    all_to_all x1, waiting for transfers between devices, per_device(): lax.all_to_all(results.reshape(experts, capacity, columns), ('group', 'me...  23.7 us
    all_to_all x1, waiting for transfers between devices, per_device(): lax.all_to_all(outgoing.reshape(experts, capacity, columns), ('group', 'm...  19.2 us
    all_to_all x1, waiting for transfers between devices, per_device(): lax.all_to_all(partial_sums.astype(jnp.bfloat16).reshape(members, -1, col...  17.5 us
    unnamed x24, local copies, waits for them, and re-layouts  11.7 us
    dot_general x1, matrix products, per_device(): jnp.einsum('sf,fgc->gsc', inner, w_down[0].reshape(-1, groups, columns),...  10.7 us
    all_to_all x1, starting transfers between devices, per_device(): lax.all_to_all(outgoing.reshape(experts, capacity, columns), ('group', 'm...  7.54 us
  transfers between devices with their start and end apart: 4, of which 4 were waited for; matrix products, arithmetic and copies ran while one was open for 11% of the time, Pallas kernels for 0%

profile of v3, /device:TPU:1, one launch (start us, length us, event | category | flops | bytes accessed | tf_op | source)
XLA Modules:
  0.0 221.3 jit_solution(5911754844365213980)
XLA Ops:
  8.2 2.3 %gather_fusion = bf16[16,128,576]{1,2,0:T(8,128)(2,1)} fusion(bf16[16,128,576]{1,2,0:T(8,128)(2,1)S(1)} %copy-done, s32[1024]{0:T(1024)S(1)} %pad_clamp_fusion), kind=kCustom, calls=%fused_computation | custom fusion | bytes 4718656 | tf_op jit(solution)/shard_map/jit(_take)/gather | solution.py:35
  10.5 4.3 %copy.75 = bf16[16,128,576]{2,1,0:T(8,128)(2,1)} copy(bf16[16,128,576]{1,2,0:T(8,128)(2,1)} %gather_fusion) | data formatting | bytes 4718592 | tf_op jit(solution)/shard_map/jit(_take)/gather | solution.py:35
  14.9 2.2 broadcast_select_fusion
  17.1 1.2 fusion.24
  19.0 3.6 %fusion.15 = bf16[16,64,512]{2,1,0:T(8,128)(2,1)S(1)} fusion(bf16[16,1,576]{2,1,0:T(2,128)(2,1)S(1)} %copy.76, bf16[16,128,576]{2,1,0:T(8,128)(2,1)} %copy-done.2, f32[16,64]{1,0:T(8,128)S(1)} %fusion.44, f32[16,64,129]{2,1,0:T(8,128)S(1)} %fusion.24), kind=kOutput, calls=%fused_computation.24 | convolution fusion | flops 140415104 | bytes 3958784 | tf_op jit(solution)/shard_map/rhc,rcl->rhl/dot_general | solution.py:39
  23.1 24.3 %all_to_all.33 = bf16[16,64,512]{2,0,1:T(8,128)(2,1)S(1)} all-to-all(bf16[16,64,512]{2,0,1:T(8,128)(2,1)S(1)} %copy.77), channel_id=1, replica_groups=mesh['group'=8,'member'=16] {'member'}, dimensions={1} | all-to-all | bytes 2097152 | tf_op jit(solution)/shard_map/all_to_all | solution.py:42
  48.8 26.9 %all-gather.2.cloned.1.call-done = bf16[2048,512]{0,1:T(8,128)(2,1)} async-done(((bf16[256,512]{0,1:T(8,128)(2,1)}), bf16[2048,512]{0,1:T(8,128)(2,1)}) %all-gather.2.cloned.1.call-update) | async-done | bytes 2097168 | tf_op jit(solution)/shard_map/all_gather | solution.py:48
  75.7 2.7 %fusion.14 = bf16[56,16,8,128]{3,2,1,0:T(8,128)(2,1)S(1)} fusion(bf16[512,448]{0,1:T(8,128)(2,1)S(1)} %copy-done.10, bf16[2048,512]{0,1:T(8,128)(2,1)} %all-gather.2.cloned.1.call-done), kind=kOutput, calls=%fused_computation.23 | convolution fusion | flops 940441600 | bytes 4390912 | tf_op jit(solution)/shard_map/dot_general | solution.py:47
  78.4 1.7 copy.99
  80.1 6.8 %all-to-all-start.1 = ((bf16[16,128,448]{1,2,0:T(8,128)(2,1)}), bf16[16,128,448]{1,2,0:T(8,128)(2,1)S(1)}, u32[]{:S(2)}, u32[]{:S(2)}) async-start(bf16[16,128,448]{1,2,0:T(8,128)(2,1)} %bitcast.66), calls=%async_computation.1 | async-start | bytes 3670016 | tf_op jit(solution)/shard_map/all_to_all | solution.py:52
  88.3 7.4 %fusion.3 = pred[2048,128]{1,0:T(8,128)(4,1)S(1)} fusion(s32[128,8]{0,1:T(8,128)S(1)} %multiply_add_fusion), kind=kLoop, calls=%fused_computation.6 | loop fusion | flops 3932160 | bytes 266240 | tf_op jit(solution)/shard_map/reduce_or | solution.py:71
  95.7 17.5 %all-to-all-done.1 = bf16[16,128,448]{1,2,0:T(8,128)(2,1)S(1)} async-done(((bf16[16,128,448]{1,2,0:T(8,128)(2,1)}), bf16[16,128,448]{1,2,0:T(8,128)(2,1)S(1)}, u32[]{:S(2)}, u32[]{:S(2)}) %all-to-all-start.1) | async-done | bytes 1835040 | tf_op jit(solution)/shard_map/all_to_all | solution.py:52
  114.2 2.5 %copy.88 = bf16[2048,448]{1,0:T(8,128)(2,1)} copy(bf16[2048,448]{0,1:T(8,128)(2,1)S(1)} %convolution_convert_fusion.1) | data formatting | bytes 3670016 | tf_op jit(solution)/shard_map/convert_element_type | solution.py:72
  116.6 7.5 %all-to-all-start.2 = ((bf16[128,16,448]{2,1,0:T(8,128)(2,1)}), bf16[128,16,448]{2,1,0:T(8,128)(2,1)S(1)}, u32[]{:S(2)}, u32[]{:S(2)}) async-start(bf16[128,16,448]{2,1,0:T(8,128)(2,1)} %bitcast.10), calls=%async_computation.2 | async-start | bytes 4194304 | tf_op jit(solution)/shard_map/all_to_all | solution.py:73
  124.2 10.4 %copy.91 = bf16[1,1024,3584]{1,2,0:T(8,128)(2,1)} copy(bf16[1,1024,3584]{2,1,0:T(8,128)(2,1)} %param.23) | data formatting | bytes 14680064 | tf_op args[11]
  134.6 19.2 %all-to-all-done.2 = bf16[128,16,448]{2,1,0:T(8,128)(2,1)S(1)} async-done(((bf16[128,16,448]{2,1,0:T(8,128)(2,1)}), bf16[128,16,448]{2,1,0:T(8,128)(2,1)S(1)}, u32[]{:S(2)}, u32[]{:S(2)}) %all-to-all-start.2) | async-done | bytes 1835040 | tf_op jit(solution)/shard_map/all_to_all | solution.py:73
  153.8 5.1 %convolution_bitcast_fusion.1 = f32[256,1024]{1,0:T(8,128)S(1)} fusion(bf16[8,256,448]{2,1,0:T(8,128)(2,1)S(1)} %bitcast.70, bf16[8,448,1024]{2,1,0:T(8,128)(2,1)} %bitcast.74), kind=kOutput, calls=%fused_computation.29 | convolution fusion | flops 1879048192 | bytes 10223616 | tf_op jit(solution)/shard_map/gsc,gcf->sf/dot_general | solution.py:81
  159.0 10.7 %convert_bitcast_fusion = bf16[8,256,448]{1,2,0:T(8,128)(2,1)} fusion(bf16[1024,8,448]{0,2,1:T(8,128)(2,1)} %bitcast.67, bf16[8,256,448]{2,1,0:T(8,128)(2,1)S(1)} %bitcast.71, bf16[8,448,1024]{2,1,0:T(8,128)(2,1)} %bitcast.75, f32[256,1024]{1,0:T(8,128)S(1)} %convolution_bitcast_fusion.1), kind=kOutput, calls=%fused_computation.22 | convolution fusion | flops 3760586752 | bytes 19398656 | tf_op jit(solution)/shard_map/sf,fgc->gsc/dot_general | solution.py:90
  169.7 3.8 %copy.92 = bf16[8,256,448]{2,1,0:T(8,128)(2,1)} copy(bf16[8,256,448]{1,2,0:T(8,128)(2,1)} %convert_bitcast_fusion) | data formatting | bytes 3670016 | tf_op jit(solution)/shard_map/convert_element_type | solution.py:93
  173.5 5.8 %all-to-all-start.3 = ((bf16[128,16,448]{2,1,0:T(8,128)(2,1)}), bf16[128,16,448]{2,1,0:T(8,128)(2,1)}, u32[]{:S(2)}, u32[]{:S(2)}) async-start(bf16[128,16,448]{2,1,0:T(8,128)(2,1)} %bitcast.19), calls=%async_computation.3 | async-start | bytes 4194304 | tf_op jit(solution)/shard_map/all_to_all | solution.py:94
  179.7 5.4 %fusion.5 = (bf16[128,2048]{1,0:T(8,128)(2,1)S(1)}, bf16[128,2048]{1,0:T(8,128)(2,1)S(1)}) fusion(s32[128,8]{1,0:T(8,128)S(1)} %copy.86, bf16[128,8]{1,0:T(8,128)(2,1)S(1)} %copy.93, bf16[128,8]{1,0:T(8,128)(2,1)S(1)} %copy.87), kind=kLoop, calls=%fused_computation.8 | loop fusion | flops 9961472 | bytes 1056768 | tf_op jit(solution)/shard_map/reduce_sum | solution.py:108
  185.1 23.7 %all-to-all-done.3 = bf16[128,16,448]{2,1,0:T(8,128)(2,1)} async-done(((bf16[128,16,448]{2,1,0:T(8,128)(2,1)}), bf16[128,16,448]{2,1,0:T(8,128)(2,1)}, u32[]{:S(2)}, u32[]{:S(2)}) %all-to-all-start.3) | async-done | bytes 1835040 | tf_op jit(solution)/shard_map/all_to_all | solution.py:94
  208.8 2.6 %fusion.45 = f32[128,448]{0,1:T(8,128)S(1)} fusion(bf16[128,2048]{1,0:T(8,128)(2,1)S(1)} %get-tuple-element.6, bf16[2048,448]{1,0:T(8,128)(2,1)} %bitcast.20), kind=kOutput, calls=%fused_computation.68 | convolution fusion | flops 234881024 | bytes 2588672 | tf_op jit(solution)/shard_map/dot_general | solution.py:109
  211.4 3.0 %fusion.30 = bf16[128,448]{0,1:T(8,128)(2,1)} fusion(f32[128,448]{0,1:T(8,128)S(1)} %fusion.45, bf16[128,2048]{1,0:T(8,128)(2,1)S(1)} %get-tuple-element.5, bf16[2048,448]{1,0:T(8,128)(2,1)} %bitcast.20, f32[128,448]{0,1:T(8,128)} %copy-done.3, bf16[128,448]{0,1:T(8,128)(2,1)S(1)} %copy-done.5), kind=kOutput, calls=%fused_computation.37 | convolution fusion | flops 235282432 | bytes 3047424 | tf_op jit(solution)/shard_map/dot_general | solution.py:109
  (51 shorter events, 6.8 us)
Async XLA Ops:
  6.5 1.7 copy-start
  6.5 69.1 %all-gather.2.cloned.1.call-start = ((), (), s32[]{:S(2)}) async-start(), calls=%async_computation.4 | async-start | bytes 2359296 | tf_op jit(solution)/shard_map/all_gather | solution.py:48
  10.5 4.3 %copy-start.6 = (bf16[16,576]{1,0:T(8,128)(2,1)S(1)}, bf16[16,576]{1,0:T(8,128)(2,1)}, u32[]{:S(2)}) copy-start(bf16[16,576]{1,0:T(8,128)(2,1)} %param.14) | copy-start | bytes 55300
  14.9 2.2 copy-start.9
  17.1 1.5 copy-start.2
  23.1 24.4 %copy-start.4 = (bf16[4,512,128]{2,1,0:T(8,128)(2,1)S(1)}, bf16[4,512,128]{2,1,0:T(8,128)(2,1)}, u32[]{:S(2)}) copy-start(bf16[4,512,128]{2,1,0:T(8,128)(2,1)} %param.16) | copy-start | bytes 1572868
  47.4 28.2 %copy-start.10 = (bf16[512,448]{0,1:T(8,128)(2,1)S(1)}, bf16[512,448]{0,1:T(8,128)(2,1)}, u32[]{:S(2)}) copy-start(bf16[512,448]{0,1:T(8,128)(2,1)} %param.17) | copy-start | bytes 1376260
  80.1 6.8 %copy-start.7 = (s32[128,8]{0,1:T(8,128)S(1)}, s32[128,8]{0,1:T(8,128)}, u32[]{:S(2)}) copy-start(s32[128,8]{0,1:T(8,128)} %param.19) | copy-start | bytes 12292
  80.1 33.1 %all-to-all-start.1 = ((bf16[16,128,448]{1,2,0:T(8,128)(2,1)}), bf16[16,128,448]{1,2,0:T(8,128)(2,1)S(1)}, u32[]{:S(2)}, u32[]{:S(2)}) async-start(bf16[16,128,448]{1,2,0:T(8,128)(2,1)} %bitcast.66), calls=%async_computation.1 | async-start | bytes 3670016 | tf_op jit(solution)/shard_map/all_to_all | solution.py:52
  87.5 25.9 %copy-start.5 = (bf16[128,448]{0,1:T(8,128)(2,1)S(1)}, bf16[128,448]{0,1:T(8,128)(2,1)}, u32[]{:S(2)}) copy-start(bf16[128,448]{0,1:T(8,128)(2,1)} %param.18) | copy-start | bytes 344068
  113.5 3.2 %copy-start.3 = (f32[128,448]{0,1:T(8,128)}, f32[128,448]{0,1:T(8,128)S(1)}, u32[]{:S(2)}) copy-start(f32[128,448]{0,1:T(8,128)S(1)} %convert_reduce_fusion) | copy-start | bytes 688132
  116.6 37.2 %all-to-all-start.2 = ((bf16[128,16,448]{2,1,0:T(8,128)(2,1)}), bf16[128,16,448]{2,1,0:T(8,128)(2,1)S(1)}, u32[]{:S(2)}, u32[]{:S(2)}) async-start(bf16[128,16,448]{2,1,0:T(8,128)(2,1)} %bitcast.10), calls=%async_computation.2 | async-start | bytes 4194304 | tf_op jit(solution)/shard_map/all_to_all | solution.py:73
  173.5 6.0 %copy-start.8 = (f32[128,8]{0,1:T(8,128)S(1)}, f32[128,8]{0,1:T(8,128)}, u32[]{:S(2)}) copy-start(f32[128,8]{0,1:T(8,128)} %param.20) | copy-start | bytes 12292
  173.5 35.3 %all-to-all-start.3 = ((bf16[128,16,448]{2,1,0:T(8,128)(2,1)}), bf16[128,16,448]{2,1,0:T(8,128)(2,1)}, u32[]{:S(2)}, u32[]{:S(2)}) async-start(bf16[128,16,448]{2,1,0:T(8,128)(2,1)} %bitcast.19), calls=%async_computation.3 | async-start | bytes 4194304 | tf_op jit(solution)/shard_map/all_to_all | solution.py:94
  208.8 5.7 %copy-start.1 = (bf16[16,128,576]{1,2,0:T(8,128)(2,1)S(1)}, bf16[16,128,576]{1,2,0:T(8,128)(2,1)}, u32[]{:S(2)}) copy-start(bf16[16,128,576]{1,2,0:T(8,128)(2,1)} %param.13) | copy-start | bytes 7077892
Sparse Core Ops, SparseCore 0:
  48.9 26.7 all-gather.1

commit v4 on v3

--- a/solution.py
+++ b/solution.py
@@ -26,7 +26,7 @@
     rows = queries.shape[0]
     latent = value_up.shape[1]
     members = lax.axis_size("member")
-    groups = lax.axis_size("group")
+    groups = lax.axis_size(("gy", "gc"))
     experts = groups * members
     columns = out_proj.shape[1]
     scale = (VHEAD + ROPE) ** (-0.5)
@@ -44,11 +44,15 @@
         "rhl,hlv->rhv", by_heads, value_up, preferred_element_type=jnp.float32
     ).astype(jnp.bfloat16)
     per_head = per_head.reshape(per_head.shape[0], per_head.shape[1] * per_head.shape[2])
-    partial_sums = jnp.dot(
-        lax.all_gather(per_head, "group", axis=0, tiled=True),
-        out_proj,
-        preferred_element_type=jnp.float32,
+    along_y = lax.all_gather(per_head, "gy", axis=0, tiled=True)
+    both_cores = lax.all_gather(along_y, "gc", axis=0, tiled=True)
+    cores = lax.axis_size("gc")
+    gathered = (
+        both_cores.reshape(cores, groups // cores, -1, per_head.shape[1])
+        .transpose(1, 0, 2, 3)
+        .reshape(-1, per_head.shape[1])
     )
+    partial_sums = jnp.dot(gathered, out_proj, preferred_element_type=jnp.float32)
     pieces = lax.all_to_all(
         partial_sums.astype(jnp.bfloat16).reshape(members, -1, columns),
         "member",
@@ -72,7 +76,7 @@
     outgoing = jnp.dot(send_map, hidden_in, preferred_element_type=jnp.float32).astype(jnp.bfloat16)
     arrived = lax.all_to_all(
         outgoing.reshape(experts, capacity, columns),
-        ("group", "member"),
+        ("gy", "gc", "member"),
         split_axis=0,
         concat_axis=0,
         tiled=True,
@@ -93,7 +97,7 @@
     ).astype(jnp.bfloat16)
     returned = lax.all_to_all(
         results.reshape(experts, capacity, columns),
-        ("group", "member"),
+        ("gy", "gc", "member"),
         split_axis=0,
         concat_axis=0,
         tiled=True,
@@ -113,21 +117,25 @@
 
 
 def solution(mesh):
+    shape = mesh.devices.shape
+    split = jax.sharding.Mesh(mesh.devices.reshape(shape[0] // 2, 2, shape[1]), ("gy", "gc", "member"))
+    group = ("gy", "gc")
+    everyone = ("gy", "gc", "member")
     in_specs = (
-        P(("group", "member"), None, None),
-        P(("group", "member"), None, None),
-        P(("group", "member"), None),
-        P(("group", "member")),
+        P(everyone, None, None),
+        P(everyone, None, None),
+        P(everyone, None),
+        P(everyone),
         P("member", None, None),
-        P("member", "group"),
-        P("member", "group"),
+        P("member", group),
+        P("member", group),
         P("member", None),
         P("member", None),
-        P(("group", "member"), None, None),
-        P(("group", "member"), None, None),
-        P(("group", "member"), None, None),
+        P(everyone, None, None),
+        P(everyone, None, None),
+        P(everyone, None, None),
     )
-    out_specs = P("member", "group")
+    out_specs = P("member", group)
     return jax.shard_map(
-        per_device, mesh=mesh, in_specs=in_specs, out_specs=out_specs, check_vma=False
+        per_device, mesh=split, in_specs=in_specs, out_specs=out_specs, check_vma=False
     )

time: 222 us -> 236 us (1.063)
  waiting for transfers between devices: 87.3 us -> 100 us
  local copies, waits for them, and re-layouts: 27.9 us -> 30.5 us
    all_gather x1 -> x2, waiting for transfers between devices: 26.9 us -> 39.5 us  [the longest x1 21.7 us: per_device(): along_y = lax.all_gather(per_head, 'gy', axis=0, tiled=True)]
  transfers between devices with their start and end apart: 4 -> 5, of which waited for: 4 -> 5; matrix products, arithmetic and copies ran while one was open for 11% -> 11% of each run, Pallas kernels for 0% -> 0%
where the time goes in v4:
time: 236 us; the launch traced here: 235 us
  waiting for transfers between devices  100 us (42%)
  local copies, waits for them, and re-layouts  30.5 us (13%)
  matrix products  28.6 us (12%)
  blocking collectives  24.3 us (10%)
  starting transfers between devices  20.7 us (9%)
  other arithmetic  17.1 us (7%)
  between operations  13.7 us (6%)
    all_to_all x1, blocking collectives, per_device(): lax.all_to_all(latent_out, 'member', split_axis=1, concat_axis=0, tiled=T...  24.3 us
    all_to_all x1, waiting for transfers between devices, per_device(): lax.all_to_all(results.reshape(experts, capacity, columns), ('gy', 'gc',...  23.7 us
    all_gather x1, waiting for transfers between devices, per_device(): along_y = lax.all_gather(per_head, 'gy', axis=0, tiled=True)  21.7 us
    all_to_all x1, waiting for transfers between devices, per_device(): lax.all_to_all(outgoing.reshape(experts, capacity, columns), ('gy', 'gc',...  19.2 us
    all_gather x1, waiting for transfers between devices, per_device(): both_cores = lax.all_gather(along_y, 'gc', axis=0, tiled=True)  17.8 us
    all_to_all x1, waiting for transfers between devices, per_device(): lax.all_to_all(partial_sums.astype(jnp.bfloat16).reshape(members, -1, col...  17.6 us
    unnamed x24, local copies, waits for them, and re-layouts  11.7 us
    dot_general x1, matrix products, per_device(): jnp.einsum('sf,fgc->gsc', inner, w_down[0].reshape(-1, groups, columns),...  10.7 us
  transfers between devices with their start and end apart: 5, of which 5 were waited for; matrix products, arithmetic and copies ran while one was open for 11% of the time, Pallas kernels for 0%

profile of v4, /device:TPU:1, one launch (start us, length us, event | category | flops | bytes accessed | tf_op | source)
XLA Modules:
  0.0 234.7 jit_solution(15841164323876635871)
XLA Ops:
  8.2 2.3 gather_fusion
  10.5 4.3 %copy.98 = bf16[16,128,576]{2,1,0:T(8,128)(2,1)} copy(bf16[16,128,576]{1,2,0:T(8,128)(2,1)} %gather_fusion) | data formatting | bytes 4718592 | tf_op jit(solution)/shard_map/jit(_take)/gather | solution.py:35
  14.9 2.2 broadcast_select_fusion
  19.0 3.6 %fusion.15 = bf16[16,64,512]{2,1,0:T(8,128)(2,1)S(1)} fusion(bf16[16,1,576]{2,1,0:T(2,128)(2,1)S(1)} %copy.99, bf16[16,128,576]{2,1,0:T(8,128)(2,1)} %copy-done.2, f32[16,64]{1,0:T(8,128)S(1)} %fusion.44, f32[16,64,129]{2,1,0:T(8,128)S(1)} %fusion.24), kind=kOutput, calls=%fused_computation.24 | convolution fusion | flops 140415104 | bytes 3958784 | tf_op jit(solution)/shard_map/rhc,rcl->rhl/dot_general | solution.py:39
  23.1 24.3 %all_to_all.33 = bf16[16,64,512]{2,0,1:T(8,128)(2,1)S(1)} all-to-all(bf16[16,64,512]{2,0,1:T(8,128)(2,1)S(1)} %copy.100), channel_id=1, replica_groups=mesh['gy'=4,'gc'=2,'member'=16] {'member'}, dimensions={1} | all-to-all | bytes 2097152 | tf_op jit(solution)/shard_map/all_to_all | solution.py:42
  48.9 21.7 %all-gather.3.cloned.1.call-done = bf16[1024,512]{1,0:T(8,128)(2,1)} async-done(((bf16[256,512]{1,0:T(8,128)(2,1)}), bf16[1024,512]{1,0:T(8,128)(2,1)}) %all-gather.3.cloned.1.call-update) | async-done | bytes 1048592 | tf_op jit(solution)/shard_map/all_gather | solution.py:47
  70.6 17.8 %all-gather.5.cloned.1.call-done = bf16[2048,512]{1,0:T(8,128)(2,1)} async-done(((bf16[1024,512]{1,0:T(8,128)(2,1)}), bf16[2048,512]{1,0:T(8,128)(2,1)}) %all-gather.5.cloned.1.call-update) | async-done | bytes 2097168 | tf_op jit(solution)/shard_map/all_gather | solution.py:48
  88.4 1.7 copy.104
  91.3 1.7 copy.124
  93.0 6.9 %all-to-all-start.1 = ((bf16[16,128,448]{1,2,0:T(8,128)(2,1)}), bf16[16,128,448]{1,2,0:T(8,128)(2,1)S(1)}, u32[]{:S(2)}, u32[]{:S(2)}) async-start(bf16[16,128,448]{1,2,0:T(8,128)(2,1)} %bitcast.70), calls=%async_computation.1 | async-start | bytes 3670016 | tf_op jit(solution)/shard_map/all_to_all | solution.py:56
  101.3 7.4 %fusion.3 = pred[2048,128]{1,0:T(8,128)(4,1)S(1)} fusion(s32[128,8]{0,1:T(8,128)S(1)} %multiply_add_fusion), kind=kLoop, calls=%fused_computation.6 | loop fusion | flops 3932160 | bytes 266240 | tf_op jit(solution)/shard_map/reduce_or | solution.py:75
  108.7 17.6 %all-to-all-done.1 = bf16[16,128,448]{1,2,0:T(8,128)(2,1)S(1)} async-done(((bf16[16,128,448]{1,2,0:T(8,128)(2,1)}), bf16[16,128,448]{1,2,0:T(8,128)(2,1)S(1)}, u32[]{:S(2)}, u32[]{:S(2)}) %all-to-all-start.1) | async-done | bytes 1835040 | tf_op jit(solution)/shard_map/all_to_all | solution.py:56
  127.3 2.5 %copy.113 = bf16[2048,448]{1,0:T(8,128)(2,1)} copy(bf16[2048,448]{0,1:T(8,128)(2,1)S(1)} %convolution_convert_fusion) | data formatting | bytes 3670016 | tf_op jit(solution)/shard_map/convert_element_type | solution.py:76
  129.8 7.9 %all-to-all-start.2 = ((bf16[128,16,448]{2,1,0:T(8,128)(2,1)}), bf16[128,16,448]{2,1,0:T(8,128)(2,1)S(1)}, u32[]{:S(2)}, u32[]{:S(2)}) async-start(bf16[128,16,448]{2,1,0:T(8,128)(2,1)} %bitcast.13), calls=%async_computation.2 | async-start | bytes 4194304 | tf_op jit(solution)/shard_map/all_to_all | solution.py:77
  137.7 10.4 %copy.116 = bf16[1,1024,3584]{1,2,0:T(8,128)(2,1)} copy(bf16[1,1024,3584]{2,1,0:T(8,128)(2,1)} %param.23) | data formatting | bytes 14680064 | tf_op args[11]
  148.1 19.2 %all-to-all-done.2 = bf16[128,16,448]{2,1,0:T(8,128)(2,1)S(1)} async-done(((bf16[128,16,448]{2,1,0:T(8,128)(2,1)}), bf16[128,16,448]{2,1,0:T(8,128)(2,1)S(1)}, u32[]{:S(2)}, u32[]{:S(2)}) %all-to-all-start.2) | async-done | bytes 1835040 | tf_op jit(solution)/shard_map/all_to_all | solution.py:77
  167.3 5.1 %convolution_bitcast_fusion.1 = f32[256,1024]{1,0:T(8,128)S(1)} fusion(bf16[8,256,448]{2,1,0:T(8,128)(2,1)S(1)} %bitcast.74, bf16[8,448,1024]{2,1,0:T(8,128)(2,1)} %bitcast.80), kind=kOutput, calls=%fused_computation.29 | convolution fusion | flops 1879048192 | bytes 10223616 | tf_op jit(solution)/shard_map/gsc,gcf->sf/dot_general | solution.py:85
  172.4 10.7 %convert_bitcast_fusion = bf16[8,256,448]{1,2,0:T(8,128)(2,1)} fusion(bf16[1024,8,448]{0,2,1:T(8,128)(2,1)} %bitcast.71, bf16[8,256,448]{2,1,0:T(8,128)(2,1)S(1)} %bitcast.75, bf16[8,448,1024]{2,1,0:T(8,128)(2,1)} %bitcast.81, f32[256,1024]{1,0:T(8,128)S(1)} %convolution_bitcast_fusion.1), kind=kOutput, calls=%fused_computation.22 | convolution fusion | flops 3760586752 | bytes 19398656 | tf_op jit(solution)/shard_map/sf,fgc->gsc/dot_general | solution.py:94
  183.1 3.8 %copy.117 = bf16[8,256,448]{2,1,0:T(8,128)(2,1)} copy(bf16[8,256,448]{1,2,0:T(8,128)(2,1)} %convert_bitcast_fusion) | data formatting | bytes 3670016 | tf_op jit(solution)/shard_map/convert_element_type | solution.py:97
  187.0 5.8 %all-to-all-start.3 = ((bf16[128,16,448]{2,1,0:T(8,128)(2,1)}), bf16[128,16,448]{2,1,0:T(8,128)(2,1)}, u32[]{:S(2)}, u32[]{:S(2)}) async-start(bf16[128,16,448]{2,1,0:T(8,128)(2,1)} %bitcast.22), calls=%async_computation.3 | async-start | bytes 4194304 | tf_op jit(solution)/shard_map/all_to_all | solution.py:98
  193.2 5.4 %fusion.5 = (bf16[128,2048]{1,0:T(8,128)(2,1)S(1)}, bf16[128,2048]{1,0:T(8,128)(2,1)S(1)}) fusion(s32[128,8]{1,0:T(8,128)S(1)} %copy.111, bf16[128,8]{1,0:T(8,128)(2,1)S(1)} %copy.118, bf16[128,8]{1,0:T(8,128)(2,1)S(1)} %copy.112), kind=kLoop, calls=%fused_computation.8 | loop fusion | flops 9961472 | bytes 1056768 | tf_op jit(solution)/shard_map/reduce_sum | solution.py:112
  198.6 23.7 %all-to-all-done.3 = bf16[128,16,448]{2,1,0:T(8,128)(2,1)} async-done(((bf16[128,16,448]{2,1,0:T(8,128)(2,1)}), bf16[128,16,448]{2,1,0:T(8,128)(2,1)}, u32[]{:S(2)}, u32[]{:S(2)}) %all-to-all-start.3) | async-done | bytes 1835040 | tf_op jit(solution)/shard_map/all_to_all | solution.py:98
  222.2 2.6 %fusion.45 = f32[128,448]{0,1:T(8,128)S(1)} fusion(bf16[128,2048]{1,0:T(8,128)(2,1)S(1)} %get-tuple-element.6, bf16[2048,448]{1,0:T(8,128)(2,1)} %bitcast.23), kind=kOutput, calls=%fused_computation.68 | convolution fusion | flops 234881024 | bytes 2588672 | tf_op jit(solution)/shard_map/dot_general | solution.py:113
  224.9 3.0 %fusion.30 = bf16[128,448]{0,1:T(8,128)(2,1)} fusion(f32[128,448]{0,1:T(8,128)S(1)} %fusion.45, bf16[128,2048]{1,0:T(8,128)(2,1)S(1)} %get-tuple-element.5, bf16[2048,448]{1,0:T(8,128)(2,1)} %bitcast.23, f32[128,448]{0,1:T(8,128)} %copy-done.3, bf16[128,448]{0,1:T(8,128)(2,1)S(1)} %copy-done.5), kind=kOutput, calls=%fused_computation.37 | convolution fusion | flops 235282432 | bytes 3047424 | tf_op jit(solution)/shard_map/dot_general | solution.py:113
  (56 shorter events, 9.4 us)
Async XLA Ops:
  6.5 1.7 copy-start
  6.5 64.1 %all-gather.3.cloned.1.call-start = ((), (), s32[]{:S(2)}) async-start(), calls=%async_computation.4 | async-start | bytes 1310720 | tf_op jit(solution)/shard_map/all_gather | solution.py:47
  10.5 4.3 %copy-start.6 = (bf16[16,576]{1,0:T(8,128)(2,1)S(1)}, bf16[16,576]{1,0:T(8,128)(2,1)}, u32[]{:S(2)}) copy-start(bf16[16,576]{1,0:T(8,128)(2,1)} %param.14) | copy-start | bytes 55300
  14.9 2.2 copy-start.9
  17.1 1.5 copy-start.2
  23.1 24.4 %copy-start.4 = (bf16[4,512,128]{2,1,0:T(8,128)(2,1)S(1)}, bf16[4,512,128]{2,1,0:T(8,128)(2,1)}, u32[]{:S(2)}) copy-start(bf16[4,512,128]{2,1,0:T(8,128)(2,1)} %param.16) | copy-start | bytes 1572868
  48.9 39.5 %all-gather.5.cloned.1.call-start = ((), (), s32[]{:S(2)}) async-start(), calls=%async_computation.5 | async-start | bytes 3145728 | tf_op jit(solution)/shard_map/all_gather | solution.py:48
  70.6 19.5 %copy-start.10 = (bf16[512,448]{0,1:T(8,128)(2,1)S(1)}, bf16[512,448]{0,1:T(8,128)(2,1)}, u32[]{:S(2)}) copy-start(bf16[512,448]{0,1:T(8,128)(2,1)} %param.17) | copy-start | bytes 1376260
  93.0 6.9 %copy-start.7 = (s32[128,8]{0,1:T(8,128)S(1)}, s32[128,8]{0,1:T(8,128)}, u32[]{:S(2)}) copy-start(s32[128,8]{0,1:T(8,128)} %param.19) | copy-start | bytes 12292
  93.0 33.3 %all-to-all-start.1 = ((bf16[16,128,448]{1,2,0:T(8,128)(2,1)}), bf16[16,128,448]{1,2,0:T(8,128)(2,1)S(1)}, u32[]{:S(2)}, u32[]{:S(2)}) async-start(bf16[16,128,448]{1,2,0:T(8,128)(2,1)} %bitcast.70), calls=%async_computation.1 | async-start | bytes 3670016 | tf_op jit(solution)/shard_map/all_to_all | solution.py:56
  100.6 26.1 %copy-start.5 = (bf16[128,448]{0,1:T(8,128)(2,1)S(1)}, bf16[128,448]{0,1:T(8,128)(2,1)}, u32[]{:S(2)}) copy-start(bf16[128,448]{0,1:T(8,128)(2,1)} %param.18) | copy-start | bytes 344068
  126.6 3.2 %copy-start.3 = (f32[128,448]{0,1:T(8,128)}, f32[128,448]{0,1:T(8,128)S(1)}, u32[]{:S(2)}) copy-start(f32[128,448]{0,1:T(8,128)S(1)} %convert_reduce_fusion) | copy-start | bytes 688132
  129.8 37.5 %all-to-all-start.2 = ((bf16[128,16,448]{2,1,0:T(8,128)(2,1)}), bf16[128,16,448]{2,1,0:T(8,128)(2,1)S(1)}, u32[]{:S(2)}, u32[]{:S(2)}) async-start(bf16[128,16,448]{2,1,0:T(8,128)(2,1)} %bitcast.13), calls=%async_computation.2 | async-start | bytes 4194304 | tf_op jit(solution)/shard_map/all_to_all | solution.py:77
  187.0 6.0 %copy-start.8 = (f32[128,8]{0,1:T(8,128)S(1)}, f32[128,8]{0,1:T(8,128)}, u32[]{:S(2)}) copy-start(f32[128,8]{0,1:T(8,128)} %param.20) | copy-start | bytes 12292
  187.0 35.3 %all-to-all-start.3 = ((bf16[128,16,448]{2,1,0:T(8,128)(2,1)}), bf16[128,16,448]{2,1,0:T(8,128)(2,1)}, u32[]{:S(2)}, u32[]{:S(2)}) async-start(bf16[128,16,448]{2,1,0:T(8,128)(2,1)} %bitcast.22), calls=%async_computation.3 | async-start | bytes 4194304 | tf_op jit(solution)/shard_map/all_to_all | solution.py:98
  222.2 5.7 %copy-start.1 = (bf16[16,128,576]{1,2,0:T(8,128)(2,1)S(1)}, bf16[16,128,576]{1,2,0:T(8,128)(2,1)}, u32[]{:S(2)}) copy-start(bf16[16,128,576]{1,2,0:T(8,128)(2,1)} %param.13) | copy-start | bytes 7077892
Sparse Core Ops, SparseCore 0:
  49.0 21.5 all-gather.2
  72.3 16.1 all-gather.4

commit v5 on v3

--- a/solution.py
+++ b/solution.py
@@ -44,19 +44,23 @@
         "rhl,hlv->rhv", by_heads, value_up, preferred_element_type=jnp.float32
     ).astype(jnp.bfloat16)
     per_head = per_head.reshape(per_head.shape[0], per_head.shape[1] * per_head.shape[2])
-    partial_sums = jnp.dot(
-        lax.all_gather(per_head, "group", axis=0, tiled=True),
-        out_proj,
-        preferred_element_type=jnp.float32,
+    weights_all = lax.all_gather(out_proj, "group", axis=1, tiled=True)
+    partial_sums = jnp.dot(per_head, weights_all, preferred_element_type=jnp.float32)
+    halves = per_head.shape[0] // residual.shape[0]
+    pieces = (
+        partial_sums.astype(jnp.bfloat16)
+        .reshape(halves, -1, groups, columns)
+        .transpose(0, 2, 1, 3)
+        .reshape(members, -1, columns)
     )
-    pieces = lax.all_to_all(
-        partial_sums.astype(jnp.bfloat16).reshape(members, -1, columns),
-        "member",
-        split_axis=0,
-        concat_axis=0,
-        tiled=True,
-    )
-    attention = jnp.sum(pieces.astype(jnp.float32), axis=0)
+    pieces = lax.all_to_all(pieces, "member", split_axis=0, concat_axis=0, tiled=True)
+    summed = jnp.sum(pieces.astype(jnp.float32), axis=0)
+    owner = [
+        (g * members + m, (m % groups) * members + (m // groups) + halves * g)
+        for g in range(groups)
+        for m in range(members)
+    ]
+    attention = lax.ppermute(summed, ("group", "member"), perm=owner)
     hidden_in = (residual.astype(jnp.float32) + attention).astype(jnp.bfloat16)
     block_rows = hidden_in.shape[0]
     capacity = max(2, 2 * rows * TOP // members)

time: 222 us -> 219 us (0.986)
  waiting for transfers between devices: 87.3 us -> 65.6 us
  starting transfers between devices: 20.2 us -> 29.8 us
  local copies, waits for them, and re-layouts: 27.9 us -> 35.5 us
    all_gather x1, waiting for transfers between devices: 26.9 us -> 0.02 us  [per_device(): weights_all = lax.all_gather(out_proj, 'group', axis=1, tiled=True)]
    ppermute x0 -> x1, starting transfers between devices: none -> 6.47 us  [per_device(): attention = lax.ppermute(summed, ('group', 'member'), perm=owner)]
    all_to_all x1, starting transfers between devices: 7.54 us -> 13.5 us  [per_device(): lax.all_to_all(outgoing.reshape(experts, capacity, columns), ('group', 'm...]
    reshape x1 -> x2, local copies, waits for them, and re-layouts: 1.73 us -> 6.83 us  [per_device(): pieces = partial_sums.astype(jnp.bfloat16).reshape(halves, -1, groups, co...]
    all_to_all x1, waiting for transfers between devices: 17.5 us -> 22 us  [per_device(): lax.all_to_all(pieces, 'member', split_axis=0, concat_axis=0, tiled=True)]
    transpose x0 -> x1, local copies, waits for them, and re-layouts: none -> 3.08 us  [per_device(): pieces = partial_sums.astype(jnp.bfloat16).reshape(halves, -1, groups, co...]
    all_to_all x1, starting transfers between devices: 6.81 us -> 3.84 us  [per_device(): lax.all_to_all(pieces, 'member', split_axis=0, concat_axis=0, tiled=True)]
    unnamed x24 -> x22, local copies, waits for them, and re-layouts: 11.7 us -> 11.1 us
  transfers between devices with their start and end apart: 4 -> 5, of which waited for: 4 -> 3; matrix products, arithmetic and copies ran while one was open for 11% -> 19% of each run, Pallas kernels for 0% -> 0%
where the time goes in v5:
time: 219 us; the launch traced here: 218 us
  waiting for transfers between devices  65.6 us (30%)
  local copies, waits for them, and re-layouts  35.5 us (16%)
  matrix products  31.9 us (15%)
  starting transfers between devices  29.8 us (14%)
  blocking collectives  24.4 us (11%)
  other arithmetic  16.9 us (8%)
  between operations  13.7 us (6%)
    all_to_all x1, blocking collectives, per_device(): lax.all_to_all(latent_out, 'member', split_axis=1, concat_axis=0, tiled=T...  24.4 us
    all_to_all x1, waiting for transfers between devices, per_device(): lax.all_to_all(results.reshape(experts, capacity, columns), ('group', 'me...  23.7 us
    all_to_all x1, waiting for transfers between devices, per_device(): lax.all_to_all(pieces, 'member', split_axis=0, concat_axis=0, tiled=True)  22 us
    all_to_all x1, waiting for transfers between devices, per_device(): lax.all_to_all(outgoing.reshape(experts, capacity, columns), ('group', 'm...  19.2 us
    all_to_all x1, starting transfers between devices, per_device(): lax.all_to_all(outgoing.reshape(experts, capacity, columns), ('group', 'm...  13.5 us
    unnamed x22, local copies, waits for them, and re-layouts  11.1 us
    dot_general x1, matrix products, per_device(): jnp.einsum('sf,fgc->gsc', inner, w_down[0].reshape(-1, groups, columns),...  10.7 us
    reduce_or x1, other arithmetic, per_device(): send_map = jnp.any(matches, axis=2).astype(jnp.bfloat16)  7.42 us
  transfers between devices with their start and end apart: 5, of which 3 were waited for; matrix products, arithmetic and copies ran while one was open for 19% of the time, Pallas kernels for 0%

profile of v5, /device:TPU:1, one launch (start us, length us, event | category | flops | bytes accessed | tf_op | source)
XLA Modules:
  0.0 217.8 jit_solution(11651172660603257934)
XLA Ops:
  8.2 2.3 %gather_fusion = bf16[16,128,576]{1,2,0:T(8,128)(2,1)} fusion(bf16[16,128,576]{1,2,0:T(8,128)(2,1)S(1)} %copy-done, s32[1024]{0:T(1024)S(1)} %pad_clamp_fusion), kind=kCustom, calls=%fused_computation | custom fusion | bytes 4718656 | tf_op jit(solution)/shard_map/jit(_take)/gather | solution.py:35
  10.5 4.4 %copy.79 = bf16[16,128,576]{2,1,0:T(8,128)(2,1)} copy(bf16[16,128,576]{1,2,0:T(8,128)(2,1)} %gather_fusion) | data formatting | bytes 4718592 | tf_op jit(solution)/shard_map/jit(_take)/gather | solution.py:35
  18.9 3.6 %fusion.14 = bf16[16,64,512]{2,1,0:T(8,128)(2,1)S(1)} fusion(bf16[16,1,576]{2,1,0:T(2,128)(2,1)S(1)} %copy.80, bf16[16,128,576]{2,1,0:T(8,128)(2,1)} %copy-done.2, f32[16,64]{1,0:T(8,128)S(1)} %fusion.41, f32[16,64,129]{2,1,0:T(8,128)S(1)} %fusion.23), kind=kOutput, calls=%fused_computation.22 | convolution fusion | flops 140415104 | bytes 3958784 | tf_op jit(solution)/shard_map/rhc,rcl->rhl/dot_general | solution.py:39
  23.1 24.4 %all_to_all.33 = bf16[16,64,512]{2,0,1:T(8,128)(2,1)S(1)} all-to-all(bf16[16,64,512]{2,0,1:T(8,128)(2,1)S(1)} %copy.81), channel_id=1, replica_groups=mesh['group'=8,'member'=16] {'member'}, dimensions={1} | all-to-all | bytes 2097152 | tf_op jit(solution)/shard_map/all_to_all | solution.py:42
  48.2 4.5 %convolution_convert_fusion = bf16[256,3584]{1,0:T(8,128)(2,1)} fusion(bf16[256,512]{0,1:T(8,128)(2,1)S(1)} %bitcast.70, bf16[512,3584]{0,1:T(8,128)(2,1)} %all-gather.2.cloned.1.call-done), kind=kOutput, calls=%fused_computation.7 | convolution fusion | flops 940441600 | bytes 5767168 | tf_op jit(solution)/shard_map/dot_general | solution.py:48
  52.6 3.9 %reshape.91 = bf16[2,128,8,448]{3,2,1,0:T(8,128)(2,1)S(1)} reshape(bf16[256,3584]{1,0:T(8,128)(2,1)} %convolution_convert_fusion) | data formatting | bytes 3670016 | tf_op jit(solution)/shard_map/reshape | solution.py:52
  56.6 2.9 %copy.102 = bf16[2,128,8,448]{1,0,3,2:T(2,128)(2,1)} copy(bf16[2,128,8,448]{3,2,1,0:T(8,128)(2,1)S(1)} %reshape.91) | data formatting | bytes 3670016 | tf_op jit(solution)/shard_map/reshape | solution.py:52
  59.5 3.1 %copy.85 = bf16[2,8,128,448]{2,3,1,0:T(8,128)(2,1)} copy(bf16[2,8,128,448]{2,0,3,1:T(2,128)(2,1)} %bitcast.65) | data formatting | bytes 3670016 | tf_op jit(solution)/shard_map/transpose | solution.py:53
  62.6 3.8 %all-to-all-start.1 = ((bf16[16,128,448]{1,2,0:T(8,128)(2,1)}), bf16[16,128,448]{1,2,0:T(8,128)(2,1)S(1)}, u32[]{:S(2)}, u32[]{:S(2)}) async-start(bf16[16,128,448]{1,2,0:T(8,128)(2,1)} %bitcast.8), calls=%async_computation.1 | async-start | bytes 3670016 | tf_op jit(solution)/shard_map/all_to_all | solution.py:56
  67.7 22.0 %all-to-all-done.1 = bf16[16,128,448]{1,2,0:T(8,128)(2,1)S(1)} async-done(((bf16[16,128,448]{1,2,0:T(8,128)(2,1)}), bf16[16,128,448]{1,2,0:T(8,128)(2,1)S(1)}, u32[]{:S(2)}, u32[]{:S(2)}) %all-to-all-start.1) | async-done | bytes 1835040 | tf_op jit(solution)/shard_map/all_to_all | solution.py:56
  89.9 6.5 %collective-permute-start = (f32[128,448]{0,1:T(8,128)S(1)}, f32[128,448]{0,1:T(8,128)S(1)}, u32[]{:S(2)}, u32[]{:S(2)}) collective-permute-start(f32[128,448]{0,1:T(8,128)S(1)} %convert_reduce_fusion), channel_id=1, source_target_pairs={{0,0},{1,16},{2,32},{3,48},{4,64},{5,80},{6,96},{7,112},{8,1},{9,1... | collective-permute-start | bytes 688136 | tf_op jit(solution)/shard_map/ppermute | solution.py:63
  96.4 7.4 %fusion.3 = pred[2048,128]{1,0:T(8,128)(4,1)S(1)} fusion(s32[128,8]{0,1:T(8,128)S(1)} %multiply_add_fusion), kind=kLoop, calls=%fused_computation.6 | loop fusion | flops 3932160 | bytes 266240 | tf_op jit(solution)/shard_map/reduce_or | solution.py:75
  104.5 2.5 %copy.93 = bf16[2048,448]{1,0:T(8,128)(2,1)} copy(bf16[2048,448]{0,1:T(8,128)(2,1)S(1)} %convolution_convert_fusion.1) | data formatting | bytes 3670016 | tf_op jit(solution)/shard_map/convert_element_type | solution.py:76
  107.0 13.5 %all-to-all-start.2 = ((bf16[128,16,448]{2,1,0:T(8,128)(2,1)}), bf16[128,16,448]{2,1,0:T(8,128)(2,1)S(1)}, u32[]{:S(2)}, u32[]{:S(2)}) async-start(bf16[128,16,448]{2,1,0:T(8,128)(2,1)} %bitcast.12), calls=%async_computation.2 | async-start | bytes 4194304 | tf_op jit(solution)/shard_map/all_to_all | solution.py:77
  120.5 10.4 %copy.96 = bf16[1,1024,3584]{1,2,0:T(8,128)(2,1)} copy(bf16[1,1024,3584]{2,1,0:T(8,128)(2,1)} %param.23) | data formatting | bytes 14680064 | tf_op args[11]
  130.9 19.2 %all-to-all-done.2 = bf16[128,16,448]{2,1,0:T(8,128)(2,1)S(1)} async-done(((bf16[128,16,448]{2,1,0:T(8,128)(2,1)}), bf16[128,16,448]{2,1,0:T(8,128)(2,1)S(1)}, u32[]{:S(2)}, u32[]{:S(2)}) %all-to-all-start.2) | async-done | bytes 1835040 | tf_op jit(solution)/shard_map/all_to_all | solution.py:77
  150.1 5.1 %convolution_bitcast_fusion.1 = f32[256,1024]{1,0:T(8,128)S(1)} fusion(bf16[8,256,448]{2,1,0:T(8,128)(2,1)S(1)} %bitcast.68, bf16[8,448,1024]{2,1,0:T(8,128)(2,1)} %bitcast.72), kind=kOutput, calls=%fused_computation.27 | convolution fusion | flops 1879048192 | bytes 10223616 | tf_op jit(solution)/shard_map/gsc,gcf->sf/dot_general | solution.py:85
  155.3 10.7 %convert_bitcast_fusion = bf16[8,256,448]{1,2,0:T(8,128)(2,1)} fusion(bf16[1024,8,448]{0,2,1:T(8,128)(2,1)} %bitcast.64, bf16[8,256,448]{2,1,0:T(8,128)(2,1)S(1)} %bitcast.69, bf16[8,448,1024]{2,1,0:T(8,128)(2,1)} %bitcast.73, f32[256,1024]{1,0:T(8,128)S(1)} %convolution_bitcast_fusion.1), kind=kOutput, calls=%fused_computation.21 | convolution fusion | flops 3760586752 | bytes 19398656 | tf_op jit(solution)/shard_map/sf,fgc->gsc/dot_general | solution.py:94
  166.0 3.8 %copy.97 = bf16[8,256,448]{2,1,0:T(8,128)(2,1)} copy(bf16[8,256,448]{1,2,0:T(8,128)(2,1)} %convert_bitcast_fusion) | data formatting | bytes 3670016 | tf_op jit(solution)/shard_map/convert_element_type | solution.py:97
  169.8 6.1 %all-to-all-start.3 = ((bf16[128,16,448]{2,1,0:T(8,128)(2,1)}), bf16[128,16,448]{2,1,0:T(8,128)(2,1)}, u32[]{:S(2)}, u32[]{:S(2)}) async-start(bf16[128,16,448]{2,1,0:T(8,128)(2,1)} %bitcast.21), calls=%async_computation.3 | async-start | bytes 4194304 | tf_op jit(solution)/shard_map/all_to_all | solution.py:98
  176.3 5.4 %fusion.5 = (bf16[128,2048]{1,0:T(8,128)(2,1)S(1)}, bf16[128,2048]{1,0:T(8,128)(2,1)S(1)}) fusion(s32[128,8]{1,0:T(8,128)S(1)} %copy.91, bf16[128,8]{1,0:T(8,128)(2,1)S(1)} %copy.98, bf16[128,8]{1,0:T(8,128)(2,1)S(1)} %copy.92), kind=kLoop, calls=%fused_computation.9 | loop fusion | flops 9961472 | bytes 1056768 | tf_op jit(solution)/shard_map/reduce_sum | solution.py:112
  181.6 23.7 %all-to-all-done.3 = bf16[128,16,448]{2,1,0:T(8,128)(2,1)} async-done(((bf16[128,16,448]{2,1,0:T(8,128)(2,1)}), bf16[128,16,448]{2,1,0:T(8,128)(2,1)}, u32[]{:S(2)}, u32[]{:S(2)}) %all-to-all-start.3) | async-done | bytes 1835040 | tf_op jit(solution)/shard_map/all_to_all | solution.py:98
  205.3 2.6 %fusion.42 = f32[128,448]{0,1:T(8,128)S(1)} fusion(bf16[128,2048]{1,0:T(8,128)(2,1)S(1)} %get-tuple-element.6, bf16[2048,448]{1,0:T(8,128)(2,1)} %bitcast.22), kind=kOutput, calls=%fused_computation.65 | convolution fusion | flops 234881024 | bytes 2588672 | tf_op jit(solution)/shard_map/dot_general | solution.py:113
  208.0 3.0 %add_convert_fusion = bf16[128,448]{0,1:T(8,128)(2,1)} fusion(f32[128,448]{0,1:T(8,128)} %copy-done.3, bf16[128,448]{0,1:T(8,128)(2,1)S(1)} %copy-done.5, f32[128,448]{0,1:T(8,128)S(1)} %fusion.42, bf16[128,2048]{1,0:T(8,128)(2,1)S(1)} %get-tuple-element.5, bf16[2048,448]{1,0:T(8,128)(2,1)} %bitcast.22), kind=kOutput, calls=%fused_computation.46 | convolution fusion | flops 235282432 | bytes 3047424 | tf_op jit(solution)/shard_map/dot_general | solution.py:113
  (53 shorter events, 9.5 us)
Async XLA Ops:
  6.5 1.7 copy-start
  6.5 41.6 %all-gather.2.cloned.1.call-start = ((), (), s32[]{:S(2)}) async-start(), calls=%async_computation.4 | async-start | bytes 4128768 | tf_op jit(solution)/shard_map/all_gather | solution.py:47
  10.5 4.4 %copy-start.6 = (bf16[16,576]{1,0:T(8,128)(2,1)S(1)}, bf16[16,576]{1,0:T(8,128)(2,1)}, u32[]{:S(2)}) copy-start(bf16[16,576]{1,0:T(8,128)(2,1)} %param.14) | copy-start | bytes 55300
  14.9 2.2 %copy-start.9 = (bf16[16,64,576]{2,1,0:T(8,128)(2,1)S(1)}, bf16[16,64,576]{2,1,0:T(8,128)(2,1)}, u32[]{:S(2)}) copy-start(bf16[16,64,576]{2,1,0:T(8,128)(2,1)} %param.12) | copy-start | bytes 3538948
  17.1 1.5 copy-start.2
  23.1 24.5 %copy-start.4 = (bf16[4,512,128]{2,1,0:T(8,128)(2,1)S(1)}, bf16[4,512,128]{2,1,0:T(8,128)(2,1)}, u32[]{:S(2)}) copy-start(bf16[4,512,128]{2,1,0:T(8,128)(2,1)} %param.16) | copy-start | bytes 1572868
  62.6 3.9 %copy-start.7 = (s32[128,8]{0,1:T(8,128)S(1)}, s32[128,8]{0,1:T(8,128)}, u32[]{:S(2)}) copy-start(s32[128,8]{0,1:T(8,128)} %param.19) | copy-start | bytes 12292
  62.6 27.1 %all-to-all-start.1 = ((bf16[16,128,448]{1,2,0:T(8,128)(2,1)}), bf16[16,128,448]{1,2,0:T(8,128)(2,1)S(1)}, u32[]{:S(2)}, u32[]{:S(2)}) async-start(bf16[16,128,448]{1,2,0:T(8,128)(2,1)} %bitcast.8), calls=%async_computation.1 | async-start | bytes 3670016 | tf_op jit(solution)/shard_map/all_to_all | solution.py:56
  67.0 36.9 %copy-start.5 = (bf16[128,448]{0,1:T(8,128)(2,1)S(1)}, bf16[128,448]{0,1:T(8,128)(2,1)}, u32[]{:S(2)}) copy-start(bf16[128,448]{0,1:T(8,128)(2,1)} %param.18) | copy-start | bytes 344068
  89.9 13.9 %collective-permute-start = (f32[128,448]{0,1:T(8,128)S(1)}, f32[128,448]{0,1:T(8,128)S(1)}, u32[]{:S(2)}, u32[]{:S(2)}) collective-permute-start(f32[128,448]{0,1:T(8,128)S(1)} %convert_reduce_fusion), channel_id=1, source_target_pairs={{0,0},{1,16},{2,32},{3,48},{4,64},{5,80},{6,96},{7,112},{8,1},{9,1... | collective-permute-start | bytes 688136 | tf_op jit(solution)/shard_map/ppermute | solution.py:63
  103.9 3.2 %copy-start.3 = (f32[128,448]{0,1:T(8,128)}, f32[128,448]{0,1:T(8,128)S(1)}, u32[]{:S(2)}) copy-start(f32[128,448]{0,1:T(8,128)S(1)} %collective-permute-done) | copy-start | bytes 688132
  107.0 43.1 %all-to-all-start.2 = ((bf16[128,16,448]{2,1,0:T(8,128)(2,1)}), bf16[128,16,448]{2,1,0:T(8,128)(2,1)S(1)}, u32[]{:S(2)}, u32[]{:S(2)}) async-start(bf16[128,16,448]{2,1,0:T(8,128)(2,1)} %bitcast.12), calls=%async_computation.2 | async-start | bytes 4194304 | tf_op jit(solution)/shard_map/all_to_all | solution.py:77
  169.8 6.2 %copy-start.8 = (f32[128,8]{0,1:T(8,128)S(1)}, f32[128,8]{0,1:T(8,128)}, u32[]{:S(2)}) copy-start(f32[128,8]{0,1:T(8,128)} %param.20) | copy-start | bytes 12292
  169.8 35.5 %all-to-all-start.3 = ((bf16[128,16,448]{2,1,0:T(8,128)(2,1)}), bf16[128,16,448]{2,1,0:T(8,128)(2,1)}, u32[]{:S(2)}, u32[]{:S(2)}) async-start(bf16[128,16,448]{2,1,0:T(8,128)(2,1)} %bitcast.21), calls=%async_computation.3 | async-start | bytes 4194304 | tf_op jit(solution)/shard_map/all_to_all | solution.py:98
  205.3 5.7 %copy-start.1 = (bf16[16,128,576]{1,2,0:T(8,128)(2,1)S(1)}, bf16[16,128,576]{1,2,0:T(8,128)(2,1)}, u32[]{:S(2)}) copy-start(bf16[16,128,576]{1,2,0:T(8,128)(2,1)} %param.13) | copy-start | bytes 7077892
Sparse Core Ops, SparseCore 0:
  9.0 33.4 all-gather.1

commit v6 on v5

--- a/solution.py
+++ b/solution.py
@@ -44,15 +44,14 @@
         "rhl,hlv->rhv", by_heads, value_up, preferred_element_type=jnp.float32
     ).astype(jnp.bfloat16)
     per_head = per_head.reshape(per_head.shape[0], per_head.shape[1] * per_head.shape[2])
-    weights_all = lax.all_gather(out_proj, "group", axis=1, tiled=True)
-    partial_sums = jnp.dot(per_head, weights_all, preferred_element_type=jnp.float32)
+    weights_all = lax.all_gather(out_proj, "group", axis=0, tiled=False)
     halves = per_head.shape[0] // residual.shape[0]
-    pieces = (
-        partial_sums.astype(jnp.bfloat16)
-        .reshape(halves, -1, groups, columns)
-        .transpose(0, 2, 1, 3)
-        .reshape(members, -1, columns)
-    )
+    pieces = jnp.einsum(
+        "irk,ckn->icrn",
+        per_head.reshape(halves, -1, per_head.shape[1]),
+        weights_all,
+        preferred_element_type=jnp.float32,
+    ).astype(jnp.bfloat16).reshape(members, -1, columns)
     pieces = lax.all_to_all(pieces, "member", split_axis=0, concat_axis=0, tiled=True)
     summed = jnp.sum(pieces.astype(jnp.float32), axis=0)
     owner = [

time: 219 us -> 209 us (0.954)
  local copies, waits for them, and re-layouts: 35.5 us -> 25.9 us
    reshape x2 -> x0, local copies, waits for them, and re-layouts: 6.83 us -> none  [per_device(): pieces = partial_sums.astype(jnp.bfloat16).reshape(halves, -1, groups, co...]
    transpose x1 -> x0, local copies, waits for them, and re-layouts: 3.08 us -> none  [per_device(): pieces = partial_sums.astype(jnp.bfloat16).reshape(halves, -1, groups, co...]
  transfers between devices with their start and end apart: 5 -> 5, of which waited for: 3 -> 3; matrix products, arithmetic and copies ran while one was open for 19% -> 20% of each run, Pallas kernels for 0% -> 0%
where the time goes in v6:
time: 209 us; the launch traced here: 208 us
  waiting for transfers between devices  65.6 us (31%)
  matrix products  31.8 us (15%)
  starting transfers between devices  29.9 us (14%)
  local copies, waits for them, and re-layouts  25.9 us (12%)
  blocking collectives  24.4 us (12%)
  other arithmetic  16.9 us (8%)
  between operations  13.7 us (7%)
    all_to_all x1, blocking collectives, per_device(): lax.all_to_all(latent_out, 'member', split_axis=1, concat_axis=0, tiled=T...  24.4 us
    all_to_all x1, waiting for transfers between devices, per_device(): lax.all_to_all(results.reshape(experts, capacity, columns), ('group', 'me...  23.7 us
    all_to_all x1, waiting for transfers between devices, per_device(): lax.all_to_all(pieces, 'member', split_axis=0, concat_axis=0, tiled=True)  22 us
    all_to_all x1, waiting for transfers between devices, per_device(): lax.all_to_all(outgoing.reshape(experts, capacity, columns), ('group', 'm...  19.2 us
    all_to_all x1, starting transfers between devices, per_device(): lax.all_to_all(outgoing.reshape(experts, capacity, columns), ('group', 'm...  13.5 us
    unnamed x22, local copies, waits for them, and re-layouts  11.1 us
    dot_general x1, matrix products, per_device(): jnp.einsum('sf,fgc->gsc', inner, w_down[0].reshape(-1, groups, columns),...  10.7 us
    reduce_or x1, other arithmetic, per_device(): send_map = jnp.any(matches, axis=2).astype(jnp.bfloat16)  7.42 us
  transfers between devices with their start and end apart: 5, of which 3 were waited for; matrix products, arithmetic and copies ran while one was open for 20% of the time, Pallas kernels for 0%

profile of v6, /device:TPU:1, one launch (start us, length us, event | category | flops | bytes accessed | tf_op | source)
XLA Modules:
  0.0 208.1 jit_solution(4532438414489333938)
XLA Ops:
  6.5 0.7 all-gather.3.cloned.1.call-update
  8.2 2.3 %gather_fusion = bf16[16,128,576]{1,2,0:T(8,128)(2,1)} fusion(bf16[16,128,576]{1,2,0:T(8,128)(2,1)S(1)} %copy-done, s32[1024]{0:T(1024)S(1)} %pad_clamp_fusion), kind=kCustom, calls=%fused_computation | custom fusion | bytes 4718656 | tf_op jit(solution)/shard_map/jit(_take)/gather | solution.py:35
  10.5 4.4 %copy.75 = bf16[16,128,576]{2,1,0:T(8,128)(2,1)} copy(bf16[16,128,576]{1,2,0:T(8,128)(2,1)} %gather_fusion) | data formatting | bytes 4718592 | tf_op jit(solution)/shard_map/jit(_take)/gather | solution.py:35
  14.9 2.2 %broadcast_select_fusion = bf16[16,128,576]{2,1,0:T(8,128)(2,1)S(1)} fusion(bf16[16,128,576]{2,1,0:T(8,128)(2,1)} %copy.75, pred[16]{0:T(512)(128)(4,1)S(1)} %get-tuple-element.7), kind=kLoop, calls=%fused_computation.18 | loop fusion | flops 1179648 | bytes 4718608 | tf_op jit(solution)/shard_map/jit(_take)/select_n | solution.py:35
  17.1 1.2 fusion.26
  18.9 3.6 %fusion.17 = bf16[16,64,512]{2,1,0:T(8,128)(2,1)S(1)} fusion(bf16[16,1,576]{2,1,0:T(2,128)(2,1)S(1)} %copy.76, bf16[16,128,576]{2,1,0:T(8,128)(2,1)} %copy-done.2, f32[16,64]{1,0:T(8,128)S(1)} %fusion.46, f32[16,64,129]{2,1,0:T(8,128)S(1)} %fusion.26), kind=kOutput, calls=%fused_computation.25 | convolution fusion | flops 140415104 | bytes 3958784 | tf_op jit(solution)/shard_map/rhc,rcl->rhl/dot_general | solution.py:39
  23.1 24.4 %all_to_all.33 = bf16[16,64,512]{2,0,1:T(8,128)(2,1)S(1)} all-to-all(bf16[16,64,512]{2,0,1:T(8,128)(2,1)S(1)} %copy.77), channel_id=1, replica_groups=mesh['group'=8,'member'=16] {'member'}, dimensions={1} | all-to-all | bytes 2097152 | tf_op jit(solution)/shard_map/all_to_all | solution.py:42
  48.4 4.4 %fusion.16 = bf16[2,128,8,448]{1,3,2,0:T(8,128)(2,1)} fusion(bf16[56,8,8,512]{3,2,1,0:T(8,128)(2,1)} %bitcast.85, bf16[2,128,512,1]{2,1,0,3:T(8,128)(2,1)S(1)} %reshape.81), kind=kOutput, calls=%fused_computation.24 | convolution fusion | flops 940441600 | bytes 5767168 | tf_op jit(solution)/shard_map/irk,ckn->icrn/dot_general | solution.py:49
  52.9 3.8 %all-to-all-start.1 = ((bf16[16,128,448]{1,2,0:T(8,128)(2,1)}), bf16[16,128,448]{1,2,0:T(8,128)(2,1)S(1)}, u32[]{:S(2)}, u32[]{:S(2)}) async-start(bf16[16,128,448]{1,2,0:T(8,128)(2,1)} %bitcast.81), calls=%async_computation.1 | async-start | bytes 3670016 | tf_op jit(solution)/shard_map/all_to_all | solution.py:55
  58.0 22.0 %all-to-all-done.1 = bf16[16,128,448]{1,2,0:T(8,128)(2,1)S(1)} async-done(((bf16[16,128,448]{1,2,0:T(8,128)(2,1)}), bf16[16,128,448]{1,2,0:T(8,128)(2,1)S(1)}, u32[]{:S(2)}, u32[]{:S(2)}) %all-to-all-start.1) | async-done | bytes 1835040 | tf_op jit(solution)/shard_map/all_to_all | solution.py:55
  80.3 6.5 %collective-permute-start = (f32[128,448]{0,1:T(8,128)S(1)}, f32[128,448]{0,1:T(8,128)S(1)}, u32[]{:S(2)}, u32[]{:S(2)}) collective-permute-start(f32[128,448]{0,1:T(8,128)S(1)} %convert_reduce_fusion), channel_id=1, source_target_pairs={{0,0},{1,16},{2,32},{3,48},{4,64},{5,80},{6,96},{7,112},{8,1},{9,1... | collective-permute-start | bytes 688136 | tf_op jit(solution)/shard_map/ppermute | solution.py:62
  86.7 7.4 %fusion.3 = pred[2048,128]{1,0:T(8,128)(4,1)S(1)} fusion(s32[128,8]{0,1:T(8,128)S(1)} %multiply_add_fusion), kind=kLoop, calls=%fused_computation.6 | loop fusion | flops 3932160 | bytes 266240 | tf_op jit(solution)/shard_map/reduce_or | solution.py:74
  94.9 2.5 %copy.88 = bf16[2048,448]{1,0:T(8,128)(2,1)} copy(bf16[2048,448]{0,1:T(8,128)(2,1)S(1)} %convolution_convert_fusion) | data formatting | bytes 3670016 | tf_op jit(solution)/shard_map/convert_element_type | solution.py:75
  97.4 13.5 %all-to-all-start.2 = ((bf16[128,16,448]{2,1,0:T(8,128)(2,1)}), bf16[128,16,448]{2,1,0:T(8,128)(2,1)S(1)}, u32[]{:S(2)}, u32[]{:S(2)}) async-start(bf16[128,16,448]{2,1,0:T(8,128)(2,1)} %bitcast.13), calls=%async_computation.2 | async-start | bytes 4194304 | tf_op jit(solution)/shard_map/all_to_all | solution.py:76
  110.8 10.4 %copy.91 = bf16[1,1024,3584]{1,2,0:T(8,128)(2,1)} copy(bf16[1,1024,3584]{2,1,0:T(8,128)(2,1)} %param.23) | data formatting | bytes 14680064 | tf_op args[11]
  121.3 19.2 %all-to-all-done.2 = bf16[128,16,448]{2,1,0:T(8,128)(2,1)S(1)} async-done(((bf16[128,16,448]{2,1,0:T(8,128)(2,1)}), bf16[128,16,448]{2,1,0:T(8,128)(2,1)S(1)}, u32[]{:S(2)}, u32[]{:S(2)}) %all-to-all-start.2) | async-done | bytes 1835040 | tf_op jit(solution)/shard_map/all_to_all | solution.py:76
  140.5 5.1 %convolution_bitcast_fusion.1 = f32[256,1024]{1,0:T(8,128)S(1)} fusion(bf16[8,256,448]{2,1,0:T(8,128)(2,1)S(1)} %bitcast.79, bf16[8,448,1024]{2,1,0:T(8,128)(2,1)} %bitcast.83), kind=kOutput, calls=%fused_computation.30 | convolution fusion | flops 1879048192 | bytes 10223616 | tf_op jit(solution)/shard_map/gsc,gcf->sf/dot_general | solution.py:84
  145.6 10.7 %convert_bitcast_fusion = bf16[8,256,448]{1,2,0:T(8,128)(2,1)} fusion(bf16[1024,8,448]{0,2,1:T(8,128)(2,1)} %bitcast.76, bf16[8,256,448]{2,1,0:T(8,128)(2,1)S(1)} %bitcast.80, bf16[8,448,1024]{2,1,0:T(8,128)(2,1)} %bitcast.84, f32[256,1024]{1,0:T(8,128)S(1)} %convolution_bitcast_fusion.1), kind=kOutput, calls=%fused_computation.23 | convolution fusion | flops 3760586752 | bytes 19398656 | tf_op jit(solution)/shard_map/sf,fgc->gsc/dot_general | solution.py:93
  156.3 3.8 %copy.92 = bf16[8,256,448]{2,1,0:T(8,128)(2,1)} copy(bf16[8,256,448]{1,2,0:T(8,128)(2,1)} %convert_bitcast_fusion) | data formatting | bytes 3670016 | tf_op jit(solution)/shard_map/convert_element_type | solution.py:96
  160.1 6.1 %all-to-all-start.3 = ((bf16[128,16,448]{2,1,0:T(8,128)(2,1)}), bf16[128,16,448]{2,1,0:T(8,128)(2,1)}, u32[]{:S(2)}, u32[]{:S(2)}) async-start(bf16[128,16,448]{2,1,0:T(8,128)(2,1)} %bitcast.22), calls=%async_computation.3 | async-start | bytes 4194304 | tf_op jit(solution)/shard_map/all_to_all | solution.py:97
  166.6 5.4 %fusion.5 = (bf16[128,2048]{1,0:T(8,128)(2,1)S(1)}, bf16[128,2048]{1,0:T(8,128)(2,1)S(1)}) fusion(s32[128,8]{1,0:T(8,128)S(1)} %copy.86, bf16[128,8]{1,0:T(8,128)(2,1)S(1)} %copy.93, bf16[128,8]{1,0:T(8,128)(2,1)S(1)} %copy.87), kind=kLoop, calls=%fused_computation.8 | loop fusion | flops 9961472 | bytes 1056768 | tf_op jit(solution)/shard_map/reduce_sum | solution.py:111
  172.0 23.7 %all-to-all-done.3 = bf16[128,16,448]{2,1,0:T(8,128)(2,1)} async-done(((bf16[128,16,448]{2,1,0:T(8,128)(2,1)}), bf16[128,16,448]{2,1,0:T(8,128)(2,1)}, u32[]{:S(2)}, u32[]{:S(2)}) %all-to-all-start.3) | async-done | bytes 1835040 | tf_op jit(solution)/shard_map/all_to_all | solution.py:97
  195.6 2.6 %fusion.47 = f32[128,448]{0,1:T(8,128)S(1)} fusion(bf16[128,2048]{1,0:T(8,128)(2,1)S(1)} %get-tuple-element.6, bf16[2048,448]{1,0:T(8,128)(2,1)} %bitcast.23), kind=kOutput, calls=%fused_computation.70 | convolution fusion | flops 234881024 | bytes 2588672 | tf_op jit(solution)/shard_map/dot_general | solution.py:112
  198.3 3.0 %add_convert_fusion = bf16[128,448]{0,1:T(8,128)(2,1)} fusion(f32[128,448]{0,1:T(8,128)} %copy-done.3, bf16[128,448]{0,1:T(8,128)(2,1)S(1)} %copy-done.5, f32[128,448]{0,1:T(8,128)S(1)} %fusion.47, bf16[128,2048]{1,0:T(8,128)(2,1)S(1)} %get-tuple-element.5, bf16[2048,448]{1,0:T(8,128)(2,1)} %bitcast.23), kind=kOutput, calls=%fused_computation.51 | convolution fusion | flops 235282432 | bytes 3047424 | tf_op jit(solution)/shard_map/dot_general | solution.py:112
  (52 shorter events, 5.6 us)
Async XLA Ops:
  6.5 1.7 copy-start
  6.5 41.9 %all-gather.3.cloned.1.call-start = ((), (), s32[]{:S(2)}) async-start(), calls=%async_computation.4 | async-start | bytes 4128768 | tf_op jit(solution)/shard_map/all_gather | solution.py:47
  10.5 4.4 %copy-start.6 = (bf16[16,576]{1,0:T(8,128)(2,1)S(1)}, bf16[16,576]{1,0:T(8,128)(2,1)}, u32[]{:S(2)}) copy-start(bf16[16,576]{1,0:T(8,128)(2,1)} %param.14) | copy-start | bytes 55300
  14.9 2.2 %copy-start.9 = (bf16[16,64,576]{2,1,0:T(8,128)(2,1)S(1)}, bf16[16,64,576]{2,1,0:T(8,128)(2,1)}, u32[]{:S(2)}) copy-start(bf16[16,64,576]{2,1,0:T(8,128)(2,1)} %param.12) | copy-start | bytes 3538948
  17.1 1.5 copy-start.2
  23.1 24.5 %copy-start.4 = (bf16[4,512,128]{2,1,0:T(8,128)(2,1)S(1)}, bf16[4,512,128]{2,1,0:T(8,128)(2,1)}, u32[]{:S(2)}) copy-start(bf16[4,512,128]{2,1,0:T(8,128)(2,1)} %param.16) | copy-start | bytes 1572868
  52.9 3.9 %copy-start.7 = (s32[128,8]{0,1:T(8,128)S(1)}, s32[128,8]{0,1:T(8,128)}, u32[]{:S(2)}) copy-start(s32[128,8]{0,1:T(8,128)} %param.19) | copy-start | bytes 12292
  52.9 27.1 %all-to-all-start.1 = ((bf16[16,128,448]{1,2,0:T(8,128)(2,1)}), bf16[16,128,448]{1,2,0:T(8,128)(2,1)S(1)}, u32[]{:S(2)}, u32[]{:S(2)}) async-start(bf16[16,128,448]{1,2,0:T(8,128)(2,1)} %bitcast.81), calls=%async_computation.1 | async-start | bytes 3670016 | tf_op jit(solution)/shard_map/all_to_all | solution.py:55
  57.3 36.9 %copy-start.5 = (bf16[128,448]{0,1:T(8,128)(2,1)S(1)}, bf16[128,448]{0,1:T(8,128)(2,1)}, u32[]{:S(2)}) copy-start(bf16[128,448]{0,1:T(8,128)(2,1)} %param.18) | copy-start | bytes 344068
  80.3 13.9 %collective-permute-start = (f32[128,448]{0,1:T(8,128)S(1)}, f32[128,448]{0,1:T(8,128)S(1)}, u32[]{:S(2)}, u32[]{:S(2)}) collective-permute-start(f32[128,448]{0,1:T(8,128)S(1)} %convert_reduce_fusion), channel_id=1, source_target_pairs={{0,0},{1,16},{2,32},{3,48},{4,64},{5,80},{6,96},{7,112},{8,1},{9,1... | collective-permute-start | bytes 688136 | tf_op jit(solution)/shard_map/ppermute | solution.py:62
  94.2 3.2 %copy-start.3 = (f32[128,448]{0,1:T(8,128)}, f32[128,448]{0,1:T(8,128)S(1)}, u32[]{:S(2)}) copy-start(f32[128,448]{0,1:T(8,128)S(1)} %collective-permute-done) | copy-start | bytes 688132
  97.4 43.1 %all-to-all-start.2 = ((bf16[128,16,448]{2,1,0:T(8,128)(2,1)}), bf16[128,16,448]{2,1,0:T(8,128)(2,1)S(1)}, u32[]{:S(2)}, u32[]{:S(2)}) async-start(bf16[128,16,448]{2,1,0:T(8,128)(2,1)} %bitcast.13), calls=%async_computation.2 | async-start | bytes 4194304 | tf_op jit(solution)/shard_map/all_to_all | solution.py:76
  160.1 6.2 %copy-start.8 = (f32[128,8]{0,1:T(8,128)S(1)}, f32[128,8]{0,1:T(8,128)}, u32[]{:S(2)}) copy-start(f32[128,8]{0,1:T(8,128)} %param.20) | copy-start | bytes 12292
  160.1 35.5 %all-to-all-start.3 = ((bf16[128,16,448]{2,1,0:T(8,128)(2,1)}), bf16[128,16,448]{2,1,0:T(8,128)(2,1)}, u32[]{:S(2)}, u32[]{:S(2)}) async-start(bf16[128,16,448]{2,1,0:T(8,128)(2,1)} %bitcast.22), calls=%async_computation.3 | async-start | bytes 4194304 | tf_op jit(solution)/shard_map/all_to_all | solution.py:97
  195.6 5.7 %copy-start.1 = (bf16[16,128,576]{1,2,0:T(8,128)(2,1)S(1)}, bf16[16,128,576]{1,2,0:T(8,128)(2,1)}, u32[]{:S(2)}) copy-start(bf16[16,128,576]{1,2,0:T(8,128)(2,1)} %param.13) | copy-start | bytes 7077892
Sparse Core Ops, SparseCore 0:
  9.0 33.4 all-gather.2

commit v7 on v6

--- a/solution.py
+++ b/solution.py
@@ -30,15 +30,27 @@
     experts = groups * members
     columns = out_proj.shape[1]
     scale = (VHEAD + ROPE) ** (-0.5)
-    local_rows = jnp.arange(rows, dtype=jnp.int32)
-    parent = local_rows // BEAM * BEAM + parent_beam
-    keys = jnp.concatenate([jnp.take(latent_cache, parent, axis=0), new_key[:, None, :]], axis=1)
-    scores = jnp.einsum("rhw,rcw->rhc", queries, keys, preferred_element_type=jnp.float32) * scale
-    shifted = jnp.exp(scores - jnp.max(scores, axis=-1, keepdims=True))
-    weights = (shifted / jnp.sum(shifted, axis=-1, keepdims=True)).astype(jnp.bfloat16)
-    latent_out = jnp.einsum(
-        "rhc,rcl->rhl", weights, keys[:, :, :latent], preferred_element_type=jnp.float32
-    ).astype(jnp.bfloat16)
+    context = latent_cache.shape[1]
+    width = latent_cache.shape[2]
+    beams = latent_cache.reshape(rows // BEAM, BEAM, context, width)
+    chosen = parent_beam.reshape(rows // BEAM, BEAM, 1, 1)
+    held = jnp.broadcast_to(beams[:, BEAM - 1 : BEAM], beams.shape)
+    for beam in range(BEAM - 2, -1, -1):
+        held = jnp.where(chosen == beam, beams[:, beam : beam + 1], held)
+    held = held.reshape(rows, context, width)
+    scores = jnp.einsum("rhw,rcw->rhc", queries, held, preferred_element_type=jnp.float32) * scale
+    own = jnp.einsum("rhw,rw->rh", queries, new_key, preferred_element_type=jnp.float32) * scale
+    top = jnp.maximum(jnp.max(scores, axis=-1), own)
+    shifted = jnp.exp(scores - top[:, :, None])
+    own_shifted = jnp.exp(own - top)
+    total = jnp.sum(shifted, axis=-1) + own_shifted
+    weights = (shifted / total[:, :, None]).astype(jnp.bfloat16)
+    own_weight = (own_shifted / total).astype(jnp.bfloat16)
+    mixed_cache = jnp.einsum(
+        "rhc,rcl->rhl", weights, held[:, :, :latent], preferred_element_type=jnp.float32
+    )
+    mixed_new = own_weight.astype(jnp.float32)[:, :, None] * new_key[:, None, :latent].astype(jnp.float32)
+    latent_out = (mixed_cache + mixed_new).astype(jnp.bfloat16)
     by_heads = lax.all_to_all(latent_out, "member", split_axis=1, concat_axis=0, tiled=True)
     per_head = jnp.einsum(
         "rhl,hlv->rhv", by_heads, value_up, preferred_element_type=jnp.float32

time: 209 us -> 205 us (0.981)
  matrix products: 31.8 us -> 29.7 us
    broadcast_in_dim x1 -> x5, local copies, waits for them, and re-layouts: 0.03 us -> 6.89 us  [the longest x4 4.75 us: per_device(): held = jnp.where(chosen == beam, beams[:, beam:beam + 1], held)]
    gather x2 -> x0, local copies, waits for them, and re-layouts: 6.62 us -> none  [per_device(): jnp.take(latent_cache, parent, axis=0)]
    dot_general x2 -> x3, matrix products: 4.82 us -> 2.57 us  [the longest x1 1.27 us: per_device(): jnp.einsum('rhw,rcw->rhc', queries, held, preferred_element_type=jnp.floa...]
  transfers between devices with their start and end apart: 5 -> 5, of which waited for: 3 -> 3; matrix products, arithmetic and copies ran while one was open for 20% -> 19% of each run, Pallas kernels for 0% -> 0%
where the time goes in v7:
time: 205 us; the launch traced here: 204 us
  waiting for transfers between devices  64.9 us (32%)
  matrix products  29.7 us (14%)
  starting transfers between devices  29 us (14%)
  local copies, waits for them, and re-layouts  25.6 us (12%)
  blocking collectives  24.3 us (12%)
  other arithmetic  16.7 us (8%)
  between operations  13.7 us (7%)
    all_to_all x1, blocking collectives, per_device(): lax.all_to_all(latent_out, 'member', split_axis=1, concat_axis=0, tiled=T...  24.3 us
    all_to_all x1, waiting for transfers between devices, per_device(): lax.all_to_all(results.reshape(experts, capacity, columns), ('group', 'me...  23.1 us
    all_to_all x1, waiting for transfers between devices, per_device(): lax.all_to_all(pieces, 'member', split_axis=0, concat_axis=0, tiled=True)  21.9 us
    all_to_all x1, waiting for transfers between devices, per_device(): lax.all_to_all(outgoing.reshape(experts, capacity, columns), ('group', 'm...  19.2 us
    all_to_all x1, starting transfers between devices, per_device(): lax.all_to_all(outgoing.reshape(experts, capacity, columns), ('group', 'm...  12.8 us
    dot_general x1, matrix products, per_device(): jnp.einsum('sf,fgc->gsc', inner, w_down[0].reshape(-1, groups, columns),...  11 us
    unnamed x22, local copies, waits for them, and re-layouts  10.6 us
    reduce_or x1, other arithmetic, per_device(): send_map = jnp.any(matches, axis=2).astype(jnp.bfloat16)  7.42 us
  transfers between devices with their start and end apart: 5, of which 3 were waited for; matrix products, arithmetic and copies ran while one was open for 19% of the time, Pallas kernels for 0%

profile of v7, /device:TPU:1, one launch (start us, length us, event | category | flops | bytes accessed | tf_op | source)
XLA Modules:
  0.0 204.0 jit_solution(9997611946800001956)
XLA Ops:
  7.3 2.8 %slice_bitcast_fusion.3 = (bf16[4,128,576]{1,2,0:T(8,128)(2,1)S(1)}, bf16[4,128,576]{1,2,0:T(8,128)(2,1)}, bf16[4,128,576]{1,2,0:T(8,128)(2,1)}, bf16[4,128,576]{1,2,0:T(8,128)(2,1)S(1)}) fusion(bf16[4,4,128,576]{2,3,1,0:T(8,128)(2,1)} %bitcast.105), kind=kLoop, calls=%fused_computation.33 | loop fusion | bytes 4718592 | tf_op jit(solution)/shard_map/jit(_where)/broadcast_in_dim | solution.py:39
  10.7 1.4 copy.91
  12.0 2.1 %copy.92 = bf16[4,128,576]{2,1,0:T(8,128)(2,1)} copy(bf16[4,128,576]{1,2,0:T(8,128)(2,1)} %get-tuple-element.10) | data formatting | bytes 1179648 | tf_op jit(solution)/shard_map/broadcast_in_dim | solution.py:37
  14.2 1.7 fusion.8
  16.4 1.3 fusion.34
  18.1 0.8 add_convert_fusion
  19.5 24.3 %all_to_all.33 = bf16[16,64,512]{2,0,1:T(8,128)(2,1)S(1)} all-to-all(bf16[16,64,512]{2,0,1:T(8,128)(2,1)S(1)} %copy.94), channel_id=1, replica_groups=mesh['group'=8,'member'=16] {'member'}, dimensions={1} | all-to-all | bytes 2097152 | tf_op jit(solution)/shard_map/all_to_all | solution.py:54
  44.7 4.4 %fusion.11 = bf16[2,128,8,448]{1,3,2,0:T(8,128)(2,1)} fusion(bf16[56,8,8,512]{3,2,1,0:T(8,128)(2,1)} %bitcast.114, bf16[2,128,512,1]{2,1,0,3:T(8,128)(2,1)S(1)} %reshape.106), kind=kOutput, calls=%fused_computation.19 | convolution fusion | flops 940441600 | bytes 5767168 | tf_op jit(solution)/shard_map/irk,ckn->icrn/dot_general | solution.py:61
  49.2 4.6 %all-to-all-start.1 = ((bf16[16,128,448]{1,2,0:T(8,128)(2,1)}), bf16[16,128,448]{1,2,0:T(8,128)(2,1)S(1)}, u32[]{:S(2)}, u32[]{:S(2)}) async-start(bf16[16,128,448]{1,2,0:T(8,128)(2,1)} %bitcast.108), calls=%async_computation.1 | async-start | bytes 3670016 | tf_op jit(solution)/shard_map/all_to_all | solution.py:67
  55.1 21.9 %all-to-all-done.1 = bf16[16,128,448]{1,2,0:T(8,128)(2,1)S(1)} async-done(((bf16[16,128,448]{1,2,0:T(8,128)(2,1)}), bf16[16,128,448]{1,2,0:T(8,128)(2,1)S(1)}, u32[]{:S(2)}, u32[]{:S(2)}) %all-to-all-start.1) | async-done | bytes 1835040 | tf_op jit(solution)/shard_map/all_to_all | solution.py:67
  77.2 6.6 %collective-permute-start = (f32[128,448]{0,1:T(8,128)S(1)}, f32[128,448]{0,1:T(8,128)S(1)}, u32[]{:S(2)}, u32[]{:S(2)}) collective-permute-start(f32[128,448]{0,1:T(8,128)S(1)} %convert_reduce_fusion), channel_id=1, source_target_pairs={{0,0},{1,16},{2,32},{3,48},{4,64},{5,80},{6,96},{7,112},{8,1},{9,1... | collective-permute-start | bytes 688136 | tf_op jit(solution)/shard_map/ppermute | solution.py:74
  83.9 7.4 %fusion.2 = pred[2048,128]{1,0:T(8,128)(4,1)S(1)} fusion(s32[128,8]{0,1:T(8,128)S(1)} %multiply_add_fusion), kind=kLoop, calls=%fused_computation.4 | loop fusion | flops 3932160 | bytes 266240 | tf_op jit(solution)/shard_map/reduce_or | solution.py:86
  92.0 2.5 %copy.105 = bf16[2048,448]{1,0:T(8,128)(2,1)} copy(bf16[2048,448]{0,1:T(8,128)(2,1)S(1)} %convolution_convert_fusion) | data formatting | bytes 3670016 | tf_op jit(solution)/shard_map/convert_element_type | solution.py:87
  94.5 12.8 %all-to-all-start.2 = ((bf16[128,16,448]{2,1,0:T(8,128)(2,1)}), bf16[128,16,448]{2,1,0:T(8,128)(2,1)S(1)}, u32[]{:S(2)}, u32[]{:S(2)}) async-start(bf16[128,16,448]{2,1,0:T(8,128)(2,1)} %bitcast.24), calls=%async_computation.2 | async-start | bytes 4194304 | tf_op jit(solution)/shard_map/all_to_all | solution.py:88
  107.3 10.4 %copy.108 = bf16[1,1024,3584]{1,2,0:T(8,128)(2,1)} copy(bf16[1,1024,3584]{2,1,0:T(8,128)(2,1)} %param.23) | data formatting | bytes 14680064 | tf_op args[11]
  117.7 19.2 %all-to-all-done.2 = bf16[128,16,448]{2,1,0:T(8,128)(2,1)S(1)} async-done(((bf16[128,16,448]{2,1,0:T(8,128)(2,1)}), bf16[128,16,448]{2,1,0:T(8,128)(2,1)S(1)}, u32[]{:S(2)}, u32[]{:S(2)}) %all-to-all-start.2) | async-done | bytes 1835040 | tf_op jit(solution)/shard_map/all_to_all | solution.py:88
  136.9 6.1 %convolution_bitcast_fusion.1 = f32[256,1024]{1,0:T(8,128)} fusion(bf16[8,256,448]{2,1,0:T(8,128)(2,1)S(1)} %bitcast.106, bf16[8,448,1024]{2,1,0:T(8,128)(2,1)} %bitcast.112), kind=kOutput, calls=%fused_computation.22 | convolution fusion | flops 1879048192 | bytes 10223616 | tf_op jit(solution)/shard_map/gsc,gcf->sf/dot_general | solution.py:96
  143.0 11.0 %convert_bitcast_fusion = bf16[8,256,448]{1,2,0:T(8,128)(2,1)} fusion(bf16[1024,8,448]{0,2,1:T(8,128)(2,1)} %bitcast.102, bf16[8,256,448]{2,1,0:T(8,128)(2,1)S(1)} %bitcast.107, bf16[8,448,1024]{2,1,0:T(8,128)(2,1)} %bitcast.113, f32[256,1024]{1,0:T(8,128)} %convolution_bitcast_fusion.1), kind=kOutput, calls=%fused_computation.18 | convolution fusion | flops 3760586752 | bytes 19398656 | tf_op jit(solution)/shard_map/sf,fgc->gsc/dot_general | solution.py:105
  154.0 3.8 %copy.109 = bf16[8,256,448]{2,1,0:T(8,128)(2,1)} copy(bf16[8,256,448]{1,2,0:T(8,128)(2,1)} %convert_bitcast_fusion) | data formatting | bytes 3670016 | tf_op jit(solution)/shard_map/convert_element_type | solution.py:108
  157.9 5.0 %all-to-all-start.3 = ((bf16[128,16,448]{2,1,0:T(8,128)(2,1)}), bf16[128,16,448]{2,1,0:T(8,128)(2,1)S(1)}, u32[]{:S(2)}, u32[]{:S(2)}) async-start(bf16[128,16,448]{2,1,0:T(8,128)(2,1)} %bitcast.101), calls=%async_computation.3 | async-start | bytes 4194304 | tf_op jit(solution)/shard_map/all_to_all | solution.py:109
  163.3 6.3 %fusion.4 = (bf16[128,2048]{1,0:T(8,128)(2,1)}, bf16[128,2048]{1,0:T(8,128)(2,1)}) fusion(s32[128,8]{1,0:T(8,128)S(1)} %copy.103, bf16[128,8]{1,0:T(8,128)(2,1)S(1)} %copy.110, bf16[128,8]{1,0:T(8,128)(2,1)S(1)} %copy.104), kind=kLoop, calls=%fused_computation.6 | loop fusion | flops 9961472 | bytes 1056768 | tf_op jit(solution)/shard_map/reduce_sum | solution.py:123
  169.6 23.1 %all-to-all-done.3 = bf16[128,16,448]{2,1,0:T(8,128)(2,1)S(1)} async-done(((bf16[128,16,448]{2,1,0:T(8,128)(2,1)}), bf16[128,16,448]{2,1,0:T(8,128)(2,1)S(1)}, u32[]{:S(2)}, u32[]{:S(2)}) %all-to-all-start.3) | async-done | bytes 1835040 | tf_op jit(solution)/shard_map/all_to_all | solution.py:109
  192.7 2.1 %fusion.35 = f32[128,448]{0,1:T(8,128)S(1)} fusion(bf16[128,2048]{1,0:T(8,128)(2,1)} %get-tuple-element.6, bf16[2048,448]{1,0:T(8,128)(2,1)S(1)} %bitcast.99), kind=kOutput, calls=%fused_computation.68 | convolution fusion | flops 234881024 | bytes 2588672 | tf_op jit(solution)/shard_map/dot_general | solution.py:124
  194.7 2.4 %add_convert_fusion.1 = bf16[128,448]{0,1:T(8,128)(2,1)} fusion(f32[128,448]{0,1:T(8,128)} %copy-done.3, bf16[128,448]{0,1:T(8,128)(2,1)S(1)} %copy-done.5, f32[128,448]{0,1:T(8,128)S(1)} %fusion.35, bf16[128,2048]{1,0:T(8,128)(2,1)S(1)} %copy-done.2, bf16[2048,448]{1,0:T(8,128)(2,1)S(1)} %bitcast.100), kind=kOutput, calls=%fused_computation.50 | convolution fusion | flops 235282432 | bytes 3047424 | tf_op jit(solution)/shard_map/dot_general | solution.py:124
  (57 shorter events, 6.2 us)
Async XLA Ops:
  6.5 9.4 %copy-start = (bf16[16,64,576]{2,1,0:T(8,128)(2,1)S(1)}, bf16[16,64,576]{2,1,0:T(8,128)(2,1)}, u32[]{:S(2)}) copy-start(bf16[16,64,576]{2,1,0:T(8,128)(2,1)} %param.12) | copy-start | bytes 3538948
  6.5 38.2 %all-gather.3.cloned.1.call-start = ((), (), s32[]{:S(2)}) async-start(), calls=%async_computation.4 | async-start | bytes 4128768 | tf_op jit(solution)/shard_map/all_gather | solution.py:59
  10.0 4.1 %copy-start.9 = (s32[16]{0:T(128)S(1)}, s32[16]{0:T(128)}, u32[]{:S(2)}) copy-start(s32[16]{0:T(128)} %param.15) | copy-start | bytes 196
  14.2 1.7 copy-start.7
  19.5 24.4 %copy-start.4 = (bf16[4,512,128]{2,1,0:T(8,128)(2,1)S(1)}, bf16[4,512,128]{2,1,0:T(8,128)(2,1)}, u32[]{:S(2)}) copy-start(bf16[4,512,128]{2,1,0:T(8,128)(2,1)} %param.16) | copy-start | bytes 1572868
  49.2 4.6 %copy-start.6 = (s32[128,8]{0,1:T(8,128)S(1)}, s32[128,8]{0,1:T(8,128)}, u32[]{:S(2)}) copy-start(s32[128,8]{0,1:T(8,128)} %param.19) | copy-start | bytes 12292
  49.2 27.8 %all-to-all-start.1 = ((bf16[16,128,448]{1,2,0:T(8,128)(2,1)}), bf16[16,128,448]{1,2,0:T(8,128)(2,1)S(1)}, u32[]{:S(2)}, u32[]{:S(2)}) async-start(bf16[16,128,448]{1,2,0:T(8,128)(2,1)} %bitcast.108), calls=%async_computation.1 | async-start | bytes 3670016 | tf_op jit(solution)/shard_map/all_to_all | solution.py:67
  54.4 36.9 %copy-start.5 = (bf16[128,448]{0,1:T(8,128)(2,1)S(1)}, bf16[128,448]{0,1:T(8,128)(2,1)}, u32[]{:S(2)}) copy-start(bf16[128,448]{0,1:T(8,128)(2,1)} %param.18) | copy-start | bytes 344068
  77.2 14.1 %collective-permute-start = (f32[128,448]{0,1:T(8,128)S(1)}, f32[128,448]{0,1:T(8,128)S(1)}, u32[]{:S(2)}, u32[]{:S(2)}) collective-permute-start(f32[128,448]{0,1:T(8,128)S(1)} %convert_reduce_fusion), channel_id=1, source_target_pairs={{0,0},{1,16},{2,32},{3,48},{4,64},{5,80},{6,96},{7,112},{8,1},{9,1... | collective-permute-start | bytes 688136 | tf_op jit(solution)/shard_map/ppermute | solution.py:74
  91.3 3.2 %copy-start.3 = (f32[128,448]{0,1:T(8,128)}, f32[128,448]{0,1:T(8,128)S(1)}, u32[]{:S(2)}) copy-start(f32[128,448]{0,1:T(8,128)S(1)} %collective-permute-done) | copy-start | bytes 688132
  94.5 42.4 %all-to-all-start.2 = ((bf16[128,16,448]{2,1,0:T(8,128)(2,1)}), bf16[128,16,448]{2,1,0:T(8,128)(2,1)S(1)}, u32[]{:S(2)}, u32[]{:S(2)}) async-start(bf16[128,16,448]{2,1,0:T(8,128)(2,1)} %bitcast.24), calls=%async_computation.2 | async-start | bytes 4194304 | tf_op jit(solution)/shard_map/all_to_all | solution.py:88
  157.9 5.1 %copy-start.8 = (f32[128,8]{0,1:T(8,128)S(1)}, f32[128,8]{0,1:T(8,128)}, u32[]{:S(2)}) copy-start(f32[128,8]{0,1:T(8,128)} %param.20) | copy-start | bytes 12292
  157.9 34.8 %all-to-all-start.3 = ((bf16[128,16,448]{2,1,0:T(8,128)(2,1)}), bf16[128,16,448]{2,1,0:T(8,128)(2,1)S(1)}, u32[]{:S(2)}, u32[]{:S(2)}) async-start(bf16[128,16,448]{2,1,0:T(8,128)(2,1)} %bitcast.101), calls=%async_computation.3 | async-start | bytes 4194304 | tf_op jit(solution)/shard_map/all_to_all | solution.py:109
  192.7 2.1 %copy-start.2 = (bf16[128,2048]{1,0:T(8,128)(2,1)S(1)}, bf16[128,2048]{1,0:T(8,128)(2,1)}, u32[]{:S(2)}) copy-start(bf16[128,2048]{1,0:T(8,128)(2,1)} %get-tuple-element.5) | copy-start | bytes 1572868
  192.7 4.5 %copy-start.1 = (bf16[16,64,576]{2,1,0:T(8,128)(2,1)S(1)}, bf16[16,64,576]{2,1,0:T(8,128)(2,1)}, u32[]{:S(2)}) copy-start(bf16[16,64,576]{2,1,0:T(8,128)(2,1)} %param.12) | copy-start | bytes 3538948
Sparse Core Ops, SparseCore 0:
  9.0 33.4 all-gather.2

commit v8 on v7

--- a/solution.py
+++ b/solution.py
@@ -65,15 +65,7 @@
         preferred_element_type=jnp.float32,
     ).astype(jnp.bfloat16).reshape(members, -1, columns)
     pieces = lax.all_to_all(pieces, "member", split_axis=0, concat_axis=0, tiled=True)
-    summed = jnp.sum(pieces.astype(jnp.float32), axis=0)
-    owner = [
-        (g * members + m, (m % groups) * members + (m // groups) + halves * g)
-        for g in range(groups)
-        for m in range(members)
-    ]
-    attention = lax.ppermute(summed, ("group", "member"), perm=owner)
-    hidden_in = (residual.astype(jnp.float32) + attention).astype(jnp.bfloat16)
-    block_rows = hidden_in.shape[0]
+    block_rows = residual.shape[0]
     capacity = max(2, 2 * rows * TOP // members)
     flat_ids = expert_ids.reshape(-1)
     onehot = (flat_ids[:, None] == jnp.arange(experts, dtype=jnp.int32)[None, :]).astype(jnp.int32)
@@ -84,6 +76,15 @@
         experts * capacity, block_rows, TOP
     )
     send_map = jnp.any(matches, axis=2).astype(jnp.bfloat16)
+    pieces, send_map, slot_index = lax.optimization_barrier((pieces, send_map, slot_index))
+    summed = jnp.sum(pieces.astype(jnp.float32), axis=0)
+    owner = [
+        (g * members + m, (m % groups) * members + (m // groups) + halves * g)
+        for g in range(groups)
+        for m in range(members)
+    ]
+    attention = lax.ppermute(summed, ("group", "member"), perm=owner)
+    hidden_in = (residual.astype(jnp.float32) + attention).astype(jnp.bfloat16)
     outgoing = jnp.dot(send_map, hidden_in, preferred_element_type=jnp.float32).astype(jnp.bfloat16)
     arrived = lax.all_to_all(
         outgoing.reshape(experts, capacity, columns),

time: 205 us -> 205 us (level)
    all_to_all x1, waiting for transfers between devices: 21.9 us -> 14.3 us  [per_device(): lax.all_to_all(pieces, 'member', split_axis=0, concat_axis=0, tiled=True)]
    ppermute x1, waiting for transfers between devices: 0.01 us -> 6.07 us  [per_device(): attention = lax.ppermute(summed, ('group', 'member'), perm=owner)]
  transfers between devices with their start and end apart: 5 -> 5, of which waited for: 3 -> 4; matrix products, arithmetic and copies ran while one was open for 19% -> 19% of each run, Pallas kernels for 0% -> 0%
where the time goes in v8:
time: 205 us; the launch traced here: 204 us
  waiting for transfers between devices  63.4 us (31%)
  starting transfers between devices  30.3 us (15%)
  matrix products  29.7 us (14%)
  local copies, waits for them, and re-layouts  25.6 us (12%)
  blocking collectives  24.3 us (12%)
  other arithmetic  16.9 us (8%)
  between operations  13.7 us (7%)
    all_to_all x1, blocking collectives, per_device(): lax.all_to_all(latent_out, 'member', split_axis=1, concat_axis=0, tiled=T...  24.3 us
    all_to_all x1, waiting for transfers between devices, per_device(): lax.all_to_all(results.reshape(experts, capacity, columns), ('group', 'me...  23.1 us
    all_to_all x1, waiting for transfers between devices, per_device(): lax.all_to_all(outgoing.reshape(experts, capacity, columns), ('group', 'm...  19.2 us
    all_to_all x1, starting transfers between devices, per_device(): lax.all_to_all(outgoing.reshape(experts, capacity, columns), ('group', 'm...  14.4 us
    all_to_all x1, waiting for transfers between devices, per_device(): lax.all_to_all(pieces, 'member', split_axis=0, concat_axis=0, tiled=True)  14.3 us
    dot_general x1, matrix products, per_device(): jnp.einsum('sf,fgc->gsc', inner, w_down[0].reshape(-1, groups, columns),...  11 us
    unnamed x22, local copies, waits for them, and re-layouts  10.6 us
    reduce_or x1, other arithmetic, per_device(): send_map = jnp.any(matches, axis=2).astype(jnp.bfloat16)  7.43 us
  transfers between devices with their start and end apart: 5, of which 4 were waited for; matrix products, arithmetic and copies ran while one was open for 19% of the time, Pallas kernels for 0%

profile of v8, /device:TPU:1, one launch (start us, length us, event | category | flops | bytes accessed | tf_op | source)
XLA Modules:
  0.0 203.8 jit_solution(17530087797017512457)
XLA Ops:
  7.3 2.8 %slice_bitcast_fusion.3 = (bf16[4,128,576]{1,2,0:T(8,128)(2,1)S(1)}, bf16[4,128,576]{1,2,0:T(8,128)(2,1)}, bf16[4,128,576]{1,2,0:T(8,128)(2,1)}, bf16[4,128,576]{1,2,0:T(8,128)(2,1)S(1)}) fusion(bf16[4,4,128,576]{2,3,1,0:T(8,128)(2,1)} %bitcast.105), kind=kLoop, calls=%fused_computation.33 | loop fusion | bytes 4718592 | tf_op jit(solution)/shard_map/jit(_where)/broadcast_in_dim | solution.py:39
  10.7 1.4 copy.90
  12.0 2.1 %copy.91 = bf16[4,128,576]{2,1,0:T(8,128)(2,1)} copy(bf16[4,128,576]{1,2,0:T(8,128)(2,1)} %get-tuple-element.16) | data formatting | bytes 1179648 | tf_op jit(solution)/shard_map/broadcast_in_dim | solution.py:37
  14.2 1.7 fusion.8
  16.4 1.3 fusion.34
  19.5 24.3 %all_to_all.33 = bf16[16,64,512]{2,0,1:T(8,128)(2,1)S(1)} all-to-all(bf16[16,64,512]{2,0,1:T(8,128)(2,1)S(1)} %copy.93), channel_id=1, replica_groups=mesh['group'=8,'member'=16] {'member'}, dimensions={1} | all-to-all | bytes 2097152 | tf_op jit(solution)/shard_map/all_to_all | solution.py:54
  44.7 4.4 %fusion.11 = bf16[2,128,8,448]{1,3,2,0:T(8,128)(2,1)} fusion(bf16[56,8,8,512]{3,2,1,0:T(8,128)(2,1)} %bitcast.114, bf16[2,128,512,1]{2,1,0,3:T(8,128)(2,1)S(1)} %reshape.101), kind=kOutput, calls=%fused_computation.19 | convolution fusion | flops 940441600 | bytes 5767168 | tf_op jit(solution)/shard_map/irk,ckn->icrn/dot_general | solution.py:61
  49.2 4.6 %all-to-all-start.1 = ((bf16[16,128,448]{1,2,0:T(8,128)(2,1)}), bf16[16,128,448]{1,2,0:T(8,128)(2,1)S(1)}, u32[]{:S(2)}, u32[]{:S(2)}) async-start(bf16[16,128,448]{1,2,0:T(8,128)(2,1)} %bitcast.108), calls=%async_computation.1 | async-start | bytes 3670016 | tf_op jit(solution)/shard_map/all_to_all | solution.py:67
  55.1 7.4 %fusion.2 = pred[2048,128]{1,0:T(8,128)(4,1)S(1)} fusion(s32[128,8]{0,1:T(8,128)S(1)} %multiply_add_fusion.1), kind=kLoop, calls=%fused_computation.4 | loop fusion | flops 3932160 | bytes 266240 | tf_op jit(solution)/shard_map/reduce_or | solution.py:78
  62.7 14.3 %all-to-all-done.1 = bf16[16,128,448]{1,2,0:T(8,128)(2,1)S(1)} async-done(((bf16[16,128,448]{1,2,0:T(8,128)(2,1)}), bf16[16,128,448]{1,2,0:T(8,128)(2,1)S(1)}, u32[]{:S(2)}, u32[]{:S(2)}) %all-to-all-start.1) | async-done | bytes 1835040 | tf_op jit(solution)/shard_map/all_to_all | solution.py:67
  77.2 6.5 %collective-permute-start = (f32[128,448]{0,1:T(8,128)S(1)}, f32[128,448]{0,1:T(8,128)S(1)}, u32[]{:S(2)}, u32[]{:S(2)}) collective-permute-start(f32[128,448]{0,1:T(8,128)S(1)} %convert_reduce_fusion), channel_id=1, source_target_pairs={{0,0},{1,16},{2,32},{3,48},{4,64},{5,80},{6,96},{7,112},{8,1},{9,1... | collective-permute-start | bytes 688136 | tf_op jit(solution)/shard_map/ppermute | solution.py:86
  83.7 6.1 %collective-permute-done = f32[128,448]{0,1:T(8,128)S(1)} collective-permute-done((f32[128,448]{0,1:T(8,128)S(1)}, f32[128,448]{0,1:T(8,128)S(1)}, u32[]{:S(2)}, u32[]{:S(2)}) %collective-permute-start) | collective-permute-done | bytes 229408 | tf_op jit(solution)/shard_map/ppermute | solution.py:86
  90.4 2.5 %copy.103 = bf16[2048,448]{1,0:T(8,128)(2,1)} copy(bf16[2048,448]{0,1:T(8,128)(2,1)S(1)} %convolution_convert_fusion) | data formatting | bytes 3670016 | tf_op jit(solution)/shard_map/convert_element_type | solution.py:88
  92.9 14.4 %all-to-all-start.2 = ((bf16[128,16,448]{2,1,0:T(8,128)(2,1)}), bf16[128,16,448]{2,1,0:T(8,128)(2,1)S(1)}, u32[]{:S(2)}, u32[]{:S(2)}) async-start(bf16[128,16,448]{2,1,0:T(8,128)(2,1)} %bitcast.24), calls=%async_computation.2 | async-start | bytes 4194304 | tf_op jit(solution)/shard_map/all_to_all | solution.py:89
  107.3 10.4 %copy.106 = bf16[1,1024,3584]{1,2,0:T(8,128)(2,1)} copy(bf16[1,1024,3584]{2,1,0:T(8,128)(2,1)} %param.23) | data formatting | bytes 14680064 | tf_op args[11]
  117.7 19.2 %all-to-all-done.2 = bf16[128,16,448]{2,1,0:T(8,128)(2,1)S(1)} async-done(((bf16[128,16,448]{2,1,0:T(8,128)(2,1)}), bf16[128,16,448]{2,1,0:T(8,128)(2,1)S(1)}, u32[]{:S(2)}, u32[]{:S(2)}) %all-to-all-start.2) | async-done | bytes 1835040 | tf_op jit(solution)/shard_map/all_to_all | solution.py:89
  136.9 6.1 %convolution_bitcast_fusion.1 = f32[256,1024]{1,0:T(8,128)} fusion(bf16[8,256,448]{2,1,0:T(8,128)(2,1)S(1)} %bitcast.106, bf16[8,448,1024]{2,1,0:T(8,128)(2,1)} %bitcast.112), kind=kOutput, calls=%fused_computation.22 | convolution fusion | flops 1879048192 | bytes 10223616 | tf_op jit(solution)/shard_map/gsc,gcf->sf/dot_general | solution.py:97
  143.0 11.0 %convert_bitcast_fusion = bf16[8,256,448]{1,2,0:T(8,128)(2,1)} fusion(bf16[1024,8,448]{0,2,1:T(8,128)(2,1)} %bitcast.102, bf16[8,256,448]{2,1,0:T(8,128)(2,1)S(1)} %bitcast.107, bf16[8,448,1024]{2,1,0:T(8,128)(2,1)} %bitcast.113, f32[256,1024]{1,0:T(8,128)} %convolution_bitcast_fusion.1), kind=kOutput, calls=%fused_computation.18 | convolution fusion | flops 3760586752 | bytes 19398656 | tf_op jit(solution)/shard_map/sf,fgc->gsc/dot_general | solution.py:106
  154.1 3.8 %copy.107 = bf16[8,256,448]{2,1,0:T(8,128)(2,1)} copy(bf16[8,256,448]{1,2,0:T(8,128)(2,1)} %convert_bitcast_fusion) | data formatting | bytes 3670016 | tf_op jit(solution)/shard_map/convert_element_type | solution.py:109
  157.9 4.8 %all-to-all-start.3 = ((bf16[128,16,448]{2,1,0:T(8,128)(2,1)}), bf16[128,16,448]{2,1,0:T(8,128)(2,1)S(1)}, u32[]{:S(2)}, u32[]{:S(2)}) async-start(bf16[128,16,448]{2,1,0:T(8,128)(2,1)} %bitcast.101), calls=%async_computation.3 | async-start | bytes 4194304 | tf_op jit(solution)/shard_map/all_to_all | solution.py:110
  163.0 6.3 %fusion.4 = (bf16[128,2048]{1,0:T(8,128)(2,1)}, bf16[128,2048]{1,0:T(8,128)(2,1)}) fusion(s32[128,8]{1,0:T(8,128)S(1)} %eq.92, bf16[128,8]{1,0:T(8,128)(2,1)S(1)} %copy.108, bf16[128,8]{1,0:T(8,128)(2,1)S(1)} %copy.102), kind=kLoop, calls=%fused_computation.6 | loop fusion | flops 9961472 | bytes 1056768 | tf_op jit(solution)/shard_map/reduce_sum | solution.py:124
  169.3 23.1 %all-to-all-done.3 = bf16[128,16,448]{2,1,0:T(8,128)(2,1)S(1)} async-done(((bf16[128,16,448]{2,1,0:T(8,128)(2,1)}), bf16[128,16,448]{2,1,0:T(8,128)(2,1)S(1)}, u32[]{:S(2)}, u32[]{:S(2)}) %all-to-all-start.3) | async-done | bytes 1835040 | tf_op jit(solution)/shard_map/all_to_all | solution.py:110
  192.4 2.1 %fusion.35 = f32[128,448]{0,1:T(8,128)S(1)} fusion(bf16[128,2048]{1,0:T(8,128)(2,1)} %get-tuple-element.12, bf16[2048,448]{1,0:T(8,128)(2,1)S(1)} %bitcast.99), kind=kOutput, calls=%fused_computation.69 | convolution fusion | flops 234881024 | bytes 2588672 | tf_op jit(solution)/shard_map/dot_general | solution.py:125
  194.5 2.4 %add_convert_fusion.1 = bf16[128,448]{0,1:T(8,128)(2,1)} fusion(f32[128,448]{0,1:T(8,128)} %copy-done.3, bf16[128,448]{0,1:T(8,128)(2,1)S(1)} %copy-done.5, f32[128,448]{0,1:T(8,128)S(1)} %fusion.35, bf16[128,2048]{1,0:T(8,128)(2,1)S(1)} %copy-done.2, bf16[2048,448]{1,0:T(8,128)(2,1)S(1)} %bitcast.100), kind=kOutput, calls=%fused_computation.50 | convolution fusion | flops 235282432 | bytes 3047424 | tf_op jit(solution)/shard_map/dot_general | solution.py:125
  (59 shorter events, 7.1 us)
Async XLA Ops:
  6.5 9.4 %copy-start = (bf16[16,64,576]{2,1,0:T(8,128)(2,1)S(1)}, bf16[16,64,576]{2,1,0:T(8,128)(2,1)}, u32[]{:S(2)}) copy-start(bf16[16,64,576]{2,1,0:T(8,128)(2,1)} %param.12) | copy-start | bytes 3538948
  6.5 38.2 %all-gather.3.cloned.1.call-start = ((), (), s32[]{:S(2)}) async-start(), calls=%async_computation.4 | async-start | bytes 4128768 | tf_op jit(solution)/shard_map/all_gather | solution.py:59
  10.0 4.1 %copy-start.9 = (s32[16]{0:T(128)S(1)}, s32[16]{0:T(128)}, u32[]{:S(2)}) copy-start(s32[16]{0:T(128)} %param.15) | copy-start | bytes 196
  14.2 1.7 copy-start.7
  19.5 24.4 %copy-start.4 = (bf16[4,512,128]{2,1,0:T(8,128)(2,1)S(1)}, bf16[4,512,128]{2,1,0:T(8,128)(2,1)}, u32[]{:S(2)}) copy-start(bf16[4,512,128]{2,1,0:T(8,128)(2,1)} %param.16) | copy-start | bytes 1572868
  49.2 4.6 %copy-start.6 = (s32[128,8]{0,1:T(8,128)S(1)}, s32[128,8]{0,1:T(8,128)}, u32[]{:S(2)}) copy-start(s32[128,8]{0,1:T(8,128)} %param.19) | copy-start | bytes 12292
  49.2 27.8 %all-to-all-start.1 = ((bf16[16,128,448]{1,2,0:T(8,128)(2,1)}), bf16[16,128,448]{1,2,0:T(8,128)(2,1)S(1)}, u32[]{:S(2)}, u32[]{:S(2)}) async-start(bf16[16,128,448]{1,2,0:T(8,128)(2,1)} %bitcast.108), calls=%async_computation.1 | async-start | bytes 3670016 | tf_op jit(solution)/shard_map/all_to_all | solution.py:67
  54.5 35.3 %copy-start.5 = (bf16[128,448]{0,1:T(8,128)(2,1)S(1)}, bf16[128,448]{0,1:T(8,128)(2,1)}, u32[]{:S(2)}) copy-start(bf16[128,448]{0,1:T(8,128)(2,1)} %param.18) | copy-start | bytes 344068
  77.2 12.5 %collective-permute-start = (f32[128,448]{0,1:T(8,128)S(1)}, f32[128,448]{0,1:T(8,128)S(1)}, u32[]{:S(2)}, u32[]{:S(2)}) collective-permute-start(f32[128,448]{0,1:T(8,128)S(1)} %convert_reduce_fusion), channel_id=1, source_target_pairs={{0,0},{1,16},{2,32},{3,48},{4,64},{5,80},{6,96},{7,112},{8,1},{9,1... | collective-permute-start | bytes 688136 | tf_op jit(solution)/shard_map/ppermute | solution.py:86
  89.8 3.1 %copy-start.3 = (f32[128,448]{0,1:T(8,128)}, f32[128,448]{0,1:T(8,128)S(1)}, u32[]{:S(2)}) copy-start(f32[128,448]{0,1:T(8,128)S(1)} %collective-permute-done) | copy-start | bytes 688132
  92.9 44.0 %all-to-all-start.2 = ((bf16[128,16,448]{2,1,0:T(8,128)(2,1)}), bf16[128,16,448]{2,1,0:T(8,128)(2,1)S(1)}, u32[]{:S(2)}, u32[]{:S(2)}) async-start(bf16[128,16,448]{2,1,0:T(8,128)(2,1)} %bitcast.24), calls=%async_computation.2 | async-start | bytes 4194304 | tf_op jit(solution)/shard_map/all_to_all | solution.py:89
  157.9 4.8 %copy-start.8 = (f32[128,8]{0,1:T(8,128)S(1)}, f32[128,8]{0,1:T(8,128)}, u32[]{:S(2)}) copy-start(f32[128,8]{0,1:T(8,128)} %param.20) | copy-start | bytes 12292
  157.9 34.6 %all-to-all-start.3 = ((bf16[128,16,448]{2,1,0:T(8,128)(2,1)}), bf16[128,16,448]{2,1,0:T(8,128)(2,1)S(1)}, u32[]{:S(2)}, u32[]{:S(2)}) async-start(bf16[128,16,448]{2,1,0:T(8,128)(2,1)} %bitcast.101), calls=%async_computation.3 | async-start | bytes 4194304 | tf_op jit(solution)/shard_map/all_to_all | solution.py:110
  192.4 2.1 %copy-start.2 = (bf16[128,2048]{1,0:T(8,128)(2,1)S(1)}, bf16[128,2048]{1,0:T(8,128)(2,1)}, u32[]{:S(2)}) copy-start(bf16[128,2048]{1,0:T(8,128)(2,1)} %get-tuple-element.11) | copy-start | bytes 1572868
  192.4 4.5 %copy-start.1 = (bf16[16,64,576]{2,1,0:T(8,128)(2,1)S(1)}, bf16[16,64,576]{2,1,0:T(8,128)(2,1)}, u32[]{:S(2)}) copy-start(bf16[16,64,576]{2,1,0:T(8,128)(2,1)} %param.12) | copy-start | bytes 3538948
Sparse Core Ops, SparseCore 0:
  9.0 33.4 all-gather.2

commit v9 on v7

--- a/solution.py
+++ b/solution.py
@@ -65,42 +65,51 @@
         preferred_element_type=jnp.float32,
     ).astype(jnp.bfloat16).reshape(members, -1, columns)
     pieces = lax.all_to_all(pieces, "member", split_axis=0, concat_axis=0, tiled=True)
-    summed = jnp.sum(pieces.astype(jnp.float32), axis=0)
-    owner = [
+    block_rows = residual.shape[0]
+    capacity = max(2, 2 * rows * TOP // members)
+    positions = jnp.arange(experts * capacity, dtype=jnp.int32)
+    to_owner = [
         (g * members + m, (m % groups) * members + (m // groups) + halves * g)
         for g in range(groups)
         for m in range(members)
     ]
-    attention = lax.ppermute(summed, ("group", "member"), perm=owner)
-    hidden_in = (residual.astype(jnp.float32) + attention).astype(jnp.bfloat16)
-    block_rows = hidden_in.shape[0]
-    capacity = max(2, 2 * rows * TOP // members)
-    flat_ids = expert_ids.reshape(-1)
-    onehot = (flat_ids[:, None] == jnp.arange(experts, dtype=jnp.int32)[None, :]).astype(jnp.int32)
-    ranking = jnp.sum((jnp.cumsum(onehot, axis=0) - onehot) * onehot, axis=1)
-    slot_index = flat_ids * capacity + ranking
-    positions = jnp.arange(experts * capacity, dtype=jnp.int32)
-    matches = (positions[:, None] == slot_index[None, :]).reshape(
+    to_holder = [(b, a) for a, b in to_owner]
+    everyone = ("group", "member")
+    held_residual = lax.ppermute(residual, everyone, perm=to_holder)
+    held_ids = lax.ppermute(expert_ids, everyone, perm=to_holder)
+
+    def route(ids):
+        flat_ids = ids.reshape(-1)
+        onehot = (flat_ids[:, None] == jnp.arange(experts, dtype=jnp.int32)[None, :]).astype(jnp.int32)
+        ranking = jnp.sum((jnp.cumsum(onehot, axis=0) - onehot) * onehot, axis=1)
+        return flat_ids * capacity + ranking
+
+    held_slots = route(held_ids)
+    matches = (positions[:, None] == held_slots[None, :]).reshape(
         experts * capacity, block_rows, TOP
     )
     send_map = jnp.any(matches, axis=2).astype(jnp.bfloat16)
-    outgoing = jnp.dot(send_map, hidden_in, preferred_element_type=jnp.float32).astype(jnp.bfloat16)
+    pieces, send_map = lax.optimization_barrier((pieces, send_map))
+    summed = jnp.sum(pieces.astype(jnp.float32), axis=0)
+    held_hidden = (held_residual.astype(jnp.float32) + summed).astype(jnp.bfloat16)
+    outgoing = jnp.dot(send_map, held_hidden, preferred_element_type=jnp.float32).astype(jnp.bfloat16)
+    hidden_in = lax.ppermute(held_hidden, everyone, perm=to_owner)
     arrived = lax.all_to_all(
         outgoing.reshape(experts, capacity, columns),
-        ("group", "member"),
+        everyone,
         split_axis=0,
         concat_axis=0,
         tiled=True,
     )
-    arrived = arrived.reshape(groups, members * capacity, columns)
+    arrived = arrived.reshape(groups, halves, groups, capacity, columns)
     gate = jnp.einsum(
-        "gsc,gcf->sf", arrived, w_gate[0].reshape(groups, columns, -1),
+        "gicsn,cnf->gisf", arrived, w_gate[0].reshape(groups, columns, -1),
         preferred_element_type=jnp.float32,
-    )
+    ).reshape(members * capacity, -1)
     upper = jnp.einsum(
-        "gsc,gcf->sf", arrived, w_up[0].reshape(groups, columns, -1),
+        "gicsn,cnf->gisf", arrived, w_up[0].reshape(groups, columns, -1),
         preferred_element_type=jnp.float32,
-    )
+    ).reshape(members * capacity, -1)
     inner = (jax.nn.silu(gate) * upper).astype(jnp.bfloat16)
     results = jnp.einsum(
         "sf,fgc->gsc", inner, w_down[0].reshape(-1, groups, columns),
@@ -108,13 +117,13 @@
     ).astype(jnp.bfloat16)
     returned = lax.all_to_all(
         results.reshape(experts, capacity, columns),
-        ("group", "member"),
+        everyone,
         split_axis=0,
         concat_axis=0,
         tiled=True,
     )
     returned = returned.reshape(experts * capacity, columns)
-    slots = slot_index.reshape(block_rows, TOP)
+    slots = route(expert_ids).reshape(block_rows, TOP)
     gate_hi = route_gates.astype(jnp.bfloat16)
     gate_lo = (route_gates - gate_hi.astype(jnp.float32)).astype(jnp.bfloat16)
     hit = slots[:, :, None] == positions[None, None, :]

time: 205 us -> 203 us (level)
  waiting for transfers between devices: 64.9 us -> 44.3 us
  starting transfers between devices: 29 us -> 41.9 us
  local copies, waits for them, and re-layouts: 25.6 us -> 32.1 us
  matrix products: 29.7 us -> 26.8 us
  other arithmetic: 16.7 us -> 19.1 us
    all_to_all x1, waiting for transfers between devices: 21.9 us -> 0.01 us  [per_device(): lax.all_to_all(pieces, 'member', split_axis=0, concat_axis=0, tiled=True)]
    ppermute x1 -> x3, starting transfers between devices: 6.63 us -> 15.3 us  [the longest x1 5.55 us: per_device(): hidden_in = lax.ppermute(held_hidden, everyone, perm=to_owner)]
    ppermute x1 -> x3, waiting for transfers between devices: 0.01 us -> 7.72 us  [the longest x1 7.71 us: per_device(): held_ids = lax.ppermute(expert_ids, everyone, perm=to_holder)]
    all_to_all x2, waiting for transfers between devices: 42.3 us -> 35.9 us  [the longest x1 18.8 us: per_device(): lax.all_to_all(outgoing.reshape(experts, capacity, columns), everyone, sp...]
    all_to_all x2, starting transfers between devices: 17.8 us -> 22 us  [the longest x1 17.4 us: per_device(): lax.all_to_all(outgoing.reshape(experts, capacity, columns), everyone, sp...]
    dot_general x0 -> x1, local copies, waits for them, and re-layouts: none -> 3.1 us  [per_device(): jnp.einsum('gicsn,cnf->gisf', arrived, w_gate[0].reshape(groups, columns,...]
    reshape x0 -> x1, local copies, waits for them, and re-layouts: none -> 2.76 us  [per_device(): arrived = arrived.reshape(groups, halves, groups, capacity, columns)]
    unnamed x22 -> x20, local copies, waits for them, and re-layouts: 10.6 us -> 10.6 us
  transfers between devices with their start and end apart: 5 -> 7, of which waited for: 3 -> 3; matrix products, arithmetic and copies ran while one was open for 19% -> 21% of each run, Pallas kernels for 0% -> 0%
where the time goes in v9:
time: 203 us; the launch traced here: 202 us
  waiting for transfers between devices  44.3 us (22%)
  starting transfers between devices  41.9 us (21%)
  local copies, waits for them, and re-layouts  32.1 us (16%)
  matrix products  26.8 us (13%)
  blocking collectives  24.3 us (12%)
  other arithmetic  19.1 us (9%)
  between operations  13.8 us (7%)
    all_to_all x1, blocking collectives, per_device(): lax.all_to_all(latent_out, 'member', split_axis=1, concat_axis=0, tiled=T...  24.3 us
    all_to_all x1, waiting for transfers between devices, per_device(): lax.all_to_all(outgoing.reshape(experts, capacity, columns), everyone, sp...  18.8 us
    all_to_all x1, starting transfers between devices, per_device(): lax.all_to_all(outgoing.reshape(experts, capacity, columns), everyone, sp...  17.4 us
    all_to_all x1, waiting for transfers between devices, per_device(): lax.all_to_all(results.reshape(experts, capacity, columns), everyone, spl...  17 us
    dot_general x1, matrix products, per_device(): jnp.einsum('sf,fgc->gsc', inner, w_down[0].reshape(-1, groups, columns),...  10.7 us
    unnamed x20, local copies, waits for them, and re-layouts  10.6 us
    ppermute x1, waiting for transfers between devices, per_device(): held_ids = lax.ppermute(expert_ids, everyone, perm=to_holder)  7.71 us
    reduce_or x1, other arithmetic, per_device(): send_map = jnp.any(matches, axis=2).astype(jnp.bfloat16)  7.43 us
  transfers between devices with their start and end apart: 7, of which 3 were waited for; matrix products, arithmetic and copies ran while one was open for 21% of the time, Pallas kernels for 0%

profile of v9, /device:TPU:1, one launch (start us, length us, event | category | flops | bytes accessed | tf_op | source)
XLA Modules:
  0.0 202.4 jit_solution(8732762531402283836)
XLA Ops:
  7.3 2.8 %slice_bitcast_fusion.3 = (bf16[4,128,576]{1,2,0:T(8,128)(2,1)S(1)}, bf16[4,128,576]{1,2,0:T(8,128)(2,1)}, bf16[4,128,576]{1,2,0:T(8,128)(2,1)}, bf16[4,128,576]{1,2,0:T(8,128)(2,1)S(1)}) fusion(bf16[4,4,128,576]{2,3,1,0:T(8,128)(2,1)} %bitcast.123), kind=kLoop, calls=%fused_computation.33 | loop fusion | bytes 4718592 | tf_op jit(solution)/shard_map/jit(_where)/broadcast_in_dim | solution.py:39
  12.0 2.1 %copy.105 = bf16[4,128,576]{2,1,0:T(8,128)(2,1)} copy(bf16[4,128,576]{1,2,0:T(8,128)(2,1)} %get-tuple-element.14) | data formatting | bytes 1179648 | tf_op jit(solution)/shard_map/broadcast_in_dim | solution.py:37
  14.2 1.7 fusion.8
  19.5 24.3 %all_to_all.33 = bf16[16,64,512]{2,0,1:T(8,128)(2,1)S(1)} all-to-all(bf16[16,64,512]{2,0,1:T(8,128)(2,1)S(1)} %copy.107), channel_id=1, replica_groups=mesh['group'=8,'member'=16] {'member'}, dimensions={1} | all-to-all | bytes 2097152 | tf_op jit(solution)/shard_map/all_to_all | solution.py:54
  44.7 4.4 %fusion.11 = bf16[2,128,8,448]{1,3,2,0:T(8,128)(2,1)} fusion(bf16[56,8,8,512]{3,2,1,0:T(8,128)(2,1)} %bitcast.129, bf16[2,128,512,1]{2,1,0,3:T(8,128)(2,1)S(1)} %reshape.129), kind=kOutput, calls=%fused_computation.19 | convolution fusion | flops 940441600 | bytes 5767168 | tf_op jit(solution)/shard_map/irk,ckn->icrn/dot_general | solution.py:61
  49.2 4.6 %all-to-all-start.1 = ((bf16[16,128,448]{1,2,0:T(8,128)(2,1)}), bf16[16,128,448]{1,2,0:T(8,128)(2,1)S(1)}, u32[]{:S(2)}, u32[]{:S(2)}) async-start(bf16[16,128,448]{1,2,0:T(8,128)(2,1)} %bitcast.124), calls=%async_computation.1 | async-start | bytes 3670016 | tf_op jit(solution)/shard_map/all_to_all | solution.py:67
  53.8 4.7 %collective-permute-start.1 = (s32[128,8]{0,1:T(8,128)S(1)}, s32[128,8]{0,1:T(8,128)S(1)}, u32[]{:S(2)}, u32[]{:S(2)}) collective-permute-start(s32[128,8]{0,1:T(8,128)S(1)} %copy-done.4), channel_id=1, source_target_pairs={{0,0},{16,1},{32,2},{48,3},{64,4},{80,5},{96,6},{112,7},{1,8},{17,... | collective-permute-start | bytes 12296 | tf_op jit(solution)/shard_map/ppermute | solution.py:79
  58.5 5.1 %collective-permute-start = (bf16[128,448]{0,1:T(8,128)(2,1)S(1)}, bf16[128,448]{0,1:T(8,128)(2,1)S(1)}, u32[]{:S(2)}, u32[]{:S(2)}) collective-permute-start(bf16[128,448]{0,1:T(8,128)(2,1)S(1)} %copy-done.8), channel_id=1, source_target_pairs={{0,0},{16,1},{32,2},{48,3},{64,4},{80,5},{96,6},{112,7},{1,8},{17,... | collective-permute-start | bytes 344072 | tf_op jit(solution)/shard_map/ppermute | solution.py:78
  63.5 7.7 %collective-permute-done.1 = s32[128,8]{0,1:T(8,128)S(1)} collective-permute-done((s32[128,8]{0,1:T(8,128)S(1)}, s32[128,8]{0,1:T(8,128)S(1)}, u32[]{:S(2)}, u32[]{:S(2)}) %collective-permute-start.1) | collective-permute-done | bytes 4128 | tf_op jit(solution)/shard_map/ppermute | solution.py:79
  72.6 7.4 %fusion.2 = pred[2048,128]{1,0:T(8,128)(4,1)S(1)} fusion(s32[128,8]{0,1:T(8,128)S(1)} %multiply_add_fusion.1), kind=kLoop, calls=%fused_computation.4 | loop fusion | flops 3932160 | bytes 266240 | tf_op jit(solution)/shard_map/reduce_or | solution.py:91
  81.1 2.5 %copy.123 = bf16[2048,448]{1,0:T(8,128)(2,1)} copy(bf16[2048,448]{0,1:T(8,128)(2,1)S(1)} %convolution_convert_fusion) | data formatting | bytes 3670016 | tf_op jit(solution)/shard_map/convert_element_type | solution.py:95
  83.6 17.4 %all-to-all-start.2 = ((bf16[128,16,448]{2,1,0:T(8,128)(2,1)}), bf16[128,16,448]{2,1,0:T(8,128)(2,1)S(1)}, u32[]{:S(2)}, u32[]{:S(2)}) async-start(bf16[128,16,448]{2,1,0:T(8,128)(2,1)} %bitcast.117), calls=%async_computation.2 | async-start | bytes 4194304 | tf_op jit(solution)/shard_map/all_to_all | solution.py:97
  101.2 10.4 %copy.127 = bf16[1,1024,3584]{1,2,0:T(8,128)(2,1)} copy(bf16[1,1024,3584]{2,1,0:T(8,128)(2,1)} %param.23) | data formatting | bytes 14680064 | tf_op args[11]
  111.7 18.8 %all-to-all-done.2 = bf16[128,16,448]{2,1,0:T(8,128)(2,1)S(1)} async-done(((bf16[128,16,448]{2,1,0:T(8,128)(2,1)}), bf16[128,16,448]{2,1,0:T(8,128)(2,1)S(1)}, u32[]{:S(2)}, u32[]{:S(2)}) %all-to-all-start.2) | async-done | bytes 1835040 | tf_op jit(solution)/shard_map/all_to_all | solution.py:97
  130.6 2.8 %copy.124 = bf16[8,2,8,16,448]{4,2,3,1,0:T(8,128)(2,1)} copy(bf16[8,2,8,16,448]{4,3,2,1,0:T(8,128)(2,1)S(1)} %bitcast.116) | data formatting | bytes 3670016 | tf_op jit(solution)/shard_map/reshape | solution.py:104
  133.3 3.1 %copy.125 = bf16[256,8,448]{0,2,1:T(8,128)(2,1)S(1)} copy(bf16[256,8,448]{2,1,0:T(8,128)(2,1)} %bitcast.118) | data formatting | bytes 3670016 | tf_op jit(solution)/shard_map/gicsn,cnf->gisf/dot_general | solution.py:105
  136.4 5.2 %convolution_bitcast_fusion.1 = f32[256,1024]{1,0:T(8,128)S(1)} fusion(bf16[256,8,448]{0,2,1:T(8,128)(2,1)S(1)} %copy.125, bf16[8,448,1024]{2,1,0:T(8,128)(2,1)} %bitcast.119), kind=kOutput, calls=%fused_computation.22 | convolution fusion | flops 1879048192 | bytes 10223616 | tf_op jit(solution)/shard_map/gicsn,cnf->gisf/dot_general | solution.py:105
  141.6 10.7 %convert_bitcast_fusion = bf16[8,256,448]{1,2,0:T(8,128)(2,1)} fusion(bf16[1024,8,448]{0,2,1:T(8,128)(2,1)} %bitcast.120, bf16[256,8,448]{0,2,1:T(8,128)(2,1)S(1)} %copy.125, bf16[8,448,1024]{2,1,0:T(8,128)(2,1)} %bitcast.128, f32[256,1024]{1,0:T(8,128)S(1)} %convolution_bitcast_fusion.1), kind=kOutput, calls=%fused_computation.18 | convolution fusion | flops 3760586752 | bytes 19398656 | tf_op jit(solution)/shard_map/sf,fgc->gsc/dot_general | solution.py:114
  152.3 3.8 %copy.128 = bf16[8,256,448]{2,1,0:T(8,128)(2,1)} copy(bf16[8,256,448]{1,2,0:T(8,128)(2,1)} %convert_bitcast_fusion) | data formatting | bytes 3670016 | tf_op jit(solution)/shard_map/convert_element_type | solution.py:117
  156.1 4.7 %all-to-all-start.3 = ((bf16[128,16,448]{2,1,0:T(8,128)(2,1)}), bf16[128,16,448]{2,1,0:T(8,128)(2,1)S(1)}, u32[]{:S(2)}, u32[]{:S(2)}) async-start(bf16[128,16,448]{2,1,0:T(8,128)(2,1)} %bitcast.115), calls=%async_computation.3 | async-start | bytes 4194304 | tf_op jit(solution)/shard_map/all_to_all | solution.py:118
  162.1 6.3 %fusion.4 = (bf16[128,2048]{1,0:T(8,128)(2,1)}, bf16[128,2048]{1,0:T(8,128)(2,1)}) fusion(s32[128,8]{1,0:T(8,128)S(1)} %copy.121, bf16[128,8]{1,0:T(8,128)(2,1)S(1)} %copy.129, bf16[128,8]{1,0:T(8,128)(2,1)S(1)} %copy.122), kind=kLoop, calls=%fused_computation.6 | loop fusion | flops 9961472 | bytes 1056768 | tf_op jit(solution)/shard_map/reduce_sum | solution.py:132
  168.4 5.6 %collective-permute-start.2 = (bf16[128,448]{0,1:T(8,128)(2,1)S(1)}, bf16[128,448]{0,1:T(8,128)(2,1)}, u32[]{:S(2)}, u32[]{:S(2)}) collective-permute-start(bf16[128,448]{0,1:T(8,128)(2,1)S(1)} %add_convert_fusion.2), channel_id=1, source_target_pairs={{0,0},{1,16},{2,32},{3,48},{4,64},{5,80},{6,96},{7,112},{8,1},{9,1... | collective-permute-start | bytes 344072 | tf_op jit(solution)/shard_map/ppermute | solution.py:96
  174.0 17.0 %all-to-all-done.3 = bf16[128,16,448]{2,1,0:T(8,128)(2,1)S(1)} async-done(((bf16[128,16,448]{2,1,0:T(8,128)(2,1)}), bf16[128,16,448]{2,1,0:T(8,128)(2,1)S(1)}, u32[]{:S(2)}, u32[]{:S(2)}) %all-to-all-start.3) | async-done | bytes 1835040 | tf_op jit(solution)/shard_map/all_to_all | solution.py:118
  191.0 2.1 %fusion.40 = f32[128,448]{0,1:T(8,128)S(1)} fusion(bf16[128,2048]{1,0:T(8,128)(2,1)} %get-tuple-element.10, bf16[2048,448]{1,0:T(8,128)(2,1)S(1)} %bitcast.113), kind=kOutput, calls=%fused_computation.79 | convolution fusion | flops 234881024 | bytes 2588672 | tf_op jit(solution)/shard_map/dot_general | solution.py:133
  (78 shorter events, 13.4 us)
Async XLA Ops:
  6.5 9.4 %copy-start = (bf16[16,64,576]{2,1,0:T(8,128)(2,1)S(1)}, bf16[16,64,576]{2,1,0:T(8,128)(2,1)}, u32[]{:S(2)}) copy-start(bf16[16,64,576]{2,1,0:T(8,128)(2,1)} %param.12) | copy-start | bytes 3538948
  6.5 38.2 %all-gather.3.cloned.1.call-start = ((), (), s32[]{:S(2)}) async-start(), calls=%async_computation.4 | async-start | bytes 4128768 | tf_op jit(solution)/shard_map/all_gather | solution.py:59
  10.0 4.1 %copy-start.7 = (s32[16]{0:T(128)S(1)}, s32[16]{0:T(128)}, u32[]{:S(2)}) copy-start(s32[16]{0:T(128)} %param.15) | copy-start | bytes 196
  14.2 1.7 copy-start.5
  19.5 24.4 %copy-start.3 = (bf16[4,512,128]{2,1,0:T(8,128)(2,1)S(1)}, bf16[4,512,128]{2,1,0:T(8,128)(2,1)}, u32[]{:S(2)}) copy-start(bf16[4,512,128]{2,1,0:T(8,128)(2,1)} %param.16) | copy-start | bytes 1572868
  49.2 4.6 %copy-start.4 = (s32[128,8]{0,1:T(8,128)S(1)}, s32[128,8]{0,1:T(8,128)}, u32[]{:S(2)}) copy-start(s32[128,8]{0,1:T(8,128)} %param.19) | copy-start | bytes 12292
  49.2 9.3 %copy-start.8 = (bf16[128,448]{0,1:T(8,128)(2,1)S(1)}, bf16[128,448]{0,1:T(8,128)(2,1)}, u32[]{:S(2)}) copy-start(bf16[128,448]{0,1:T(8,128)(2,1)} %param.18) | copy-start | bytes 344068
  49.2 31.0 %all-to-all-start.1 = ((bf16[16,128,448]{1,2,0:T(8,128)(2,1)}), bf16[16,128,448]{1,2,0:T(8,128)(2,1)S(1)}, u32[]{:S(2)}, u32[]{:S(2)}) async-start(bf16[16,128,448]{1,2,0:T(8,128)(2,1)} %bitcast.124), calls=%async_computation.1 | async-start | bytes 3670016 | tf_op jit(solution)/shard_map/all_to_all | solution.py:67
  53.8 17.5 %collective-permute-start.1 = (s32[128,8]{0,1:T(8,128)S(1)}, s32[128,8]{0,1:T(8,128)S(1)}, u32[]{:S(2)}, u32[]{:S(2)}) collective-permute-start(s32[128,8]{0,1:T(8,128)S(1)} %copy-done.4), channel_id=1, source_target_pairs={{0,0},{16,1},{32,2},{48,3},{64,4},{80,5},{96,6},{112,7},{1,8},{17,... | collective-permute-start | bytes 12296 | tf_op jit(solution)/shard_map/ppermute | solution.py:79
  58.5 21.9 %collective-permute-start = (bf16[128,448]{0,1:T(8,128)(2,1)S(1)}, bf16[128,448]{0,1:T(8,128)(2,1)S(1)}, u32[]{:S(2)}, u32[]{:S(2)}) collective-permute-start(bf16[128,448]{0,1:T(8,128)(2,1)S(1)} %copy-done.8), channel_id=1, source_target_pairs={{0,0},{16,1},{32,2},{48,3},{64,4},{80,5},{96,6},{112,7},{1,8},{17,... | collective-permute-start | bytes 344072 | tf_op jit(solution)/shard_map/ppermute | solution.py:78
  83.6 47.0 %all-to-all-start.2 = ((bf16[128,16,448]{2,1,0:T(8,128)(2,1)}), bf16[128,16,448]{2,1,0:T(8,128)(2,1)S(1)}, u32[]{:S(2)}, u32[]{:S(2)}) async-start(bf16[128,16,448]{2,1,0:T(8,128)(2,1)} %bitcast.117), calls=%async_computation.2 | async-start | bytes 4194304 | tf_op jit(solution)/shard_map/all_to_all | solution.py:97
  156.1 34.9 %all-to-all-start.3 = ((bf16[128,16,448]{2,1,0:T(8,128)(2,1)}), bf16[128,16,448]{2,1,0:T(8,128)(2,1)S(1)}, u32[]{:S(2)}, u32[]{:S(2)}) async-start(bf16[128,16,448]{2,1,0:T(8,128)(2,1)} %bitcast.115), calls=%async_computation.3 | async-start | bytes 4194304 | tf_op jit(solution)/shard_map/all_to_all | solution.py:118
  160.8 1.1 copy-start.6
  168.4 25.5 %collective-permute-start.2 = (bf16[128,448]{0,1:T(8,128)(2,1)S(1)}, bf16[128,448]{0,1:T(8,128)(2,1)}, u32[]{:S(2)}, u32[]{:S(2)}) collective-permute-start(bf16[128,448]{0,1:T(8,128)(2,1)S(1)} %add_convert_fusion.2), channel_id=1, source_target_pairs={{0,0},{1,16},{2,32},{3,48},{4,64},{5,80},{6,96},{7,112},{8,1},{9,1... | collective-permute-start | bytes 344072 | tf_op jit(solution)/shard_map/ppermute | solution.py:96
  191.0 2.1 %copy-start.2 = (bf16[128,2048]{1,0:T(8,128)(2,1)S(1)}, bf16[128,2048]{1,0:T(8,128)(2,1)}, u32[]{:S(2)}) copy-start(bf16[128,2048]{1,0:T(8,128)(2,1)} %get-tuple-element.9) | copy-start | bytes 1572868
  191.0 4.5 %copy-start.1 = (bf16[16,64,576]{2,1,0:T(8,128)(2,1)S(1)}, bf16[16,64,576]{2,1,0:T(8,128)(2,1)}, u32[]{:S(2)}) copy-start(bf16[16,64,576]{2,1,0:T(8,128)(2,1)} %param.12) | copy-start | bytes 3538948
Sparse Core Ops, SparseCore 0:
  9.0 33.4 all-gather.2

commit v10 on v9

--- a/solution.py
+++ b/solution.py
@@ -102,14 +102,16 @@
         tiled=True,
     )
     arrived = arrived.reshape(groups, halves, groups, capacity, columns)
-    gate = jnp.einsum(
-        "gicsn,cnf->gisf", arrived, w_gate[0].reshape(groups, columns, -1),
-        preferred_element_type=jnp.float32,
-    ).reshape(members * capacity, -1)
-    upper = jnp.einsum(
-        "gicsn,cnf->gisf", arrived, w_up[0].reshape(groups, columns, -1),
-        preferred_element_type=jnp.float32,
-    ).reshape(members * capacity, -1)
+    gate_w = w_gate[0].reshape(groups, columns, -1)
+    up_w = w_up[0].reshape(groups, columns, -1)
+    gate = None
+    upper = None
+    for c in range(groups):
+        block = arrived[:, :, c].reshape(members * capacity, columns)
+        g_part = jnp.dot(block, gate_w[c], preferred_element_type=jnp.float32)
+        u_part = jnp.dot(block, up_w[c], preferred_element_type=jnp.float32)
+        gate = g_part if gate is None else gate + g_part
+        upper = u_part if upper is None else upper + u_part
     inner = (jax.nn.silu(gate) * upper).astype(jnp.bfloat16)
     results = jnp.einsum(
         "sf,fgc->gsc", inner, w_down[0].reshape(-1, groups, columns),

time: 203 us -> 214 us (1.054)
  matrix products: 26.8 us -> 43.7 us
  waiting for transfers between devices: 44.3 us -> 39.3 us
  local copies, waits for them, and re-layouts: 32.1 us -> 28 us
    dot_general x1 -> x15, matrix products: 5.17 us -> 25.5 us  [the longest x8 13.1 us: per_device(): g_part = jnp.dot(block, gate_w[c], preferred_element_type=jnp.float32)]
    dot_general x1, matrix products: 10.7 us -> 6.33 us  [per_device(): jnp.einsum('sf,fgc->gsc', inner, w_down[0].reshape(-1, groups, columns),...]
    all_to_all x1, waiting for transfers between devices: 17 us -> 13.7 us  [per_device(): lax.all_to_all(results.reshape(experts, capacity, columns), everyone, spl...]
    dot_general x1 -> x0, local copies, waits for them, and re-layouts: 3.1 us -> none  [per_device(): jnp.einsum('gicsn,cnf->gisf', arrived, w_gate[0].reshape(groups, columns,...]
    reshape x1 -> x0, local copies, waits for them, and re-layouts: 2.76 us -> none  [per_device(): arrived = arrived.reshape(groups, halves, groups, capacity, columns)]
    unnamed x20 -> x22, local copies, waits for them, and re-layouts: 10.6 us -> 10.6 us
  transfers between devices with their start and end apart: 7 -> 7, of which waited for: 3 -> 3; matrix products, arithmetic and copies ran while one was open for 21% -> 23% of each run, Pallas kernels for 0% -> 0%
where the time goes in v10:
time: 214 us; the launch traced here: 213 us
  matrix products  43.7 us (20%)
  starting transfers between devices  42.9 us (20%)
  waiting for transfers between devices  39.3 us (18%)
  local copies, waits for them, and re-layouts  28 us (13%)
  blocking collectives  24.2 us (11%)
  other arithmetic  20.5 us (10%)
  between operations  13.9 us (6%)
    all_to_all x1, blocking collectives, per_device(): lax.all_to_all(latent_out, 'member', split_axis=1, concat_axis=0, tiled=T...  24.2 us
    all_to_all x1, starting transfers between devices, per_device(): lax.all_to_all(outgoing.reshape(experts, capacity, columns), everyone, sp...  18.4 us
    all_to_all x1, waiting for transfers between devices, per_device(): lax.all_to_all(outgoing.reshape(experts, capacity, columns), everyone, sp...  18.2 us
    all_to_all x1, waiting for transfers between devices, per_device(): lax.all_to_all(results.reshape(experts, capacity, columns), everyone, spl...  13.7 us
    dot_general x8, matrix products, per_device(): g_part = jnp.dot(block, gate_w[c], preferred_element_type=jnp.float32)  13.1 us
    dot_general x7, matrix products, per_device(): u_part = jnp.dot(block, up_w[c], preferred_element_type=jnp.float32)  12.4 us
    unnamed x22, local copies, waits for them, and re-layouts  10.6 us
    reduce_or x1, other arithmetic, per_device(): send_map = jnp.any(matches, axis=2).astype(jnp.bfloat16)  7.43 us
  transfers between devices with their start and end apart: 7, of which 3 were waited for; matrix products, arithmetic and copies ran while one was open for 23% of the time, Pallas kernels for 0%

profile of v10, /device:TPU:1, one launch (start us, length us, event | category | flops | bytes accessed | tf_op | source)
XLA Modules:
  0.0 212.5 jit_solution(16721088804674924748)
XLA Ops:
  7.3 2.8 %slice_bitcast_fusion.3 = (bf16[4,128,576]{1,2,0:T(8,128)(2,1)S(1)}, bf16[4,128,576]{1,2,0:T(8,128)(2,1)}, bf16[4,128,576]{1,2,0:T(8,128)(2,1)}, bf16[4,128,576]{1,2,0:T(8,128)(2,1)S(1)}) fusion(bf16[4,4,128,576]{2,3,1,0:T(8,128)(2,1)} %bitcast.204), kind=kLoop, calls=%fused_computation.79 | loop fusion | bytes 4718592 | tf_op jit(solution)/shard_map/jit(_where)/broadcast_in_dim | solution.py:39
  12.0 2.1 %copy.120 = bf16[4,128,576]{2,1,0:T(8,128)(2,1)} copy(bf16[4,128,576]{1,2,0:T(8,128)(2,1)} %get-tuple-element.14) | data formatting | bytes 1179648 | tf_op jit(solution)/shard_map/broadcast_in_dim | solution.py:37
  14.2 1.7 fusion.8
  19.6 24.2 %all_to_all.33 = bf16[16,64,512]{2,0,1:T(8,128)(2,1)S(1)} all-to-all(bf16[16,64,512]{2,0,1:T(8,128)(2,1)S(1)} %copy.122), channel_id=1, replica_groups=mesh['group'=8,'member'=16] {'member'}, dimensions={1} | all-to-all | bytes 2097152 | tf_op jit(solution)/shard_map/all_to_all | solution.py:54
  44.6 4.5 %fusion.11 = bf16[2,128,8,448]{1,3,2,0:T(8,128)(2,1)} fusion(bf16[56,8,8,512]{3,2,1,0:T(8,128)(2,1)} %bitcast.211, bf16[2,128,512,1]{2,1,0,3:T(8,128)(2,1)S(1)} %reshape.157), kind=kOutput, calls=%fused_computation.19 | convolution fusion | flops 940441600 | bytes 5767168 | tf_op jit(solution)/shard_map/irk,ckn->icrn/dot_general | solution.py:61
  49.1 4.6 %all-to-all-start.1 = ((bf16[16,128,448]{1,2,0:T(8,128)(2,1)}), bf16[16,128,448]{1,2,0:T(8,128)(2,1)S(1)}, u32[]{:S(2)}, u32[]{:S(2)}) async-start(bf16[16,128,448]{1,2,0:T(8,128)(2,1)} %bitcast.205), calls=%async_computation.1 | async-start | bytes 3670016 | tf_op jit(solution)/shard_map/all_to_all | solution.py:67
  53.7 4.5 %collective-permute-start.1 = (s32[128,8]{0,1:T(8,128)S(1)}, s32[128,8]{0,1:T(8,128)S(1)}, u32[]{:S(2)}, u32[]{:S(2)}) collective-permute-start(s32[128,8]{0,1:T(8,128)S(1)} %copy-done.5), channel_id=1, source_target_pairs={{0,0},{16,1},{32,2},{48,3},{64,4},{80,5},{96,6},{112,7},{1,8},{17,... | collective-permute-start | bytes 12296 | tf_op jit(solution)/shard_map/ppermute | solution.py:79
  58.3 5.1 %collective-permute-start = (bf16[128,448]{0,1:T(8,128)(2,1)S(1)}, bf16[128,448]{0,1:T(8,128)(2,1)S(1)}, u32[]{:S(2)}, u32[]{:S(2)}) collective-permute-start(bf16[128,448]{0,1:T(8,128)(2,1)S(1)} %copy-done.9), channel_id=1, source_target_pairs={{0,0},{16,1},{32,2},{48,3},{64,4},{80,5},{96,6},{112,7},{1,8},{17,... | collective-permute-start | bytes 344072 | tf_op jit(solution)/shard_map/ppermute | solution.py:78
  63.3 6.7 %collective-permute-done.1 = s32[128,8]{0,1:T(8,128)S(1)} collective-permute-done((s32[128,8]{0,1:T(8,128)S(1)}, s32[128,8]{0,1:T(8,128)S(1)}, u32[]{:S(2)}, u32[]{:S(2)}) %collective-permute-start.1) | collective-permute-done | bytes 4128 | tf_op jit(solution)/shard_map/ppermute | solution.py:79
  71.3 7.4 %fusion.2 = pred[2048,128]{1,0:T(8,128)(4,1)S(1)} fusion(s32[128,8]{0,1:T(8,128)S(1)} %multiply_add_fusion.1), kind=kLoop, calls=%fused_computation.4 | loop fusion | flops 3932160 | bytes 266240 | tf_op jit(solution)/shard_map/reduce_or | solution.py:91
  79.8 2.5 %copy.138 = bf16[2048,448]{1,0:T(8,128)(2,1)} copy(bf16[2048,448]{0,1:T(8,128)(2,1)S(1)} %convolution_convert_fusion) | data formatting | bytes 3670016 | tf_op jit(solution)/shard_map/convert_element_type | solution.py:95
  82.3 18.4 %all-to-all-start.2 = ((bf16[128,16,448]{2,1,0:T(8,128)(2,1)}), bf16[128,16,448]{2,1,0:T(8,128)(2,1)S(1)}, u32[]{:S(2)}, u32[]{:S(2)}) async-start(bf16[128,16,448]{2,1,0:T(8,128)(2,1)} %bitcast.186), calls=%async_computation.2 | async-start | bytes 4194304 | tf_op jit(solution)/shard_map/all_to_all | solution.py:97
  101.0 10.4 %copy.147 = bf16[1,1024,3584]{1,2,0:T(8,128)(2,1)} copy(bf16[1,1024,3584]{2,1,0:T(8,128)(2,1)} %param.23) | data formatting | bytes 14680064 | tf_op args[11]
  112.1 18.2 %all-to-all-done.2 = bf16[128,16,448]{2,1,0:T(8,128)(2,1)S(1)} async-done(((bf16[128,16,448]{2,1,0:T(8,128)(2,1)}), bf16[128,16,448]{2,1,0:T(8,128)(2,1)S(1)}, u32[]{:S(2)}, u32[]{:S(2)}) %all-to-all-start.2) | async-done | bytes 1835040 | tf_op jit(solution)/shard_map/all_to_all | solution.py:97
  130.5 1.7 fusion.37
  151.9 2.6 %convolution_add_fusion.1 = f32[256,1024]{1,0:T(8,128)} fusion(f32[256,1024]{1,0:T(8,128)S(1)} %convolution_add_fusion.2, bf16[256,448]{1,0:T(8,128)(2,1)S(1)} %bitcast.191, bf16[1,3584,1024]{2,1,0:T(8,128)(2,1)} %param.22), kind=kOutput, calls=%fused_computation.22 | convolution fusion | flops 235143168 | bytes 3244032 | tf_op jit(solution)/shard_map/dot_general | solution.py:112
  156.2 6.3 %convert_bitcast_fusion = bf16[8,256,448]{1,2,0:T(8,128)(2,1)S(1)} fusion(bf16[1024,8,448]{0,2,1:T(8,128)(2,1)} %bitcast.187, f32[256,1024]{1,0:T(8,128)} %convolution_add_fusion.1, bf16[256,448]{1,0:T(8,128)(2,1)} %bitcast.207, f32[256,1024]{1,0:T(8,128)S(1)} %convolution_add_fusion.7, bf16[1,3584,1024]{2,1,0:T(8,128)(2,1)} %param.22), kind=kOutput, calls=%fused_computation.18 | convolution fusion | flops 2116681728 | bytes 12451840 | tf_op jit(solution)/shard_map/sf,fgc->gsc/dot_general | solution.py:116
  162.5 2.8 %copy.148 = bf16[8,256,448]{2,1,0:T(8,128)(2,1)} copy(bf16[8,256,448]{1,2,0:T(8,128)(2,1)S(1)} %convert_bitcast_fusion) | data formatting | bytes 3670016 | tf_op jit(solution)/shard_map/convert_element_type | solution.py:119
  165.3 4.8 %all-to-all-start.3 = ((bf16[128,16,448]{2,1,0:T(8,128)(2,1)}), bf16[128,16,448]{2,1,0:T(8,128)(2,1)S(1)}, u32[]{:S(2)}, u32[]{:S(2)}) async-start(bf16[128,16,448]{2,1,0:T(8,128)(2,1)} %bitcast.184), calls=%async_computation.3 | async-start | bytes 4194304 | tf_op jit(solution)/shard_map/all_to_all | solution.py:120
  174.0 7.1 %fusion.4 = (bf16[128,2048]{1,0:T(8,128)(2,1)}, bf16[128,2048]{1,0:T(8,128)(2,1)}) fusion(s32[128,8]{1,0:T(8,128)} %copy.136, bf16[128,8]{1,0:T(8,128)(2,1)} %copy.149, bf16[128,8]{1,0:T(8,128)(2,1)S(1)} %copy.137), kind=kLoop, calls=%fused_computation.6 | loop fusion | flops 9961472 | bytes 1056768 | tf_op jit(solution)/shard_map/reduce_sum | solution.py:134
  181.1 5.6 %collective-permute-start.2 = (bf16[128,448]{0,1:T(8,128)(2,1)S(1)}, bf16[128,448]{0,1:T(8,128)(2,1)}, u32[]{:S(2)}, u32[]{:S(2)}) collective-permute-start(bf16[128,448]{0,1:T(8,128)(2,1)S(1)} %add_convert_fusion.2), channel_id=1, source_target_pairs={{0,0},{1,16},{2,32},{3,48},{4,64},{5,80},{6,96},{7,112},{8,1},{9,1... | collective-permute-start | bytes 344072 | tf_op jit(solution)/shard_map/ppermute | solution.py:96
  186.6 13.7 %all-to-all-done.3 = bf16[128,16,448]{2,1,0:T(8,128)(2,1)S(1)} async-done(((bf16[128,16,448]{2,1,0:T(8,128)(2,1)}), bf16[128,16,448]{2,1,0:T(8,128)(2,1)S(1)}, u32[]{:S(2)}, u32[]{:S(2)}) %all-to-all-start.3) | async-done | bytes 1835040 | tf_op jit(solution)/shard_map/all_to_all | solution.py:120
  200.3 1.9 fusion.78
  202.3 1.8 convolution_add_fusion.14
  (93 shorter events, 37.3 us)
Async XLA Ops:
  6.5 9.4 %copy-start = (bf16[16,64,576]{2,1,0:T(8,128)(2,1)S(1)}, bf16[16,64,576]{2,1,0:T(8,128)(2,1)}, u32[]{:S(2)}) copy-start(bf16[16,64,576]{2,1,0:T(8,128)(2,1)} %param.12) | copy-start | bytes 3538948
  6.5 38.0 %all-gather.3.cloned.1.call-start = ((), (), s32[]{:S(2)}) async-start(), calls=%async_computation.4 | async-start | bytes 4128768 | tf_op jit(solution)/shard_map/all_gather | solution.py:59
  10.0 4.1 %copy-start.8 = (s32[16]{0:T(128)S(1)}, s32[16]{0:T(128)}, u32[]{:S(2)}) copy-start(s32[16]{0:T(128)} %param.15) | copy-start | bytes 196
  10.7 5.2 %copy-start.6 = (bf16[16,576]{1,0:T(8,128)(2,1)S(1)}, bf16[16,576]{1,0:T(8,128)(2,1)}, u32[]{:S(2)}) copy-start(bf16[16,576]{1,0:T(8,128)(2,1)} %param.14) | copy-start | bytes 55300
  19.0 24.8 %copy-start.3 = (bf16[4,512,128]{2,1,0:T(8,128)(2,1)S(1)}, bf16[4,512,128]{2,1,0:T(8,128)(2,1)}, u32[]{:S(2)}) copy-start(bf16[4,512,128]{2,1,0:T(8,128)(2,1)} %param.16) | copy-start | bytes 1572868
  44.6 9.1 %copy-start.5 = (s32[128,8]{0,1:T(8,128)S(1)}, s32[128,8]{0,1:T(8,128)}, u32[]{:S(2)}) copy-start(s32[128,8]{0,1:T(8,128)} %param.19) | copy-start | bytes 12292
  44.6 13.7 %copy-start.9 = (bf16[128,448]{0,1:T(8,128)(2,1)S(1)}, bf16[128,448]{0,1:T(8,128)(2,1)}, u32[]{:S(2)}) copy-start(bf16[128,448]{0,1:T(8,128)(2,1)} %param.18) | copy-start | bytes 344068
  49.1 29.8 %all-to-all-start.1 = ((bf16[16,128,448]{1,2,0:T(8,128)(2,1)}), bf16[16,128,448]{1,2,0:T(8,128)(2,1)S(1)}, u32[]{:S(2)}, u32[]{:S(2)}) async-start(bf16[16,128,448]{1,2,0:T(8,128)(2,1)} %bitcast.205), calls=%async_computation.1 | async-start | bytes 3670016 | tf_op jit(solution)/shard_map/all_to_all | solution.py:67
  53.7 16.3 %collective-permute-start.1 = (s32[128,8]{0,1:T(8,128)S(1)}, s32[128,8]{0,1:T(8,128)S(1)}, u32[]{:S(2)}, u32[]{:S(2)}) collective-permute-start(s32[128,8]{0,1:T(8,128)S(1)} %copy-done.5), channel_id=1, source_target_pairs={{0,0},{16,1},{32,2},{48,3},{64,4},{80,5},{96,6},{112,7},{1,8},{17,... | collective-permute-start | bytes 12296 | tf_op jit(solution)/shard_map/ppermute | solution.py:79
  58.3 20.9 %collective-permute-start = (bf16[128,448]{0,1:T(8,128)(2,1)S(1)}, bf16[128,448]{0,1:T(8,128)(2,1)S(1)}, u32[]{:S(2)}, u32[]{:S(2)}) collective-permute-start(bf16[128,448]{0,1:T(8,128)(2,1)S(1)} %copy-done.9), channel_id=1, source_target_pairs={{0,0},{16,1},{32,2},{48,3},{64,4},{80,5},{96,6},{112,7},{1,8},{17,... | collective-permute-start | bytes 344072 | tf_op jit(solution)/shard_map/ppermute | solution.py:78
  82.3 48.0 %all-to-all-start.2 = ((bf16[128,16,448]{2,1,0:T(8,128)(2,1)}), bf16[128,16,448]{2,1,0:T(8,128)(2,1)S(1)}, u32[]{:S(2)}, u32[]{:S(2)}) async-start(bf16[128,16,448]{2,1,0:T(8,128)(2,1)} %bitcast.186), calls=%async_computation.2 | async-start | bytes 4194304 | tf_op jit(solution)/shard_map/all_to_all | solution.py:97
  130.5 24.0 %copy-start.2 = (bf16[8,2,1,16,448]{4,3,2,1,0:T(8,128)(2,1)}, bf16[8,2,1,16,448]{4,3,2,1,0:T(8,128)(2,1)S(1)}, u32[]{:S(2)}) copy-start(bf16[8,2,1,16,448]{4,3,2,1,0:T(8,128)(2,1)S(1)} %get-tuple-element.17) | copy-start | bytes 688132
  162.5 7.6 %copy-start.4 = (s32[8,128]{0,1:T(8,128)S(1)}, s32[8,128]{0,1:T(8,128)}, u32[]{:S(2)}) copy-start(s32[8,128]{0,1:T(8,128)} %copy.133) | copy-start | bytes 12292
  165.3 6.5 %copy-start.7 = (f32[128,8]{0,1:T(8,128)S(1)}, f32[128,8]{0,1:T(8,128)}, u32[]{:S(2)}) copy-start(f32[128,8]{0,1:T(8,128)} %param.20) | copy-start | bytes 12292
  165.3 35.0 %all-to-all-start.3 = ((bf16[128,16,448]{2,1,0:T(8,128)(2,1)}), bf16[128,16,448]{2,1,0:T(8,128)(2,1)S(1)}, u32[]{:S(2)}, u32[]{:S(2)}) async-start(bf16[128,16,448]{2,1,0:T(8,128)(2,1)} %bitcast.184), calls=%async_computation.3 | async-start | bytes 4194304 | tf_op jit(solution)/shard_map/all_to_all | solution.py:120
  172.5 33.2 %copy-start.1 = (bf16[16,64,576]{2,1,0:T(8,128)(2,1)S(1)}, bf16[16,64,576]{2,1,0:T(8,128)(2,1)}, u32[]{:S(2)}) copy-start(bf16[16,64,576]{2,1,0:T(8,128)(2,1)} %param.12) | copy-start | bytes 3538948
  181.1 23.0 %collective-permute-start.2 = (bf16[128,448]{0,1:T(8,128)(2,1)S(1)}, bf16[128,448]{0,1:T(8,128)(2,1)}, u32[]{:S(2)}, u32[]{:S(2)}) collective-permute-start(bf16[128,448]{0,1:T(8,128)(2,1)S(1)} %add_convert_fusion.2), channel_id=1, source_target_pairs={{0,0},{1,16},{2,32},{3,48},{4,64},{5,80},{6,96},{7,112},{8,1},{9,1... | collective-permute-start | bytes 344072 | tf_op jit(solution)/shard_map/ppermute | solution.py:96
Sparse Core Ops, SparseCore 0:
  9.0 33.4 all-gather.2

commit v11 on v9

--- a/solution.py
+++ b/solution.py
@@ -102,14 +102,15 @@
         tiled=True,
     )
     arrived = arrived.reshape(groups, halves, groups, capacity, columns)
+    arrived = arrived.transpose(2, 0, 1, 3, 4).reshape(groups, members * capacity, columns)
     gate = jnp.einsum(
-        "gicsn,cnf->gisf", arrived, w_gate[0].reshape(groups, columns, -1),
+        "csn,cnf->sf", arrived, w_gate[0].reshape(groups, columns, -1),
         preferred_element_type=jnp.float32,
-    ).reshape(members * capacity, -1)
+    )
     upper = jnp.einsum(
-        "gicsn,cnf->gisf", arrived, w_up[0].reshape(groups, columns, -1),
+        "csn,cnf->sf", arrived, w_up[0].reshape(groups, columns, -1),
         preferred_element_type=jnp.float32,
-    ).reshape(members * capacity, -1)
+    )
     inner = (jax.nn.silu(gate) * upper).astype(jnp.bfloat16)
     results = jnp.einsum(
         "sf,fgc->gsc", inner, w_down[0].reshape(-1, groups, columns),

time: 203 us -> 198 us (0.975)
  local copies, waits for them, and re-layouts: 32.1 us -> 25.4 us
    dot_general x1 -> x0, local copies, waits for them, and re-layouts: 3.1 us -> none  [per_device(): jnp.einsum('gicsn,cnf->gisf', arrived, w_gate[0].reshape(groups, columns,...]
    reshape x1, local copies, waits for them, and re-layouts: 2.76 us -> 0.18 us  [per_device(): arrived = arrived.reshape(groups, halves, groups, capacity, columns)]
    unnamed x20 -> x22, local copies, waits for them, and re-layouts: 10.6 us -> 10.6 us
  transfers between devices with their start and end apart: 7 -> 7, of which waited for: 3 -> 3; matrix products, arithmetic and copies ran while one was open for 21% -> 22% of each run, Pallas kernels for 0% -> 0%
where the time goes in v11:
time: 198 us; the launch traced here: 197 us
  waiting for transfers between devices  44.3 us (22%)
  starting transfers between devices  41.9 us (21%)
  matrix products  28.2 us (14%)
  local copies, waits for them, and re-layouts  25.4 us (13%)
  blocking collectives  24.3 us (12%)
  other arithmetic  19.1 us (10%)
  between operations  13.8 us (7%)
    all_to_all x1, blocking collectives, per_device(): lax.all_to_all(latent_out, 'member', split_axis=1, concat_axis=0, tiled=T...  24.3 us
    all_to_all x1, waiting for transfers between devices, per_device(): lax.all_to_all(outgoing.reshape(experts, capacity, columns), everyone, sp...  18.8 us
    all_to_all x1, starting transfers between devices, per_device(): lax.all_to_all(outgoing.reshape(experts, capacity, columns), everyone, sp...  17.4 us
    all_to_all x1, waiting for transfers between devices, per_device(): lax.all_to_all(results.reshape(experts, capacity, columns), everyone, spl...  17 us
    unnamed x22, local copies, waits for them, and re-layouts  10.6 us
    dot_general x1, matrix products, per_device(): jnp.einsum('sf,fgc->gsc', inner, w_down[0].reshape(-1, groups, columns),...  10.3 us
    ppermute x1, waiting for transfers between devices, per_device(): held_ids = lax.ppermute(expert_ids, everyone, perm=to_holder)  7.71 us
    reduce_or x1, other arithmetic, per_device(): send_map = jnp.any(matches, axis=2).astype(jnp.bfloat16)  7.43 us
  transfers between devices with their start and end apart: 7, of which 3 were waited for; matrix products, arithmetic and copies ran while one was open for 22% of the time, Pallas kernels for 0%

profile of v11, /device:TPU:1, one launch (start us, length us, event | category | flops | bytes accessed | tf_op | source)
XLA Modules:
  0.0 197.0 jit_solution(17890171417324991895)
XLA Ops:
  7.3 2.8 %slice_bitcast_fusion.3 = (bf16[4,128,576]{1,2,0:T(8,128)(2,1)S(1)}, bf16[4,128,576]{1,2,0:T(8,128)(2,1)}, bf16[4,128,576]{1,2,0:T(8,128)(2,1)}, bf16[4,128,576]{1,2,0:T(8,128)(2,1)S(1)}) fusion(bf16[4,4,128,576]{2,3,1,0:T(8,128)(2,1)} %bitcast.121), kind=kLoop, calls=%fused_computation.33 | loop fusion | bytes 4718592 | tf_op jit(solution)/shard_map/jit(_where)/broadcast_in_dim | solution.py:39
  10.7 1.4 copy.104
  12.0 2.1 %copy.105 = bf16[4,128,576]{2,1,0:T(8,128)(2,1)} copy(bf16[4,128,576]{1,2,0:T(8,128)(2,1)} %get-tuple-element.14) | data formatting | bytes 1179648 | tf_op jit(solution)/shard_map/broadcast_in_dim | solution.py:37
  14.2 1.7 fusion.8
  19.5 24.3 %all_to_all.33 = bf16[16,64,512]{2,0,1:T(8,128)(2,1)S(1)} all-to-all(bf16[16,64,512]{2,0,1:T(8,128)(2,1)S(1)} %copy.107), channel_id=1, replica_groups=mesh['group'=8,'member'=16] {'member'}, dimensions={1} | all-to-all | bytes 2097152 | tf_op jit(solution)/shard_map/all_to_all | solution.py:54
  44.7 4.4 %fusion.11 = bf16[2,128,8,448]{1,3,2,0:T(8,128)(2,1)} fusion(bf16[56,8,8,512]{3,2,1,0:T(8,128)(2,1)} %bitcast.130, bf16[2,128,512,1]{2,1,0,3:T(8,128)(2,1)S(1)} %reshape.129), kind=kOutput, calls=%fused_computation.19 | convolution fusion | flops 940441600 | bytes 5767168 | tf_op jit(solution)/shard_map/irk,ckn->icrn/dot_general | solution.py:61
  49.2 4.6 %all-to-all-start.1 = ((bf16[16,128,448]{1,2,0:T(8,128)(2,1)}), bf16[16,128,448]{1,2,0:T(8,128)(2,1)S(1)}, u32[]{:S(2)}, u32[]{:S(2)}) async-start(bf16[16,128,448]{1,2,0:T(8,128)(2,1)} %bitcast.124), calls=%async_computation.1 | async-start | bytes 3670016 | tf_op jit(solution)/shard_map/all_to_all | solution.py:67
  53.8 4.7 %collective-permute-start.1 = (s32[128,8]{0,1:T(8,128)S(1)}, s32[128,8]{0,1:T(8,128)S(1)}, u32[]{:S(2)}, u32[]{:S(2)}) collective-permute-start(s32[128,8]{0,1:T(8,128)S(1)} %copy-done.5), channel_id=1, source_target_pairs={{0,0},{16,1},{32,2},{48,3},{64,4},{80,5},{96,6},{112,7},{1,8},{17,... | collective-permute-start | bytes 12296 | tf_op jit(solution)/shard_map/ppermute | solution.py:79
  58.5 5.1 %collective-permute-start = (bf16[128,448]{0,1:T(8,128)(2,1)S(1)}, bf16[128,448]{0,1:T(8,128)(2,1)S(1)}, u32[]{:S(2)}, u32[]{:S(2)}) collective-permute-start(bf16[128,448]{0,1:T(8,128)(2,1)S(1)} %copy-done.9), channel_id=1, source_target_pairs={{0,0},{16,1},{32,2},{48,3},{64,4},{80,5},{96,6},{112,7},{1,8},{17,... | collective-permute-start | bytes 344072 | tf_op jit(solution)/shard_map/ppermute | solution.py:78
  63.5 7.7 %collective-permute-done.1 = s32[128,8]{0,1:T(8,128)S(1)} collective-permute-done((s32[128,8]{0,1:T(8,128)S(1)}, s32[128,8]{0,1:T(8,128)S(1)}, u32[]{:S(2)}, u32[]{:S(2)}) %collective-permute-start.1) | collective-permute-done | bytes 4128 | tf_op jit(solution)/shard_map/ppermute | solution.py:79
  72.6 7.4 %fusion.2 = pred[2048,128]{1,0:T(8,128)(4,1)S(1)} fusion(s32[128,8]{0,1:T(8,128)S(1)} %multiply_add_fusion.1), kind=kLoop, calls=%fused_computation.4 | loop fusion | flops 3932160 | bytes 266240 | tf_op jit(solution)/shard_map/reduce_or | solution.py:91
  81.1 2.5 %copy.123 = bf16[2048,448]{1,0:T(8,128)(2,1)} copy(bf16[2048,448]{0,1:T(8,128)(2,1)S(1)} %convolution_convert_fusion) | data formatting | bytes 3670016 | tf_op jit(solution)/shard_map/convert_element_type | solution.py:95
  83.6 17.4 %all-to-all-start.2 = ((bf16[128,16,448]{2,1,0:T(8,128)(2,1)}), bf16[128,16,448]{2,1,0:T(8,128)(2,1)S(1)}, u32[]{:S(2)}, u32[]{:S(2)}) async-start(bf16[128,16,448]{2,1,0:T(8,128)(2,1)} %bitcast.117), calls=%async_computation.2 | async-start | bytes 4194304 | tf_op jit(solution)/shard_map/all_to_all | solution.py:97
  101.2 10.4 %copy.127 = bf16[1,1024,3584]{1,2,0:T(8,128)(2,1)} copy(bf16[1,1024,3584]{2,1,0:T(8,128)(2,1)} %param.23) | data formatting | bytes 14680064 | tf_op args[11]
  111.7 18.8 %all-to-all-done.2 = bf16[128,16,448]{2,1,0:T(8,128)(2,1)S(1)} async-done(((bf16[128,16,448]{2,1,0:T(8,128)(2,1)}), bf16[128,16,448]{2,1,0:T(8,128)(2,1)S(1)}, u32[]{:S(2)}, u32[]{:S(2)}) %all-to-all-start.2) | async-done | bytes 1835040 | tf_op jit(solution)/shard_map/all_to_all | solution.py:97
  130.8 7.0 %convolution_bitcast_fusion.1 = f32[256,1024]{1,0:T(8,128)} fusion(bf16[8,256,448]{2,1,0:T(8,128)(2,1)S(1)} %bitcast.122, bf16[8,448,1024]{2,1,0:T(8,128)(2,1)} %bitcast.128), kind=kOutput, calls=%fused_computation.22 | convolution fusion | flops 1879048192 | bytes 10223616 | tf_op jit(solution)/shard_map/csn,cnf->sf/dot_general | solution.py:106
  137.7 10.3 %convert_bitcast_fusion = bf16[8,256,448]{1,2,0:T(8,128)(2,1)S(1)} fusion(bf16[1024,8,448]{0,2,1:T(8,128)(2,1)} %bitcast.118, bf16[8,256,448]{2,1,0:T(8,128)(2,1)} %bitcast.123, bf16[8,448,1024]{2,1,0:T(8,128)(2,1)} %bitcast.129, f32[256,1024]{1,0:T(8,128)} %convolution_bitcast_fusion.1), kind=kOutput, calls=%fused_computation.18 | convolution fusion | flops 3760586752 | bytes 19398656 | tf_op jit(solution)/shard_map/sf,fgc->gsc/dot_general | solution.py:115
  148.0 2.8 %copy.128 = bf16[8,256,448]{2,1,0:T(8,128)(2,1)} copy(bf16[8,256,448]{1,2,0:T(8,128)(2,1)S(1)} %convert_bitcast_fusion) | data formatting | bytes 3670016 | tf_op jit(solution)/shard_map/convert_element_type | solution.py:118
  150.8 4.7 %all-to-all-start.3 = ((bf16[128,16,448]{2,1,0:T(8,128)(2,1)}), bf16[128,16,448]{2,1,0:T(8,128)(2,1)S(1)}, u32[]{:S(2)}, u32[]{:S(2)}) async-start(bf16[128,16,448]{2,1,0:T(8,128)(2,1)} %bitcast.115), calls=%async_computation.3 | async-start | bytes 4194304 | tf_op jit(solution)/shard_map/all_to_all | solution.py:119
  156.8 6.3 %fusion.4 = (bf16[128,2048]{1,0:T(8,128)(2,1)}, bf16[128,2048]{1,0:T(8,128)(2,1)}) fusion(s32[128,8]{1,0:T(8,128)S(1)} %copy.121, bf16[128,8]{1,0:T(8,128)(2,1)S(1)} %copy.129, bf16[128,8]{1,0:T(8,128)(2,1)S(1)} %copy.122), kind=kLoop, calls=%fused_computation.6 | loop fusion | flops 9961472 | bytes 1056768 | tf_op jit(solution)/shard_map/reduce_sum | solution.py:133
  163.1 5.6 %collective-permute-start.2 = (bf16[128,448]{0,1:T(8,128)(2,1)S(1)}, bf16[128,448]{0,1:T(8,128)(2,1)}, u32[]{:S(2)}, u32[]{:S(2)}) collective-permute-start(bf16[128,448]{0,1:T(8,128)(2,1)S(1)} %add_convert_fusion.2), channel_id=1, source_target_pairs={{0,0},{1,16},{2,32},{3,48},{4,64},{5,80},{6,96},{7,112},{8,1},{9,1... | collective-permute-start | bytes 344072 | tf_op jit(solution)/shard_map/ppermute | solution.py:96
  168.6 17.0 %all-to-all-done.3 = bf16[128,16,448]{2,1,0:T(8,128)(2,1)S(1)} async-done(((bf16[128,16,448]{2,1,0:T(8,128)(2,1)}), bf16[128,16,448]{2,1,0:T(8,128)(2,1)S(1)}, u32[]{:S(2)}, u32[]{:S(2)}) %all-to-all-start.3) | async-done | bytes 1835040 | tf_op jit(solution)/shard_map/all_to_all | solution.py:119
  185.7 2.1 %fusion.40 = f32[128,448]{0,1:T(8,128)S(1)} fusion(bf16[128,2048]{1,0:T(8,128)(2,1)} %get-tuple-element.10, bf16[2048,448]{1,0:T(8,128)(2,1)S(1)} %bitcast.113), kind=kOutput, calls=%fused_computation.79 | convolution fusion | flops 234881024 | bytes 2588672 | tf_op jit(solution)/shard_map/dot_general | solution.py:134
  188.6 1.6 add_convert_fusion.1
  (79 shorter events, 10.7 us)
Async XLA Ops:
  6.5 9.4 %copy-start = (bf16[16,64,576]{2,1,0:T(8,128)(2,1)S(1)}, bf16[16,64,576]{2,1,0:T(8,128)(2,1)}, u32[]{:S(2)}) copy-start(bf16[16,64,576]{2,1,0:T(8,128)(2,1)} %param.12) | copy-start | bytes 3538948
  6.5 38.2 %all-gather.3.cloned.1.call-start = ((), (), s32[]{:S(2)}) async-start(), calls=%async_computation.4 | async-start | bytes 4128768 | tf_op jit(solution)/shard_map/all_gather | solution.py:59
  10.0 4.1 %copy-start.8 = (s32[16]{0:T(128)S(1)}, s32[16]{0:T(128)}, u32[]{:S(2)}) copy-start(s32[16]{0:T(128)} %param.15) | copy-start | bytes 196
  14.2 1.7 copy-start.6
  19.5 24.4 %copy-start.4 = (bf16[4,512,128]{2,1,0:T(8,128)(2,1)S(1)}, bf16[4,512,128]{2,1,0:T(8,128)(2,1)}, u32[]{:S(2)}) copy-start(bf16[4,512,128]{2,1,0:T(8,128)(2,1)} %param.16) | copy-start | bytes 1572868
  49.2 4.6 %copy-start.5 = (s32[128,8]{0,1:T(8,128)S(1)}, s32[128,8]{0,1:T(8,128)}, u32[]{:S(2)}) copy-start(s32[128,8]{0,1:T(8,128)} %param.19) | copy-start | bytes 12292
  49.2 9.3 %copy-start.9 = (bf16[128,448]{0,1:T(8,128)(2,1)S(1)}, bf16[128,448]{0,1:T(8,128)(2,1)}, u32[]{:S(2)}) copy-start(bf16[128,448]{0,1:T(8,128)(2,1)} %param.18) | copy-start | bytes 344068
  49.2 31.0 %all-to-all-start.1 = ((bf16[16,128,448]{1,2,0:T(8,128)(2,1)}), bf16[16,128,448]{1,2,0:T(8,128)(2,1)S(1)}, u32[]{:S(2)}, u32[]{:S(2)}) async-start(bf16[16,128,448]{1,2,0:T(8,128)(2,1)} %bitcast.124), calls=%async_computation.1 | async-start | bytes 3670016 | tf_op jit(solution)/shard_map/all_to_all | solution.py:67
  53.8 17.5 %collective-permute-start.1 = (s32[128,8]{0,1:T(8,128)S(1)}, s32[128,8]{0,1:T(8,128)S(1)}, u32[]{:S(2)}, u32[]{:S(2)}) collective-permute-start(s32[128,8]{0,1:T(8,128)S(1)} %copy-done.5), channel_id=1, source_target_pairs={{0,0},{16,1},{32,2},{48,3},{64,4},{80,5},{96,6},{112,7},{1,8},{17,... | collective-permute-start | bytes 12296 | tf_op jit(solution)/shard_map/ppermute | solution.py:79
  58.5 21.9 %collective-permute-start = (bf16[128,448]{0,1:T(8,128)(2,1)S(1)}, bf16[128,448]{0,1:T(8,128)(2,1)S(1)}, u32[]{:S(2)}, u32[]{:S(2)}) collective-permute-start(bf16[128,448]{0,1:T(8,128)(2,1)S(1)} %copy-done.9), channel_id=1, source_target_pairs={{0,0},{16,1},{32,2},{48,3},{64,4},{80,5},{96,6},{112,7},{1,8},{17,... | collective-permute-start | bytes 344072 | tf_op jit(solution)/shard_map/ppermute | solution.py:78
  83.6 47.0 %all-to-all-start.2 = ((bf16[128,16,448]{2,1,0:T(8,128)(2,1)}), bf16[128,16,448]{2,1,0:T(8,128)(2,1)S(1)}, u32[]{:S(2)}, u32[]{:S(2)}) async-start(bf16[128,16,448]{2,1,0:T(8,128)(2,1)} %bitcast.117), calls=%async_computation.2 | async-start | bytes 4194304 | tf_op jit(solution)/shard_map/all_to_all | solution.py:97
  130.7 7.0 %copy-start.2 = (bf16[8,2,8,16,448]{4,3,1,0,2:T(8,128)(2,1)}, bf16[8,2,8,16,448]{4,3,1,0,2:T(8,128)(2,1)S(1)}, u32[]{:S(2)}) copy-start(bf16[8,2,8,16,448]{4,3,1,0,2:T(8,128)(2,1)S(1)} %copy.124) | copy-start | bytes 5505028
  150.8 34.9 %all-to-all-start.3 = ((bf16[128,16,448]{2,1,0:T(8,128)(2,1)}), bf16[128,16,448]{2,1,0:T(8,128)(2,1)S(1)}, u32[]{:S(2)}, u32[]{:S(2)}) async-start(bf16[128,16,448]{2,1,0:T(8,128)(2,1)} %bitcast.115), calls=%async_computation.3 | async-start | bytes 4194304 | tf_op jit(solution)/shard_map/all_to_all | solution.py:119
  155.4 1.1 copy-start.7
  163.1 25.5 %collective-permute-start.2 = (bf16[128,448]{0,1:T(8,128)(2,1)S(1)}, bf16[128,448]{0,1:T(8,128)(2,1)}, u32[]{:S(2)}, u32[]{:S(2)}) collective-permute-start(bf16[128,448]{0,1:T(8,128)(2,1)S(1)} %add_convert_fusion.2), channel_id=1, source_target_pairs={{0,0},{1,16},{2,32},{3,48},{4,64},{5,80},{6,96},{7,112},{8,1},{9,1... | collective-permute-start | bytes 344072 | tf_op jit(solution)/shard_map/ppermute | solution.py:96
  185.7 2.1 %copy-start.3 = (bf16[128,2048]{1,0:T(8,128)(2,1)S(1)}, bf16[128,2048]{1,0:T(8,128)(2,1)}, u32[]{:S(2)}) copy-start(bf16[128,2048]{1,0:T(8,128)(2,1)} %get-tuple-element.9) | copy-start | bytes 1572868
  185.7 4.5 %copy-start.1 = (bf16[16,64,576]{2,1,0:T(8,128)(2,1)S(1)}, bf16[16,64,576]{2,1,0:T(8,128)(2,1)}, u32[]{:S(2)}) copy-start(bf16[16,64,576]{2,1,0:T(8,128)(2,1)} %param.12) | copy-start | bytes 3538948
Sparse Core Ops, SparseCore 0:
  9.0 33.4 all-gather.2

commit v12 on v11

--- a/solution.py
+++ b/solution.py
@@ -30,6 +30,16 @@
     experts = groups * members
     columns = out_proj.shape[1]
     scale = (VHEAD + ROPE) ** (-0.5)
+    to_owner = [
+        (g * members + m, (m % groups) * members + (m // groups) + (rows * members // residual.shape[0]) * g)
+        for g in range(groups)
+        for m in range(members)
+    ]
+    to_holder = [(b, a) for a, b in to_owner]
+    everyone = ("group", "member")
+    held_residual = lax.ppermute(residual, everyone, perm=to_holder)
+    held_ids = lax.ppermute(expert_ids, everyone, perm=to_holder)
+
     context = latent_cache.shape[1]
     width = latent_cache.shape[2]
     beams = latent_cache.reshape(rows // BEAM, BEAM, context, width)
@@ -52,6 +62,7 @@
     mixed_new = own_weight.astype(jnp.float32)[:, :, None] * new_key[:, None, :latent].astype(jnp.float32)
     latent_out = (mixed_cache + mixed_new).astype(jnp.bfloat16)
     by_heads = lax.all_to_all(latent_out, "member", split_axis=1, concat_axis=0, tiled=True)
+    by_heads, held_ids, held_residual = lax.optimization_barrier((by_heads, held_ids, held_residual))
     per_head = jnp.einsum(
         "rhl,hlv->rhv", by_heads, value_up, preferred_element_type=jnp.float32
     ).astype(jnp.bfloat16)
@@ -68,16 +79,6 @@
     block_rows = residual.shape[0]
     capacity = max(2, 2 * rows * TOP // members)
     positions = jnp.arange(experts * capacity, dtype=jnp.int32)
-    to_owner = [
-        (g * members + m, (m % groups) * members + (m // groups) + halves * g)
-        for g in range(groups)
-        for m in range(members)
-    ]
-    to_holder = [(b, a) for a, b in to_owner]
-    everyone = ("group", "member")
-    held_residual = lax.ppermute(residual, everyone, perm=to_holder)
-    held_ids = lax.ppermute(expert_ids, everyone, perm=to_holder)
-
     def route(ids):
         flat_ids = ids.reshape(-1)
         onehot = (flat_ids[:, None] == jnp.arange(experts, dtype=jnp.int32)[None, :]).astype(jnp.int32)

time: 198 us -> 202 us (1.020)
  blocking collectives: 24.3 us -> 0 us
  waiting for transfers between devices: 44.3 us -> 64 us
  starting transfers between devices: 41.9 us -> 48.7 us
    all_to_all x1 -> x0, blocking collectives: 24.3 us -> none  [per_device(): lax.all_to_all(latent_out, 'member', split_axis=1, concat_axis=0, tiled=T...]
    all_to_all x1, waiting for transfers between devices: 0.01 us -> 17.6 us  [per_device(): lax.all_to_all(pieces, 'member', split_axis=0, concat_axis=0, tiled=True)]
    all_to_all x1, starting transfers between devices: 17.4 us -> 7.72 us  [per_device(): lax.all_to_all(outgoing.reshape(experts, capacity, columns), everyone, sp...]
    all_to_all x0 -> x1, starting transfers between devices: none -> 8.56 us  [per_device(): lax.all_to_all(latent_out, 'member', split_axis=1, concat_axis=0, tiled=T...]
    all_to_all x1, starting transfers between devices: 4.62 us -> 12.9 us  [per_device(): lax.all_to_all(pieces, 'member', split_axis=0, concat_axis=0, tiled=True)]
    all_to_all x0 -> x1, waiting for transfers between devices: none -> 6.77 us  [per_device(): lax.all_to_all(latent_out, 'member', split_axis=1, concat_axis=0, tiled=T...]
    ppermute x1, waiting for transfers between devices: 7.71 us -> 2.82 us  [per_device(): held_ids = lax.ppermute(expert_ids, everyone, perm=to_holder)]
    unnamed x22 -> x26, local copies, waits for them, and re-layouts: 10.6 us -> 10.6 us
  transfers between devices with their start and end apart: 7 -> 8, of which waited for: 3 -> 5; matrix products, arithmetic and copies ran while one was open for 22% -> 22% of each run, Pallas kernels for 0% -> 0%
where the time goes in v12:
time: 202 us; the launch traced here: 201 us
  waiting for transfers between devices  64 us (32%)
  starting transfers between devices  48.7 us (24%)
  matrix products  29.1 us (14%)
  local copies, waits for them, and re-layouts  26.2 us (13%)
  other arithmetic  18.9 us (9%)
  between operations  13.8 us (7%)
    all_to_all x1, waiting for transfers between devices, per_device(): lax.all_to_all(outgoing.reshape(experts, capacity, columns), everyone, sp...  18.9 us
    all_to_all x1, waiting for transfers between devices, per_device(): lax.all_to_all(pieces, 'member', split_axis=0, concat_axis=0, tiled=True)  17.6 us
    all_to_all x1, waiting for transfers between devices, per_device(): lax.all_to_all(results.reshape(experts, capacity, columns), everyone, spl...  17.1 us
    all_to_all x1, starting transfers between devices, per_device(): lax.all_to_all(pieces, 'member', split_axis=0, concat_axis=0, tiled=True)  12.9 us
    unnamed x26, local copies, waits for them, and re-layouts  10.6 us
    dot_general x1, matrix products, per_device(): jnp.einsum('sf,fgc->gsc', inner, w_down[0].reshape(-1, groups, columns),...  10.3 us
    all_to_all x1, starting transfers between devices, per_device(): lax.all_to_all(latent_out, 'member', split_axis=1, concat_axis=0, tiled=T...  8.56 us
    all_to_all x1, starting transfers between devices, per_device(): lax.all_to_all(outgoing.reshape(experts, capacity, columns), everyone, sp...  7.72 us
  transfers between devices with their start and end apart: 8, of which 5 were waited for; matrix products, arithmetic and copies ran while one was open for 22% of the time, Pallas kernels for 0%

profile of v12, /device:TPU:1, one launch (start us, length us, event | category | flops | bytes accessed | tf_op | source)
XLA Modules:
  0.0 200.6 jit_solution(1291812049535982518)
XLA Ops:
  7.3 2.8 %slice_bitcast_fusion.3 = (bf16[4,128,576]{1,2,0:T(8,128)(2,1)S(1)}, bf16[4,128,576]{1,2,0:T(8,128)(2,1)}, bf16[4,128,576]{1,2,0:T(8,128)(2,1)}, bf16[4,128,576]{1,2,0:T(8,128)(2,1)S(1)}) fusion(bf16[4,4,128,576]{2,3,1,0:T(8,128)(2,1)} %bitcast.121), kind=kLoop, calls=%fused_computation.33 | loop fusion | bytes 4718592 | tf_op jit(solution)/shard_map/jit(_where)/broadcast_in_dim | solution.py:49
  12.0 2.1 %copy.78 = bf16[4,128,576]{2,1,0:T(8,128)(2,1)} copy(bf16[4,128,576]{1,2,0:T(8,128)(2,1)} %get-tuple-element.20) | data formatting | bytes 1179648 | tf_op jit(solution)/shard_map/broadcast_in_dim | solution.py:47
  14.2 1.7 fusion.8
  20.5 8.6 %all-to-all-start = ((bf16[16,64,512]{2,0,1:T(8,128)(2,1)}), bf16[16,64,512]{2,0,1:T(8,128)(2,1)S(1)}, u32[]{:S(2)}, u32[]{:S(2)}) async-start(bf16[16,64,512]{2,0,1:T(8,128)(2,1)} %copy.80), calls=%async_computation | async-start | bytes 2097152 | tf_op jit(solution)/shard_map/all_to_all | solution.py:64
  29.1 4.4 %collective-permute-start.1 = (bf16[128,448]{0,1:T(8,128)(2,1)S(1)}, bf16[128,448]{0,1:T(8,128)(2,1)S(1)}, u32[]{:S(2)}, u32[]{:S(2)}) collective-permute-start(bf16[128,448]{0,1:T(8,128)(2,1)S(1)} %copy-done.11), channel_id=1, source_target_pairs={{0,0},{16,1},{32,2},{48,3},{64,4},{80,5},{96,6},{112,7},{1,8},{17,... | collective-permute-start | bytes 344072 | tf_op jit(solution)/shard_map/ppermute | solution.py:40
  33.6 4.9 %collective-permute-start = (s32[128,8]{1,0:T(8,128)S(1)}, s32[128,8]{1,0:T(8,128)S(1)}, u32[]{:S(2)}, u32[]{:S(2)}) collective-permute-start(s32[128,8]{1,0:T(8,128)S(1)} %copy.82), channel_id=1, source_target_pairs={{0,0},{16,1},{32,2},{48,3},{64,4},{80,5},{96,6},{112,7},{1,8},{17,... | collective-permute-start | bytes 12296 | tf_op jit(solution)/shard_map/ppermute | solution.py:41
  38.5 6.8 %all-to-all-done = bf16[16,64,512]{2,0,1:T(8,128)(2,1)S(1)} async-done(((bf16[16,64,512]{2,0,1:T(8,128)(2,1)}), bf16[16,64,512]{2,0,1:T(8,128)(2,1)S(1)}, u32[]{:S(2)}, u32[]{:S(2)}) %all-to-all-start) | async-done | bytes 1048608 | tf_op jit(solution)/shard_map/all_to_all | solution.py:64
  45.3 2.8 %collective-permute-done = s32[128,8]{1,0:T(8,128)S(1)} collective-permute-done((s32[128,8]{1,0:T(8,128)S(1)}, s32[128,8]{1,0:T(8,128)S(1)}, u32[]{:S(2)}, u32[]{:S(2)}) %collective-permute-start) | collective-permute-done | bytes 4128 | tf_op jit(solution)/shard_map/ppermute | solution.py:41
  48.9 4.4 %fusion.11 = bf16[2,128,8,448]{1,3,2,0:T(8,128)(2,1)} fusion(bf16[56,8,8,512]{3,2,1,0:T(8,128)(2,1)} %bitcast.130, bf16[2,128,512,1]{2,1,0,3:T(8,128)(2,1)S(1)} %reshape.129), kind=kOutput, calls=%fused_computation.19 | convolution fusion | flops 940441600 | bytes 5767168 | tf_op jit(solution)/shard_map/irk,ckn->icrn/dot_general | solution.py:72
  53.4 12.9 %all-to-all-start.1 = ((bf16[16,128,448]{1,2,0:T(8,128)(2,1)}), bf16[16,128,448]{1,2,0:T(8,128)(2,1)S(1)}, u32[]{:S(2)}, u32[]{:S(2)}) async-start(bf16[16,128,448]{1,2,0:T(8,128)(2,1)} %bitcast.124), calls=%async_computation.1 | async-start | bytes 3670016 | tf_op jit(solution)/shard_map/all_to_all | solution.py:78
  67.5 7.4 %fusion.2 = pred[2048,128]{1,0:T(8,128)(4,1)S(1)} fusion(s32[128,8]{0,1:T(8,128)S(1)} %copy.87), kind=kLoop, calls=%fused_computation.4 | loop fusion | flops 3932160 | bytes 266240 | tf_op jit(solution)/shard_map/reduce_or | solution.py:92
  75.1 17.6 %all-to-all-done.1 = bf16[16,128,448]{1,2,0:T(8,128)(2,1)S(1)} async-done(((bf16[16,128,448]{1,2,0:T(8,128)(2,1)}), bf16[16,128,448]{1,2,0:T(8,128)(2,1)S(1)}, u32[]{:S(2)}, u32[]{:S(2)}) %all-to-all-start.1) | async-done | bytes 1835040 | tf_op jit(solution)/shard_map/all_to_all | solution.py:78
  95.2 2.5 %copy.95 = bf16[2048,448]{1,0:T(8,128)(2,1)} copy(bf16[2048,448]{0,1:T(8,128)(2,1)S(1)} %convolution_convert_fusion) | data formatting | bytes 3670016 | tf_op jit(solution)/shard_map/convert_element_type | solution.py:96
  97.7 7.7 %all-to-all-start.2 = ((bf16[128,16,448]{2,1,0:T(8,128)(2,1)}), bf16[128,16,448]{2,1,0:T(8,128)(2,1)S(1)}, u32[]{:S(2)}, u32[]{:S(2)}) async-start(bf16[128,16,448]{2,1,0:T(8,128)(2,1)} %bitcast.117), calls=%async_computation.2 | async-start | bytes 4194304 | tf_op jit(solution)/shard_map/all_to_all | solution.py:98
  105.6 10.4 %copy.99 = bf16[1,1024,3584]{1,2,0:T(8,128)(2,1)} copy(bf16[1,1024,3584]{2,1,0:T(8,128)(2,1)} %param.23) | data formatting | bytes 14680064 | tf_op args[11]
  116.1 18.9 %all-to-all-done.2 = bf16[128,16,448]{2,1,0:T(8,128)(2,1)S(1)} async-done(((bf16[128,16,448]{2,1,0:T(8,128)(2,1)}), bf16[128,16,448]{2,1,0:T(8,128)(2,1)S(1)}, u32[]{:S(2)}, u32[]{:S(2)}) %all-to-all-start.2) | async-done | bytes 1835040 | tf_op jit(solution)/shard_map/all_to_all | solution.py:98
  135.2 7.0 %convolution_bitcast_fusion.1 = f32[256,1024]{1,0:T(8,128)} fusion(bf16[8,256,448]{2,1,0:T(8,128)(2,1)S(1)} %bitcast.122, bf16[8,448,1024]{2,1,0:T(8,128)(2,1)} %bitcast.128), kind=kOutput, calls=%fused_computation.22 | convolution fusion | flops 1879048192 | bytes 10223616 | tf_op jit(solution)/shard_map/csn,cnf->sf/dot_general | solution.py:107
  142.2 10.3 %convert_bitcast_fusion = bf16[8,256,448]{1,2,0:T(8,128)(2,1)S(1)} fusion(bf16[1024,8,448]{0,2,1:T(8,128)(2,1)} %bitcast.118, bf16[8,256,448]{2,1,0:T(8,128)(2,1)} %bitcast.123, bf16[8,448,1024]{2,1,0:T(8,128)(2,1)} %bitcast.129, f32[256,1024]{1,0:T(8,128)} %convolution_bitcast_fusion.1), kind=kOutput, calls=%fused_computation.18 | convolution fusion | flops 3760586752 | bytes 19398656 | tf_op jit(solution)/shard_map/sf,fgc->gsc/dot_general | solution.py:116
  152.5 2.8 %copy.100 = bf16[8,256,448]{2,1,0:T(8,128)(2,1)} copy(bf16[8,256,448]{1,2,0:T(8,128)(2,1)S(1)} %convert_bitcast_fusion) | data formatting | bytes 3670016 | tf_op jit(solution)/shard_map/convert_element_type | solution.py:119
  155.2 4.7 %all-to-all-start.3 = ((bf16[128,16,448]{2,1,0:T(8,128)(2,1)}), bf16[128,16,448]{2,1,0:T(8,128)(2,1)S(1)}, u32[]{:S(2)}, u32[]{:S(2)}) async-start(bf16[128,16,448]{2,1,0:T(8,128)(2,1)} %bitcast.115), calls=%async_computation.3 | async-start | bytes 4194304 | tf_op jit(solution)/shard_map/all_to_all | solution.py:120
  161.2 6.3 %fusion.4 = (bf16[128,2048]{1,0:T(8,128)(2,1)}, bf16[128,2048]{1,0:T(8,128)(2,1)}) fusion(s32[128,8]{1,0:T(8,128)S(1)} %add.35, bf16[128,8]{1,0:T(8,128)(2,1)S(1)} %copy.101, bf16[128,8]{1,0:T(8,128)(2,1)S(1)} %copy.94), kind=kLoop, calls=%fused_computation.6 | loop fusion | flops 9961472 | bytes 1056768 | tf_op jit(solution)/shard_map/reduce_sum | solution.py:134
  167.5 5.6 %collective-permute-start.2 = (bf16[128,448]{0,1:T(8,128)(2,1)}, bf16[128,448]{0,1:T(8,128)(2,1)S(1)}, u32[]{:S(2)}, u32[]{:S(2)}) collective-permute-start(bf16[128,448]{0,1:T(8,128)(2,1)} %add_convert_fusion.2), channel_id=1, source_target_pairs={{0,0},{1,16},{2,32},{3,48},{4,64},{5,80},{6,96},{7,112},{8,1},{9,1... | collective-permute-start | bytes 344072 | tf_op jit(solution)/shard_map/ppermute | solution.py:97
  173.1 17.1 %all-to-all-done.3 = bf16[128,16,448]{2,1,0:T(8,128)(2,1)S(1)} async-done(((bf16[128,16,448]{2,1,0:T(8,128)(2,1)}), bf16[128,16,448]{2,1,0:T(8,128)(2,1)S(1)}, u32[]{:S(2)}, u32[]{:S(2)}) %all-to-all-start.3) | async-done | bytes 1835040 | tf_op jit(solution)/shard_map/all_to_all | solution.py:120
  190.2 2.1 %fusion.40 = f32[128,448]{0,1:T(8,128)S(1)} fusion(bf16[128,2048]{1,0:T(8,128)(2,1)} %get-tuple-element.16, bf16[2048,448]{1,0:T(8,128)(2,1)S(1)} %bitcast.113), kind=kOutput, calls=%fused_computation.79 | convolution fusion | flops 234881024 | bytes 2588672 | tf_op jit(solution)/shard_map/dot_general | solution.py:135
  (83 shorter events, 15.1 us)
Async XLA Ops:
  6.5 9.4 %copy-start = (bf16[16,64,576]{2,1,0:T(8,128)(2,1)S(1)}, bf16[16,64,576]{2,1,0:T(8,128)(2,1)}, u32[]{:S(2)}) copy-start(bf16[16,64,576]{2,1,0:T(8,128)(2,1)} %param.12) | copy-start | bytes 3538948
  6.5 42.4 %all-gather.3.cloned.1.call-start = ((), (), s32[]{:S(2)}) async-start(), calls=%async_computation.4 | async-start | bytes 4128768 | tf_op jit(solution)/shard_map/all_gather | solution.py:70
  10.0 4.1 %copy-start.10 = (s32[16]{0:T(128)S(1)}, s32[16]{0:T(128)}, u32[]{:S(2)}) copy-start(s32[16]{0:T(128)} %param.15) | copy-start | bytes 196
  14.2 1.7 copy-start.8
  18.9 10.1 %copy-start.11 = (bf16[128,448]{0,1:T(8,128)(2,1)S(1)}, bf16[128,448]{0,1:T(8,128)(2,1)}, u32[]{:S(2)}) copy-start(bf16[128,448]{0,1:T(8,128)(2,1)} %param.18) | copy-start | bytes 344068
  19.0 14.5 %copy-start.7 = (s32[128,8]{0,1:T(8,128)S(1)}, s32[128,8]{0,1:T(8,128)}, u32[]{:S(2)}) copy-start(s32[128,8]{0,1:T(8,128)} %param.19) | copy-start | bytes 12292
  20.5 27.7 %copy-start.4 = (bf16[4,512,128]{2,1,0:T(8,128)(2,1)S(1)}, bf16[4,512,128]{2,1,0:T(8,128)(2,1)}, u32[]{:S(2)}) copy-start(bf16[4,512,128]{2,1,0:T(8,128)(2,1)} %param.16) | copy-start | bytes 1572868
  20.5 24.7 %all-to-all-start = ((bf16[16,64,512]{2,0,1:T(8,128)(2,1)}), bf16[16,64,512]{2,0,1:T(8,128)(2,1)S(1)}, u32[]{:S(2)}, u32[]{:S(2)}) async-start(bf16[16,64,512]{2,0,1:T(8,128)(2,1)} %copy.80), calls=%async_computation | async-start | bytes 2097152 | tf_op jit(solution)/shard_map/all_to_all | solution.py:64
  29.1 19.1 %collective-permute-start.1 = (bf16[128,448]{0,1:T(8,128)(2,1)S(1)}, bf16[128,448]{0,1:T(8,128)(2,1)S(1)}, u32[]{:S(2)}, u32[]{:S(2)}) collective-permute-start(bf16[128,448]{0,1:T(8,128)(2,1)S(1)} %copy-done.11), channel_id=1, source_target_pairs={{0,0},{16,1},{32,2},{48,3},{64,4},{80,5},{96,6},{112,7},{1,8},{17,... | collective-permute-start | bytes 344072 | tf_op jit(solution)/shard_map/ppermute | solution.py:40
  33.6 14.6 %collective-permute-start = (s32[128,8]{1,0:T(8,128)S(1)}, s32[128,8]{1,0:T(8,128)S(1)}, u32[]{:S(2)}, u32[]{:S(2)}) collective-permute-start(s32[128,8]{1,0:T(8,128)S(1)} %copy.82), channel_id=1, source_target_pairs={{0,0},{16,1},{32,2},{48,3},{64,4},{80,5},{96,6},{112,7},{1,8},{17,... | collective-permute-start | bytes 12296 | tf_op jit(solution)/shard_map/ppermute | solution.py:41
  48.2 5.2 %copy-start.5 = (bf16[128,448]{0,1:T(8,128)(2,1)}, bf16[128,448]{0,1:T(8,128)(2,1)S(1)}, u32[]{:S(2)}) copy-start(bf16[128,448]{0,1:T(8,128)(2,1)S(1)} %collective-permute-done.1) | copy-start | bytes 344068
  53.4 39.3 %all-to-all-start.1 = ((bf16[16,128,448]{1,2,0:T(8,128)(2,1)}), bf16[16,128,448]{1,2,0:T(8,128)(2,1)S(1)}, u32[]{:S(2)}, u32[]{:S(2)}) async-start(bf16[16,128,448]{1,2,0:T(8,128)(2,1)} %bitcast.124), calls=%async_computation.1 | async-start | bytes 3670016 | tf_op jit(solution)/shard_map/all_to_all | solution.py:78
  66.9 26.1 %copy-start.6 = (bf16[128,448]{0,1:T(8,128)(2,1)S(1)}, bf16[128,448]{0,1:T(8,128)(2,1)}, u32[]{:S(2)}) copy-start(bf16[128,448]{0,1:T(8,128)(2,1)} %copy-done.5) | copy-start | bytes 344068
  97.7 37.3 %all-to-all-start.2 = ((bf16[128,16,448]{2,1,0:T(8,128)(2,1)}), bf16[128,16,448]{2,1,0:T(8,128)(2,1)S(1)}, u32[]{:S(2)}, u32[]{:S(2)}) async-start(bf16[128,16,448]{2,1,0:T(8,128)(2,1)} %bitcast.117), calls=%async_computation.2 | async-start | bytes 4194304 | tf_op jit(solution)/shard_map/all_to_all | solution.py:98
  135.2 7.0 %copy-start.2 = (bf16[8,2,8,16,448]{4,3,1,0,2:T(8,128)(2,1)}, bf16[8,2,8,16,448]{4,3,1,0,2:T(8,128)(2,1)S(1)}, u32[]{:S(2)}) copy-start(bf16[8,2,8,16,448]{4,3,1,0,2:T(8,128)(2,1)S(1)} %copy.96) | copy-start | bytes 5505028
  155.2 34.9 %all-to-all-start.3 = ((bf16[128,16,448]{2,1,0:T(8,128)(2,1)}), bf16[128,16,448]{2,1,0:T(8,128)(2,1)S(1)}, u32[]{:S(2)}, u32[]{:S(2)}) async-start(bf16[128,16,448]{2,1,0:T(8,128)(2,1)} %bitcast.115), calls=%async_computation.3 | async-start | bytes 4194304 | tf_op jit(solution)/shard_map/all_to_all | solution.py:120
  159.9 1.0 copy-start.9
  167.5 25.6 %collective-permute-start.2 = (bf16[128,448]{0,1:T(8,128)(2,1)}, bf16[128,448]{0,1:T(8,128)(2,1)S(1)}, u32[]{:S(2)}, u32[]{:S(2)}) collective-permute-start(bf16[128,448]{0,1:T(8,128)(2,1)} %add_convert_fusion.2), channel_id=1, source_target_pairs={{0,0},{1,16},{2,32},{3,48},{4,64},{5,80},{6,96},{7,112},{8,1},{9,1... | collective-permute-start | bytes 344072 | tf_op jit(solution)/shard_map/ppermute | solution.py:97
  190.2 2.1 %copy-start.3 = (bf16[128,2048]{1,0:T(8,128)(2,1)S(1)}, bf16[128,2048]{1,0:T(8,128)(2,1)}, u32[]{:S(2)}) copy-start(bf16[128,2048]{1,0:T(8,128)(2,1)} %get-tuple-element.15) | copy-start | bytes 1572868
  190.2 3.6 %copy-start.1 = (bf16[16,64,576]{2,1,0:T(8,128)(2,1)S(1)}, bf16[16,64,576]{2,1,0:T(8,128)(2,1)}, u32[]{:S(2)}) copy-start(bf16[16,64,576]{2,1,0:T(8,128)(2,1)} %param.12) | copy-start | bytes 3538948
Sparse Core Ops, SparseCore 0:
  9.0 35.4 all-gather.2
